TPU v7x, 128 devices: a whole 4x4x4 slice. The times are simulated.
128 devices in a mesh: grp: 32 (over z, y, core), head: 4 (over x).
Axes of the slice: x: 4, y: 4, z: 4, core: 2. Of those that a mesh axis runs over, the one named last changes fastest.
Arguments:
- activations: bfloat16 [1024, 4096], P('grp', 'head'), may hold values from -1.5 to 1.5
- ln_gain: bfloat16 [4096], replicated, may hold values from 0.099609375 to 1.8984375
- ln_bias: bfloat16 [4096], replicated, may hold values from -3 to 3
- w_qkv: bfloat16 [4096, 3, 4096], P('grp', None, 'head'), may hold values from -0.09375 to 0.09375
- prefix_keys: bfloat16 [64, 1024, 4096], P('grp', None, 'head')
- prefix_values: bfloat16 [64, 1024, 4096], P('grp', None, 'head'), may hold values from -6 to 6
- own_keys: bfloat16 [1024, 32, 4096], P('grp', None, 'head'), may hold values from -6 to 6
- own_values: bfloat16 [1024, 32, 4096], P('grp', None, 'head'), may hold values from -6 to 6
- prompt_len: int32 [64], P('grp'), may hold values from 64 to 1024, as said below
- own_len: int32 [1024], P('grp'), may hold values from 1 to 32, as said below
- w_attn_out: bfloat16 [256, 16, 4096], P('grp', 'head'), may hold values from -0.09375 to 0.09375
- w_in: bfloat16 [4096, 16384], P(None, ('grp', 'head')), may hold values from -0.09375 to 0.09375
- b_in: bfloat16 [16384], P(('grp', 'head')), may hold values from -4 to 4
- w_down: bfloat16 [16384, 4096], P(('grp', 'head')), may hold values from -0.046875 to 0.046875
- b_down: bfloat16 [4096], P('head'), may hold values from -3 to 3
Outputs:
- layer_out: bfloat16 [1024, 4096], P('grp', 'head')
Inputs may be any that keep to these rules, and one draw needn't show every extreme that they name: `prompt_len`: some group's prompt has exactly 1024 tokens and some has 64. `own_len`: some request has exactly 32 own tokens.
All inputs are finite; a program needn't handle non-finite values.
Results may differ from a plain program's by a relative error of at most 0.034.
Values may be sent and summed in bfloat16 or wider, within the bound.
No kernel may reach another device: no remote copies, remote signals or barrier semaphores. Data moves between devices by JAX's collectives and lax.ppermute only.
A program may use at most 128 MiB of HBM per device.

v0:
```python
import math

import jax
import jax.numpy as jnp
from jax import lax
from jax.sharding import PartitionSpec as P

HS = 256
ROT = 64
GSIZE = 16


def normalize(rows, gain, shift):
    floats = rows.astype(jnp.float32)
    center = floats - jnp.mean(floats, axis=-1, keepdims=True)
    spread = jnp.mean(center * center, axis=-1, keepdims=True)
    return (
        center * lax.rsqrt(spread + 1e-05) * gain.astype(jnp.float32) + shift.astype(jnp.float32)
    ).astype(jnp.bfloat16)


def rotate(values, positions):
    half = ROT // 2
    index = jnp.arange(half, dtype=jnp.float32)
    freqs = jnp.power(jnp.float32(10000.0), -2.0 * index / ROT)
    angle = positions[:, None, None] * freqs[None, None, :]
    cosine = jnp.cos(angle)
    sine = jnp.sin(angle)
    pairs = values[..., :ROT].reshape(values.shape[:-1] + (half, 2))
    first = pairs[..., 0]
    second = pairs[..., 1]
    turned = jnp.stack([first * cosine - second * sine, second * cosine + first * sine], axis=-1)
    turned = turned.reshape(values.shape[:-1] + (ROT,))
    return jnp.concatenate([turned, values[..., ROT:]], axis=-1)


def local(
    activations,
    ln_gain,
    ln_bias,
    w_qkv,
    prefix_keys,
    prefix_values,
    own_keys,
    own_values,
    prompt_len,
    own_len,
    w_attn_out,
    w_in,
    b_in,
    w_down,
    b_down,
):
    grp_count = lax.axis_size("grp")
    head_count = lax.axis_size("head")
    width_here = activations.shape[1]
    full_rows = lax.all_gather(activations, "head", axis=1, tiled=True)
    normed = normalize(full_rows, ln_gain, ln_bias)
    local_rows = normed.shape[0]
    groups_here = prompt_len.shape[0]
    columns = lax.all_to_all(normed, "grp", split_axis=1, concat_axis=0, tiled=True)
    qkv = lax.psum_scatter(
        jnp.einsum("rf,fch->rch", columns, w_qkv, preferred_element_type=jnp.float32).astype(
            jnp.bfloat16
        ),
        "grp",
        scatter_dimension=0,
        tiled=True,
    ).astype(jnp.float32)
    heads_here = w_qkv.shape[2] // HS
    member = (jnp.arange(local_rows) // GSIZE)[:, None] == jnp.arange(groups_here)[None, :]
    row_prompt = jnp.sum(jnp.where(member, prompt_len[None, :], 0), axis=1)
    positions = (row_prompt + own_len).astype(jnp.float32)
    query = rotate(qkv[:, 0].reshape(local_rows, heads_here, HS), positions).astype(jnp.bfloat16)
    key_new = rotate(qkv[:, 1].reshape(local_rows, heads_here, HS), positions).astype(jnp.bfloat16)
    value_new = qkv[:, 2].reshape(local_rows, heads_here, HS).astype(jnp.bfloat16)
    scale = 1.0 / math.sqrt(HS)
    longest = prefix_keys.shape[1]
    own_count = own_keys.shape[1]
    grouped = query.reshape(groups_here, GSIZE, heads_here, HS)
    pre_keys = prefix_keys.reshape(groups_here, longest, heads_here, HS)
    pre_vals = prefix_values.reshape(groups_here, longest, heads_here, HS)
    mine_keys = own_keys.reshape(local_rows, own_count, heads_here, HS)
    mine_vals = own_values.reshape(local_rows, own_count, heads_here, HS)
    pre_scores = (
        jnp.einsum("gqhd,gjhd->gqhj", grouped, pre_keys, preferred_element_type=jnp.float32) * scale
    )
    pre_scores = jnp.where(
        jnp.arange(longest)[None, None, None, :] < prompt_len[:, None, None, None],
        pre_scores,
        -jnp.inf,
    )
    own_scores = (
        jnp.einsum("rhd,rthd->rht", query, mine_keys, preferred_element_type=jnp.float32) * scale
    )
    own_scores = jnp.where(
        jnp.arange(own_count)[None, None, :] < own_len[:, None, None], own_scores, -jnp.inf
    )
    self_scores = (
        jnp.einsum("rhd,rhd->rh", query, key_new, preferred_element_type=jnp.float32) * scale
    )
    pre_peak = jnp.max(pre_scores, axis=-1).reshape(local_rows, heads_here)
    peak = jnp.maximum(jnp.maximum(pre_peak, jnp.max(own_scores, axis=-1)), self_scores)
    pre_exp = jnp.exp(pre_scores - peak.reshape(groups_here, GSIZE, heads_here)[..., None])
    own_exp = jnp.exp(own_scores - peak[..., None])
    self_exp = jnp.exp(self_scores - peak)
    denom = (
        jnp.sum(pre_exp, axis=-1).reshape(local_rows, heads_here)
        + jnp.sum(own_exp, axis=-1)
        + self_exp
    )
    mixed = jnp.einsum(
        "gqhj,gjhd->gqhd",
        pre_exp.astype(jnp.bfloat16),
        pre_vals,
        preferred_element_type=jnp.float32,
    )
    mixed = mixed.reshape(local_rows, heads_here, HS)
    mixed = mixed + jnp.einsum(
        "rht,rthd->rhd", own_exp.astype(jnp.bfloat16), mine_vals, preferred_element_type=jnp.float32
    )
    mixed = mixed + self_exp.astype(jnp.bfloat16).astype(jnp.float32)[..., None] * value_new.astype(
        jnp.float32
    )
    attended = (mixed / denom[..., None]).astype(jnp.bfloat16)
    transposed = jnp.transpose(attended, (2, 1, 0))
    slices = lax.all_to_all(transposed, "grp", split_axis=0, concat_axis=2, tiled=True)
    dim_here = slices.shape[0]
    hidden = jax.nn.gelu(
        jnp.dot(
            lax.all_gather(normed, "grp", axis=0, tiled=True),
            w_in,
            preferred_element_type=jnp.float32,
        )
        + b_in.astype(jnp.float32),
        approximate=True,
    ).astype(jnp.bfloat16)
    units = hidden.shape[1]
    mlp_part = jnp.einsum(
        "gri,ihf->ghrf",
        hidden.reshape(grp_count, local_rows, units),
        w_down.reshape(units, head_count, width_here),
        preferred_element_type=jnp.float32,
    )
    attn_part = jnp.einsum(
        "dkgr,dkhf->ghrf",
        slices.reshape(dim_here, heads_here, grp_count, local_rows),
        w_attn_out.reshape(dim_here, heads_here, head_count, width_here),
        preferred_element_type=jnp.float32,
    )
    combined = (mlp_part + attn_part).reshape(grp_count * head_count * local_rows, width_here)
    summed = lax.psum_scatter(combined, ("grp", "head"), scatter_dimension=0, tiled=True)
    total = activations.astype(jnp.float32) + b_down.astype(jnp.float32)[None, :] + summed
    return total.astype(jnp.bfloat16)


def solution(mesh):
    in_specs = (
        P("grp", "head"),
        P(),
        P(),
        P("grp", None, "head"),
        P("grp", None, "head"),
        P("grp", None, "head"),
        P("grp", None, "head"),
        P("grp", None, "head"),
        P("grp"),
        P("grp"),
        P("grp", "head", None),
        P(None, ("grp", "head")),
        P(("grp", "head")),
        P(("grp", "head"), None),
        P("head"),
    )
    out_specs = P("grp", "head")
    return jax.shard_map(local, mesh=mesh, in_specs=in_specs, out_specs=out_specs, check_vma=False)
```

profile of v0, /device:TPU:1, one launch (start us, length us, event | category | flops | bytes accessed | tf_op | source)
XLA Modules:
  0.0 883.8 jit_solution(3418900974730946647)
XLA Ops:
  6.5 0.8 convert_element_type.65
  7.3 0.7 convert_element_type.66
  8.0 11.2 %all_gather.6 = bf16[32,4096]{1,0:T(8,128)(2,1)S(1)} all-gather(bf16[32,1024]{1,0:T(8,128)(2,1)} %param.15), channel_id=1, replica_groups=mesh['grp'=32,'head'=4] {'head'}, dimensions={1}, use_global_device_ids=true | all-gather | bytes 327680 | tf_op jit(solution)/shard_map/all_gather | solution.py:57
  19.4 0.3 fusion.27
  19.8 19.9 %all_to_all.34 = bf16[32,32,128]{2,0,1:T(8,128)(2,1)S(1)} all-to-all(bf16[32,32,128]{2,0,1:T(8,128)(2,1)S(1)} %copy_bitcast_fusion), channel_id=1, replica_groups=mesh['grp'=32,'head'=4] {'grp'}, dimensions={1} | all-to-all | bytes 524288 | tf_op jit(solution)/shard_map/all_to_all | solution.py:61
  39.7 5.6 convolution_convert_fusion
  45.4 0.9 fusion.30
  46.7 80.3 %reduce-scatter.3.cloned.1.call-done = bf16[32,3,1024]{2,0,1:T(8,128)(2,1)} async-done(((bf16[1024,3,1024]{2,0,1:T(8,128)(2,1)}), bf16[32,3,1024]{2,0,1:T(8,128)(2,1)}) %reduce-scatter.3.cloned.1.call-update) | async-done | bytes 196624 | tf_op jit(solution)/shard_map/reduce_scatter | solution.py:62
  127.0 0.9 fusion.65
  128.3 0.9 slice_convert_fusion.1
  131.0 3.5 fusion.66
  134.6 2.2 fusion.9
  137.1 2.9 fusion.21
  140.6 2.1 fusion.6
  142.9 0.9 reshape.224
  143.8 7.4 all-to-all-start.1
  151.6 6.8 all-to-all-done.1
  158.7 7.4 fusion.42
  166.0 17.5 %all-gather.2.cloned.1.call-done = bf16[1024,4096]{1,0:T(8,128)(2,1)} async-done(((bf16[32,4096]{1,0:T(8,128)(2,1)}), bf16[1024,4096]{1,0:T(8,128)(2,1)}) %all-gather.2.cloned.1.call-update) | async-done | bytes 8388624 | tf_op jit(solution)/shard_map/all_gather | solution.py:131
  183.6 5.7 fusion.38
  189.3 13.9 %bitcast_add_fusion = f32[32,32,4,1024]{3,1,2,0:T(8,128)} fusion(f32[32,32,4,1024,1]{3,1,4,2,0:T(8,128)} %fusion.42, bf16[32,32,128,1]{2,1,3,0:T(8,128)(2,1)S(1)} %bitcast.130, bf16[16,4,8,1024]{3,2,1,0:T(8,128)(2,1)S(1)} %bitcast.124), kind=kOutput, calls=%fused_computation | convolution fusion | flops 1077936128 | bytes 34865152 | tf_op jit(solution)/shard_map/gri,ihf->ghrf/dot_general | solution.py:139
  203.2 0.7 copy-done.5
  203.9 671.8 %reduce-scatter.5.cloned.1.call-done = f32[32,1024]{1,0:T(8,128)} async-done(((f32[4096,1024]{1,0:T(8,128)}), f32[32,1024]{1,0:T(8,128)}) %reduce-scatter.5.cloned.1.call-update) | async-done | bytes 131088 | tf_op jit(solution)/shard_map/reduce_scatter | solution.py:152
  875.7 1.6 add_convert_fusion
  (73 shorter events, 4.7 us)
Async XLA Ops:
  6.5 177.0 %copy-start = (bf16[4096,128]{1,0:T(8,128)(2,1)S(1)}, bf16[4096,128]{1,0:T(8,128)(2,1)}, u32[]{:S(2)}) copy-start(bf16[4096,128]{1,0:T(8,128)(2,1)} %param.26) | copy-start | bytes 3145732
  6.5 120.5 %reduce-scatter.3.cloned.1.call-start = ((), (), s32[]{:S(2)}) async-start(), calls=%async_computation.5 | async-start | bytes 6488064 | tf_op jit(solution)/shard_map/reduce_scatter | solution.py:62
  45.3 1.0 copy-start.7
  45.3 1.1 copy-start.6
  45.3 138.2 %all-gather.2.cloned.1.call-start = ((), (), s32[]{:S(2)}) async-start(), calls=%async_computation.4 | async-start | bytes 8650752 | tf_op jit(solution)/shard_map/all_gather | solution.py:131
  137.1 14.3 %copy-start.8 = (bf16[128]{0:T(256)(128)(2,1)S(1)}, bf16[128]{0:T(256)(128)(2,1)}, u32[]{:S(2)}) copy-start(bf16[128]{0:T(256)(128)(2,1)} %param.27) | copy-start | bytes 772
  137.1 14.3 %copy-start.3 = (bf16[8,4,4096]{2,1,0:T(4,128)(2,1)S(1)}, bf16[8,4,4096]{2,1,0:T(4,128)(2,1)}, u32[]{:S(2)}) copy-start(bf16[8,4,4096]{2,1,0:T(4,128)(2,1)} %param.25) | copy-start | bytes 786436
  143.8 14.7 %all-to-all-start.1 = ((bf16[32,2,512]{2,1,0:T(2,128)(2,1)}), bf16[32,2,512]{2,1,0:T(2,128)(2,1)S(1)}, u32[]{:S(2)}, u32[]{:S(2)}) async-start(bf16[32,2,512]{2,1,0:T(2,128)(2,1)} %reshape.224), calls=%async_computation.2 | async-start | bytes 131072 | tf_op jit(solution)/shard_map/all_to_all | solution.py:127
  151.2 724.5 %reduce-scatter.5.cloned.1.call-start = ((), (), s32[]{:S(2)}) async-start(), calls=%async_computation.6 | async-start | bytes 16908288 | tf_op jit(solution)/shard_map/reduce_scatter | solution.py:152
  166.0 23.3 %copy-start.2 = (bf16[128,4096]{1,0:T(8,128)(2,1)S(1)}, bf16[128,4096]{1,0:T(8,128)(2,1)}, u32[]{:S(2)}) copy-start(bf16[128,4096]{1,0:T(8,128)(2,1)} %param.28) | copy-start | bytes 3145732
  203.2 0.7 copy-start.5
  203.2 672.5 %copy-start.4 = (bf16[32,1024]{1,0:T(8,128)(2,1)S(1)}, bf16[32,1024]{1,0:T(8,128)(2,1)}, u32[]{:S(2)}) copy-start(bf16[32,1024]{1,0:T(8,128)(2,1)} %param.15) | copy-start | bytes 196612
  203.9 673.4 %copy-start.1 = (bf16[4096,128]{1,0:T(8,128)(2,1)S(1)}, bf16[4096,128]{1,0:T(8,128)(2,1)}, u32[]{:S(2)}) copy-start(bf16[4096,128]{1,0:T(8,128)(2,1)} %param.26) | copy-start | bytes 3145732
Sparse Core Ops, SparseCore 0:
  45.5 81.5 reduce-scatter.2
  129.3 54.2 all-gather.1
  203.3 672.3 reduce-scatter.4
where the time goes:
time: 892 us; the launch traced here: 884 us
  waiting for transfers between devices  777 us (87%)
  matrix products  43.3 us (5%)
  blocking collectives  31.1 us (3%)
  between operations  13.4 us (2%)
    reduce_scatter x1, waiting for transfers between devices, local(): lax.psum_scatter(combined, ('grp', 'head'), scatter_dimension=0, tiled=True)  672 us
    reduce_scatter x1, waiting for transfers between devices, local(): lax.psum_scatter(jnp.einsum('rf,fch->rch', columns, w_qkv, preferred_elem...  80.3 us
    all_to_all x1, blocking collectives, local(): lax.all_to_all(normed, 'grp', split_axis=1, concat_axis=0, tiled=True)  19.9 us
  transfers between devices with their start and end apart: 4, of which 4 were waited for; matrix products, arithmetic and copies ran while one was open for 3% of the time, Pallas kernels for 0%

commit v1 on v0

--- a/solution.py
+++ b/solution.py
@@ -149,7 +149,14 @@
         preferred_element_type=jnp.float32,
     )
     combined = (mlp_part + attn_part).reshape(grp_count * head_count * local_rows, width_here)
-    summed = lax.psum_scatter(combined, ("grp", "head"), scatter_dimension=0, tiled=True)
+    pieces = lax.all_to_all(
+        combined.astype(jnp.bfloat16).reshape(grp_count * head_count, local_rows, width_here),
+        ("grp", "head"),
+        0,
+        0,
+        tiled=True,
+    )
+    summed = jnp.sum(pieces.astype(jnp.float32), axis=0)
     total = activations.astype(jnp.float32) + b_down.astype(jnp.float32)[None, :] + summed
     return total.astype(jnp.bfloat16)
 

time: 892 us -> 325 us (0.36)
  waiting for transfers between devices: 777 us -> 208 us
    reduce_scatter x1 -> x0, waiting for transfers between devices: 672 us -> none  [local(): lax.psum_scatter(combined, ('grp', 'head'), scatter_dimension=0, tiled=True)]
    all_to_all x0 -> x1, waiting for transfers between devices: none -> 103 us  [local(): lax.all_to_all(combined.astype(jnp.bfloat16).reshape(grp_count * head_cou...]
  transfers between devices with their start and end apart: 4 -> 4, of which waited for: 4 -> 4; matrix products, arithmetic and copies ran while one was open for 3% -> 8% of each run, Pallas kernels for 0% -> 0%
where the time goes in v1:
time: 325 us; the launch traced here: 324 us
  waiting for transfers between devices  208 us (64%)
  matrix products  40.8 us (13%)
  blocking collectives  31.2 us (10%)
  starting transfers between devices  15.2 us (5%)
  between operations  13.7 us (4%)
  other arithmetic  11.7 us (4%)
  local copies, waits for them, and re-layouts  3.73 us (1%)
    all_to_all x1, waiting for transfers between devices, local(): lax.all_to_all(combined.astype(jnp.bfloat16).reshape(grp_count * head_cou...  103 us
    reduce_scatter x1, waiting for transfers between devices, local(): lax.psum_scatter(jnp.einsum('rf,fch->rch', columns, w_qkv, preferred_elem...  80.3 us
    all_to_all x1, blocking collectives, local(): lax.all_to_all(normed, 'grp', split_axis=1, concat_axis=0, tiled=True)  19.9 us
    all_gather x1, waiting for transfers between devices, local(): lax.all_gather(normed, 'grp', axis=0, tiled=True)  17.5 us
    dot_general x1, matrix products, local(): jnp.einsum('gri,ihf->ghrf', hidden.reshape(grp_count, local_rows, units),...  11.3 us
    all_gather x1, blocking collectives, local(): full_rows = lax.all_gather(activations, 'head', axis=1, tiled=True)  11.3 us
    all_to_all x1, starting transfers between devices, local(): lax.all_to_all(combined.astype(jnp.bfloat16).reshape(grp_count * head_cou...  7.82 us
    all_to_all x1, starting transfers between devices, local(): lax.all_to_all(transposed, 'grp', split_axis=0, concat_axis=2, tiled=True)  7.37 us
  transfers between devices with their start and end apart: 4, of which 4 were waited for; matrix products, arithmetic and copies ran while one was open for 8% of the time, Pallas kernels for 0%

profile of v1, /device:TPU:1, one launch (start us, length us, event | category | flops | bytes accessed | tf_op | source)
XLA Modules:
  0.0 324.4 jit_solution(8075471526212283754)
XLA Ops:
  6.5 11.3 %all_gather.6 = bf16[32,4096]{1,0:T(8,128)(2,1)S(1)} all-gather(bf16[32,1024]{1,0:T(8,128)(2,1)} %param.15), channel_id=1, replica_groups=mesh['grp'=32,'head'=4] {'head'}, dimensions={1}, use_global_device_ids=true | all-gather | bytes 327680 | tf_op jit(solution)/shard_map/all_gather | solution.py:57
  18.3 0.7 convert_element_type.78
  19.0 0.7 convert_element_type.79
  19.9 19.9 %all_to_all.39 = bf16[32,32,128]{2,0,1:T(8,128)(2,1)S(1)} all-to-all(bf16[32,32,128]{2,0,1:T(8,128)(2,1)S(1)} %copy_bitcast_fusion), channel_id=1, replica_groups=mesh['grp'=32,'head'=4] {'grp'}, dimensions={1} | all-to-all | bytes 524288 | tf_op jit(solution)/shard_map/all_to_all | solution.py:61
  39.8 5.6 %convolution_convert_fusion = bf16[1024,3,1024]{2,0,1:T(8,128)(2,1)} fusion(bf16[1024,128,1]{1,0,2:T(8,128)(2,1)S(1)} %bitcast.127, bf16[128,3,1024]{2,0,1:T(8,128)(2,1)} %param.18), kind=kOutput, calls=%fused_computation.9 | convolution fusion | flops 808452096 | bytes 7340032 | tf_op jit(solution)/shard_map/rf,fch->rch/dot_general | solution.py:63
  45.4 0.9 fusion.31
  46.7 80.3 %reduce-scatter.2.cloned.1.call-done = bf16[32,3,1024]{2,0,1:T(8,128)(2,1)} async-done(((bf16[1024,3,1024]{2,0,1:T(8,128)(2,1)}), bf16[32,3,1024]{2,0,1:T(8,128)(2,1)}) %reduce-scatter.2.cloned.1.call-update) | async-done | bytes 196624 | tf_op jit(solution)/shard_map/reduce_scatter | solution.py:62
  127.1 0.9 fusion.66
  130.1 3.5 %fusion.67 = (f32[2,16,4]{1,2,0:T(4,128)S(1)}, f32[2,16,4,1024]{3,1,2,0:T(8,128)S(1)}) fusion(bf16[2,128,4,8,256]{4,3,2,1,0:T(8,128)(2,1)} %bitcast.123, bf16[2,16,4,64]{3,1,2,0:T(8,128)(2,1)S(1)} %copy.68, pred[2,1024]{1,0:T(4,128)(4,1)S(1)} %iota_compare_fusion.1, bf16[2,16,4,192]{3,1,0,2:T(8,128)(2,1)S(1)} %bitcast.128), kind=kOutput, calls=%fused_computation.101 | convolution fusion | flops 67633024 | bytes 4786688 | tf_op jit(solution)/shard_map/gqhd,gjhd->gqhj/dot_general | solution.py:86
  133.7 2.2 fusion.10
  136.5 2.9 fusion.22
  139.5 0.9 slice_convert_fusion.1
  140.6 2.1 fusion.7
  142.9 0.9 reshape.224
  143.8 7.4 %all-to-all-start.1 = ((bf16[32,2,512]{2,1,0:T(2,128)(2,1)}), bf16[32,2,512]{2,1,0:T(2,128)(2,1)S(1)}, u32[]{:S(2)}, u32[]{:S(2)}) async-start(bf16[32,2,512]{2,1,0:T(2,128)(2,1)} %reshape.224), calls=%async_computation.2 | async-start | bytes 131072 | tf_op jit(solution)/shard_map/all_to_all | solution.py:127
  151.4 7.1 %all-to-all-done.1 = bf16[32,2,512]{2,1,0:T(2,128)(2,1)S(1)} async-done(((bf16[32,2,512]{2,1,0:T(2,128)(2,1)}), bf16[32,2,512]{2,1,0:T(2,128)(2,1)S(1)}, u32[]{:S(2)}, u32[]{:S(2)}) %all-to-all-start.1) | async-done | bytes 65568 | tf_op jit(solution)/shard_map/all_to_all | solution.py:127
  158.7 7.4 %fusion.43 = f32[32,32,4,1024,1]{3,1,4,2,0:T(8,128)} fusion(bf16[32,8,4,32]{3,2,1,0:T(4,128)(2,1)S(1)} %bitcast.125, bf16[8,4,4,1024]{3,2,1,0:T(4,128)(2,1)S(1)} %reshape.210), kind=kOutput, calls=%fused_computation.44 | convolution fusion | flops 268435456 | bytes 17104896 | tf_op jit(solution)/shard_map/dkgr,dkhf->ghrf/dot_general | solution.py:145
  166.1 17.5 %all-gather.2.cloned.1.call-done = bf16[1024,4096]{1,0:T(8,128)(2,1)} async-done(((bf16[32,4096]{1,0:T(8,128)(2,1)}), bf16[1024,4096]{1,0:T(8,128)(2,1)}) %all-gather.2.cloned.1.call-update) | async-done | bytes 8388624 | tf_op jit(solution)/shard_map/all_gather | solution.py:131
  183.6 5.7 %fusion.39 = bf16[1024,128]{1,0:T(8,128)(2,1)S(1)} fusion(bf16[1024,4096]{1,0:T(8,128)(2,1)} %all-gather.2.cloned.1.call-done, bf16[4096,128]{1,0:T(8,128)(2,1)S(1)} %copy-done, f32[128]{0:T(128)S(1)} %convert_element_type.81), kind=kOutput, calls=%fused_computation.39 | convolution fusion | flops 1075052544 | bytes 9699840 | tf_op jit(solution)/shard_map/dot_general | solution.py:130
  189.3 11.3 %fusion = bf16[32,32,4,1024]{3,1,2,0:T(8,128)(2,1)} fusion(f32[32,32,4,1024,1]{3,1,4,2,0:T(8,128)} %fusion.43, bf16[32,32,128,1]{2,1,3,0:T(8,128)(2,1)S(1)} %bitcast.132, bf16[16,4,8,1024]{3,2,1,0:T(8,128)(2,1)S(1)} %bitcast.126), kind=kOutput, calls=%fused_computation.1 | convolution fusion | flops 1082130432 | bytes 26476544 | tf_op jit(solution)/shard_map/gri,ihf->ghrf/dot_general | solution.py:139
  200.7 7.8 %all-to-all-start.2 = ((bf16[128,32,1024]{2,1,0:T(8,128)(2,1)}), bf16[128,32,1024]{2,1,0:T(8,128)(2,1)}, u32[]{:S(2)}, u32[]{:S(2)}) async-start(bf16[128,32,1024]{2,1,0:T(8,128)(2,1)} %bitcast.122), calls=%async_computation.3 | async-start | bytes 16777216 | tf_op jit(solution)/shard_map/all_to_all | solution.py:152
  208.6 103.1 %all-to-all-done.2 = bf16[128,32,1024]{2,1,0:T(8,128)(2,1)} async-done(((bf16[128,32,1024]{2,1,0:T(8,128)(2,1)}), bf16[128,32,1024]{2,1,0:T(8,128)(2,1)}, u32[]{:S(2)}, u32[]{:S(2)}) %all-to-all-start.2) | async-done | bytes 8388640 | tf_op jit(solution)/shard_map/all_to_all | solution.py:152
  311.6 5.2 %convert_reduce_fusion = f32[32,1024]{1,0:T(8,128)S(1)} fusion(bf16[128,32,1024]{2,1,0:T(8,128)(2,1)} %all-to-all-done.2), kind=kLoop, calls=%fused_computation.2 | loop fusion | flops 8355840 | bytes 8519680 | tf_op jit(solution)/shard_map/reduce_sum | solution.py:159
  316.9 0.7 add_convert_fusion
  (73 shorter events, 4.7 us)
Async XLA Ops:
  6.5 177.1 %copy-start = (bf16[4096,128]{1,0:T(8,128)(2,1)S(1)}, bf16[4096,128]{1,0:T(8,128)(2,1)}, u32[]{:S(2)}) copy-start(bf16[4096,128]{1,0:T(8,128)(2,1)} %param.26) | copy-start | bytes 3145732
  6.5 120.5 %reduce-scatter.2.cloned.1.call-start = ((), (), s32[]{:S(2)}) async-start(), calls=%async_computation.5 | async-start | bytes 6488064 | tf_op jit(solution)/shard_map/reduce_scatter | solution.py:62
  45.3 1.0 copy-start.7
  45.3 1.1 copy-start.6
  45.4 138.2 %all-gather.2.cloned.1.call-start = ((), (), s32[]{:S(2)}) async-start(), calls=%async_computation.4 | async-start | bytes 8650752 | tf_op jit(solution)/shard_map/all_gather | solution.py:131
  136.5 14.7 %copy-start.3 = (bf16[8,4,4096]{2,1,0:T(4,128)(2,1)S(1)}, bf16[8,4,4096]{2,1,0:T(4,128)(2,1)}, u32[]{:S(2)}) copy-start(bf16[8,4,4096]{2,1,0:T(4,128)(2,1)} %param.25) | copy-start | bytes 786436
  136.5 14.9 %copy-start.8 = (bf16[128]{0:T(256)(128)(2,1)S(1)}, bf16[128]{0:T(256)(128)(2,1)}, u32[]{:S(2)}) copy-start(bf16[128]{0:T(256)(128)(2,1)} %param.27) | copy-start | bytes 772
  143.8 14.7 %all-to-all-start.1 = ((bf16[32,2,512]{2,1,0:T(2,128)(2,1)}), bf16[32,2,512]{2,1,0:T(2,128)(2,1)S(1)}, u32[]{:S(2)}, u32[]{:S(2)}) async-start(bf16[32,2,512]{2,1,0:T(2,128)(2,1)} %reshape.224), calls=%async_computation.2 | async-start | bytes 131072 | tf_op jit(solution)/shard_map/all_to_all | solution.py:127
  166.1 23.3 %copy-start.2 = (bf16[128,4096]{1,0:T(8,128)(2,1)S(1)}, bf16[128,4096]{1,0:T(8,128)(2,1)}, u32[]{:S(2)}) copy-start(bf16[128,4096]{1,0:T(8,128)(2,1)} %param.28) | copy-start | bytes 3145732
  200.7 7.8 %copy-start.5 = (bf16[1024]{0:T(1024)(128)(2,1)S(1)}, bf16[1024]{0:T(1024)(128)(2,1)}, u32[]{:S(2)}) copy-start(bf16[1024]{0:T(1024)(128)(2,1)} %param.29) | copy-start | bytes 6148
  200.7 111.0 %all-to-all-start.2 = ((bf16[128,32,1024]{2,1,0:T(8,128)(2,1)}), bf16[128,32,1024]{2,1,0:T(8,128)(2,1)}, u32[]{:S(2)}, u32[]{:S(2)}) async-start(bf16[128,32,1024]{2,1,0:T(8,128)(2,1)} %bitcast.122), calls=%async_computation.3 | async-start | bytes 16777216 | tf_op jit(solution)/shard_map/all_to_all | solution.py:152
  208.5 109.0 %copy-start.1 = (bf16[4096,128]{1,0:T(8,128)(2,1)S(1)}, bf16[4096,128]{1,0:T(8,128)(2,1)}, u32[]{:S(2)}) copy-start(bf16[4096,128]{1,0:T(8,128)(2,1)} %param.26) | copy-start | bytes 3145732
  208.5 108.3 %copy-start.4 = (bf16[32,1024]{1,0:T(8,128)(2,1)S(1)}, bf16[32,1024]{1,0:T(8,128)(2,1)}, u32[]{:S(2)}) copy-start(bf16[32,1024]{1,0:T(8,128)(2,1)} %param.15) | copy-start | bytes 196612
Sparse Core Ops, SparseCore 0:
  45.5 81.5 reduce-scatter.1
  129.3 54.2 all-gather.1

commit v2 on v1

--- a/solution.py
+++ b/solution.py
@@ -125,7 +125,19 @@
     attended = (mixed / denom[..., None]).astype(jnp.bfloat16)
     transposed = jnp.transpose(attended, (2, 1, 0))
     slices = lax.all_to_all(transposed, "grp", split_axis=0, concat_axis=2, tiled=True)
+    slices = lax.all_gather(slices, "head", axis=1, tiled=True)
     dim_here = slices.shape[0]
+    out_blocks = lax.all_to_all(
+        w_attn_out.reshape(dim_here, heads_here, head_count, width_here),
+        "head",
+        split_axis=2,
+        concat_axis=1,
+        tiled=True,
+    ).reshape(dim_here, heads_here * head_count, width_here)
+    units = w_in.shape[1]
+    down_blocks = lax.all_to_all(
+        w_down.reshape(units, head_count, width_here), "head", split_axis=1, concat_axis=0, tiled=True
+    ).reshape(units * head_count, width_here)
     hidden = jax.nn.gelu(
         jnp.dot(
             lax.all_gather(normed, "grp", axis=0, tiled=True),
@@ -135,23 +147,13 @@
         + b_in.astype(jnp.float32),
         approximate=True,
     ).astype(jnp.bfloat16)
-    units = hidden.shape[1]
-    mlp_part = jnp.einsum(
-        "gri,ihf->ghrf",
-        hidden.reshape(grp_count, local_rows, units),
-        w_down.reshape(units, head_count, width_here),
-        preferred_element_type=jnp.float32,
-    )
-    attn_part = jnp.einsum(
-        "dkgr,dkhf->ghrf",
-        slices.reshape(dim_here, heads_here, grp_count, local_rows),
-        w_attn_out.reshape(dim_here, heads_here, head_count, width_here),
-        preferred_element_type=jnp.float32,
-    )
-    combined = (mlp_part + attn_part).reshape(grp_count * head_count * local_rows, width_here)
+    hidden = lax.all_gather(hidden, "head", axis=1, tiled=True)
+    mlp_part = jnp.dot(hidden, down_blocks, preferred_element_type=jnp.float32)
+    attn_part = jnp.einsum("dkr,dkf->rf", slices, out_blocks, preferred_element_type=jnp.float32)
+    combined = mlp_part + attn_part
     pieces = lax.all_to_all(
-        combined.astype(jnp.bfloat16).reshape(grp_count * head_count, local_rows, width_here),
-        ("grp", "head"),
+        combined.astype(jnp.bfloat16).reshape(grp_count, local_rows, width_here),
+        "grp",
         0,
         0,
         tiled=True,

time: 325 us -> 291 us (0.90)
  waiting for transfers between devices: 208 us -> 173 us
  matrix products: 40.8 us -> 27.4 us
  blocking collectives: 31.2 us -> 40.6 us
  starting transfers between devices: 15.2 us -> 21.3 us
  other arithmetic: 11.7 us -> 6.78 us
  local copies, waits for them, and re-layouts: 3.73 us -> 7.31 us
    all_to_all x1 -> x3, waiting for transfers between devices: 103 us -> 45 us  [the longest x1 28.3 us: local(): lax.all_to_all(combined.astype(jnp.bfloat16).reshape(grp_count, local_row...]
    all_gather x1, waiting for transfers between devices: 17.5 us -> 47.2 us  [local(): lax.all_gather(normed, 'grp', axis=0, tiled=True)]
    dot_general x2, matrix products: 18.7 us -> 4.6 us  [the longest x1 2.52 us: local(): mlp_part = jnp.dot(hidden, down_blocks, preferred_element_type=jnp.float32)]
    all_gather x0 -> x1, blocking collectives: none -> 9.37 us  [local(): slices = lax.all_gather(slices, 'head', axis=1, tiled=True)]
    all_to_all x1 -> x3, starting transfers between devices: 7.82 us -> 14.6 us  [the longest x1 7.23 us: local(): lax.all_to_all(combined.astype(jnp.bfloat16).reshape(grp_count, local_row...]
    reduce_scatter x1, waiting for transfers between devices: 80.3 us -> 74.7 us  [local(): lax.psum_scatter(jnp.einsum('rf,fch->rch', columns, w_qkv, preferred_elem...]
    reduce_sum x1, other arithmetic: 5.22 us -> 0.36 us  [local(): summed = jnp.sum(pieces.astype(jnp.float32), axis=0)]
  transfers between devices with their start and end apart: 4 -> 7, of which waited for: 4 -> 5; matrix products, arithmetic and copies ran while one was open for 8% -> 10% of each run, Pallas kernels for 0% -> 0%
where the time goes in v2:
time: 291 us; the launch traced here: 290 us
  waiting for transfers between devices  173 us (59%)
  blocking collectives  40.6 us (14%)
  matrix products  27.4 us (9%)
  starting transfers between devices  21.3 us (7%)
  between operations  13.5 us (5%)
  local copies, waits for them, and re-layouts  7.31 us (3%)
  other arithmetic  6.78 us (2%)
    reduce_scatter x1, waiting for transfers between devices, local(): lax.psum_scatter(jnp.einsum('rf,fch->rch', columns, w_qkv, preferred_elem...  74.7 us
    all_gather x1, waiting for transfers between devices, local(): lax.all_gather(normed, 'grp', axis=0, tiled=True)  47.2 us
    all_to_all x1, waiting for transfers between devices, local(): lax.all_to_all(combined.astype(jnp.bfloat16).reshape(grp_count, local_row...  28.3 us
    all_to_all x1, blocking collectives, local(): lax.all_to_all(normed, 'grp', split_axis=1, concat_axis=0, tiled=True)  19.9 us
    all_to_all x1, waiting for transfers between devices, local(): lax.all_to_all(w_down.reshape(units, head_count, width_here), 'head', spl...  16.7 us
    all_gather x1, blocking collectives, local(): full_rows = lax.all_gather(activations, 'head', axis=1, tiled=True)  11.3 us
    all_gather x1, blocking collectives, local(): slices = lax.all_gather(slices, 'head', axis=1, tiled=True)  9.37 us
    all_to_all x1, starting transfers between devices, local(): lax.all_to_all(combined.astype(jnp.bfloat16).reshape(grp_count, local_row...  7.23 us
  transfers between devices with their start and end apart: 7, of which 5 were waited for; matrix products, arithmetic and copies ran while one was open for 10% of the time, Pallas kernels for 0%

profile of v2, /device:TPU:1, one launch (start us, length us, event | category | flops | bytes accessed | tf_op | source)
XLA Modules:
  0.0 289.8 jit_solution(4815686804887249399)
XLA Ops:
  6.5 11.3 %all_gather.12 = bf16[32,4096]{1,0:T(8,128)(2,1)S(1)} all-gather(bf16[32,1024]{1,0:T(8,128)(2,1)} %param.15), channel_id=1, replica_groups=mesh['grp'=32,'head'=4] {'head'}, dimensions={1}, use_global_device_ids=true | all-gather | bytes 327680 | tf_op jit(solution)/shard_map/all_gather | solution.py:57
  19.9 19.9 %all_to_all.72 = bf16[32,32,128]{2,0,1:T(8,128)(2,1)S(1)} all-to-all(bf16[32,32,128]{2,0,1:T(8,128)(2,1)S(1)} %copy_bitcast_fusion.1), channel_id=1, replica_groups=mesh['grp'=32,'head'=4] {'grp'}, dimensions={1} | all-to-all | bytes 524288 | tf_op jit(solution)/shard_map/all_to_all | solution.py:61
  39.8 5.6 %convolution_convert_fusion = bf16[1024,3,1024]{2,0,1:T(8,128)(2,1)} fusion(bf16[1024,128,1]{1,0,2:T(8,128)(2,1)S(1)} %bitcast.125, bf16[128,3,1024]{2,0,1:T(8,128)(2,1)} %param.18), kind=kOutput, calls=%fused_computation.9 | convolution fusion | flops 808452096 | bytes 7340032 | tf_op jit(solution)/shard_map/rf,fch->rch/dot_general | solution.py:63
  47.2 3.4 %all-to-all-start.3 = ((bf16[8,4,4,1024]{3,1,0,2:T(4,128)(2,1)}), bf16[8,4,4,1024]{3,1,0,2:T(4,128)(2,1)S(1)}, u32[]{:S(2)}, u32[]{:S(2)}) async-start(bf16[8,4,4,1024]{3,1,0,2:T(4,128)(2,1)} %bitcast.119), calls=%async_computation.4 | async-start | bytes 524288 | tf_op jit(solution)/shard_map/all_to_all | solution.py:130
  50.7 1.3 copy.107
  52.4 74.7 %reduce-scatter.2.cloned.1.call-done = bf16[32,3,1024]{2,0,1:T(8,128)(2,1)} async-done(((bf16[1024,3,1024]{2,0,1:T(8,128)(2,1)}), bf16[32,3,1024]{2,0,1:T(8,128)(2,1)}) %reduce-scatter.2.cloned.1.call-update) | async-done | bytes 196624 | tf_op jit(solution)/shard_map/reduce_scatter | solution.py:62
  127.1 0.9 fusion.60
  130.2 3.5 %fusion.61 = (f32[2,16,4]{1,2,0:T(4,128)S(1)}, f32[2,16,4,1024]{3,1,2,0:T(8,128)S(1)}) fusion(bf16[2,128,4,8,256]{4,3,2,1,0:T(8,128)(2,1)} %bitcast.121, bf16[2,16,4,64]{3,1,2,0:T(8,128)(2,1)S(1)} %copy.112, pred[2,1024]{1,0:T(4,128)(4,1)S(1)} %iota_compare_fusion.1, bf16[2,16,4,192]{3,1,0,2:T(8,128)(2,1)S(1)} %bitcast.129), kind=kOutput, calls=%fused_computation.96 | convolution fusion | flops 67633024 | bytes 4786688 | tf_op jit(solution)/shard_map/gqhd,gjhd->gqhj/dot_general | solution.py:86
  133.8 2.2 fusion.10
  136.5 47.2 %all-gather.3.cloned.1.call-done = bf16[1024,4096]{1,0:T(8,128)(2,1)} async-done(((bf16[32,4096]{1,0:T(8,128)(2,1)}), bf16[1024,4096]{1,0:T(8,128)(2,1)}) %all-gather.3.cloned.1.call-update) | async-done | bytes 8388624 | tf_op jit(solution)/shard_map/all_gather | solution.py:143
  183.7 6.5 %fusion.38 = bf16[1024,128]{1,0:T(8,128)(2,1)} fusion(bf16[1024,4096]{1,0:T(8,128)(2,1)} %all-gather.3.cloned.1.call-done, bf16[4096,128]{1,0:T(8,128)(2,1)S(1)} %copy-done, f32[128]{0:T(128)S(1)} %convert_element_type.74), kind=kOutput, calls=%fused_computation.37 | convolution fusion | flops 1075052544 | bytes 9699840 | tf_op jit(solution)/shard_map/dot_general | solution.py:142
  190.1 2.9 fusion.22
  193.0 0.9 slice_convert_fusion.1
  193.9 4.0 %all-to-all-start = ((bf16[128,4,1024]{0,2,1:T(8,128)(2,1)}), bf16[128,4,1024]{0,2,1:T(8,128)(2,1)S(1)}, u32[]{:S(2)}, u32[]{:S(2)}) async-start(bf16[128,4,1024]{0,2,1:T(8,128)(2,1)} %bitcast), calls=%async_computation | async-start | bytes 2097152 | tf_op jit(solution)/shard_map/all_to_all | solution.py:138
  198.3 2.1 fusion.7
  200.6 0.9 reshape.225
  201.5 16.7 %all-to-all-done = bf16[128,4,1024]{0,2,1:T(8,128)(2,1)S(1)} async-done(((bf16[128,4,1024]{0,2,1:T(8,128)(2,1)}), bf16[128,4,1024]{0,2,1:T(8,128)(2,1)S(1)}, u32[]{:S(2)}, u32[]{:S(2)}) %all-to-all-start) | async-done | bytes 1048608 | tf_op jit(solution)/shard_map/all_to_all | solution.py:138
  218.2 6.6 %all-to-all-start.2 = ((bf16[32,2,512]{2,1,0:T(2,128)(2,1)}), bf16[32,2,512]{2,1,0:T(2,128)(2,1)S(1)}, u32[]{:S(2)}, u32[]{:S(2)}) async-start(bf16[32,2,512]{2,1,0:T(2,128)(2,1)} %reshape.225), calls=%async_computation.3 | async-start | bytes 131072 | tf_op jit(solution)/shard_map/all_to_all | solution.py:127
  226.1 6.0 %all-to-all-done.2 = bf16[32,2,512]{2,1,0:T(2,128)(2,1)S(1)} async-done(((bf16[32,2,512]{2,1,0:T(2,128)(2,1)}), bf16[32,2,512]{2,1,0:T(2,128)(2,1)S(1)}, u32[]{:S(2)}, u32[]{:S(2)}) %all-to-all-start.2) | async-done | bytes 65568 | tf_op jit(solution)/shard_map/all_to_all | solution.py:127
  232.7 9.4 %all_gather.15 = bf16[8,16,1024]{2,0,1:T(8,128)(2,1)S(1)} all-gather(bf16[8,4,1024]{2,0,1:T(8,128)(2,1)S(1)} %all_to_all.62), channel_id=1, replica_groups=mesh['grp'=32,'head'=4] {'head'}, dimensions={1}, use_global_device_ids=true | all-gather | bytes 327680 | tf_op jit(solution)/shard_map/all_gather | solution.py:128
  242.1 2.5 fusion.62
  244.6 2.1 fusion.6
  246.7 7.2 %all-to-all-start.4 = ((bf16[32,32,1024]{2,1,0:T(8,128)(2,1)}), bf16[32,32,1024]{2,1,0:T(8,128)(2,1)S(1)}, u32[]{:S(2)}, u32[]{:S(2)}) async-start(bf16[32,32,1024]{2,1,0:T(8,128)(2,1)} %bitcast.124), calls=%async_computation.5 | async-start | bytes 4194304 | tf_op jit(solution)/shard_map/all_to_all | solution.py:154
  254.0 28.3 %all-to-all-done.4 = bf16[32,32,1024]{2,1,0:T(8,128)(2,1)S(1)} async-done(((bf16[32,32,1024]{2,1,0:T(8,128)(2,1)}), bf16[32,32,1024]{2,1,0:T(8,128)(2,1)S(1)}, u32[]{:S(2)}, u32[]{:S(2)}) %all-to-all-start.4) | async-done | bytes 2097184 | tf_op jit(solution)/shard_map/all_to_all | solution.py:154
  (87 shorter events, 10.3 us)
Async XLA Ops:
  6.5 177.1 %copy-start = (bf16[4096,128]{1,0:T(8,128)(2,1)S(1)}, bf16[4096,128]{1,0:T(8,128)(2,1)}, u32[]{:S(2)}) copy-start(bf16[4096,128]{1,0:T(8,128)(2,1)} %param.26) | copy-start | bytes 3145732
  6.5 120.6 %reduce-scatter.2.cloned.1.call-start = ((), (), s32[]{:S(2)}) async-start(), calls=%async_computation.8 | async-start | bytes 6488064 | tf_op jit(solution)/shard_map/reduce_scatter | solution.py:62
  45.4 1.0 copy-start.2
  45.4 5.2 %copy-start.8 = (bf16[128]{0:T(256)(128)(2,1)S(1)}, bf16[128]{0:T(256)(128)(2,1)}, u32[]{:S(2)}) copy-start(bf16[128]{0:T(256)(128)(2,1)} %param.27) | copy-start | bytes 772
  45.4 5.3 %copy-start.1 = (bf16[128,4096]{1,0:T(8,128)(2,1)S(1)}, bf16[128,4096]{1,0:T(8,128)(2,1)}, u32[]{:S(2)}) copy-start(bf16[128,4096]{1,0:T(8,128)(2,1)} %param.28) | copy-start | bytes 3145732
  45.4 6.6 %copy-start.7 = (s32[2]{0:T(128)S(1)}, s32[2]{0:T(128)}, u32[]{:S(2)}) copy-start(s32[2]{0:T(128)} %param.23) | copy-start | bytes 28
  45.4 6.7 %copy-start.6 = (s32[32]{0:T(128)S(1)}, s32[32]{0:T(128)}, u32[]{:S(2)}) copy-start(s32[32]{0:T(128)} %param.24) | copy-start | bytes 388
  45.4 138.2 %all-gather.3.cloned.1.call-start = ((), (), s32[]{:S(2)}) async-start(), calls=%async_computation.6 | async-start | bytes 8650752 | tf_op jit(solution)/shard_map/all_gather | solution.py:143
  47.2 146.7 %all-to-all-start.3 = ((bf16[8,4,4,1024]{3,1,0,2:T(4,128)(2,1)}), bf16[8,4,4,1024]{3,1,0,2:T(4,128)(2,1)S(1)}, u32[]{:S(2)}, u32[]{:S(2)}) async-start(bf16[8,4,4,1024]{3,1,0,2:T(4,128)(2,1)} %bitcast.119), calls=%async_computation.4 | async-start | bytes 524288 | tf_op jit(solution)/shard_map/all_to_all | solution.py:130
  50.6 191.5 %all-gather.5.cloned.1.call-start = ((), (), s32[]{:S(2)}) async-start(), calls=%async_computation.7 | async-start | bytes 1310720 | tf_op jit(solution)/shard_map/all_gather | solution.py:150
  193.9 24.3 %all-to-all-start = ((bf16[128,4,1024]{0,2,1:T(8,128)(2,1)}), bf16[128,4,1024]{0,2,1:T(8,128)(2,1)S(1)}, u32[]{:S(2)}, u32[]{:S(2)}) async-start(bf16[128,4,1024]{0,2,1:T(8,128)(2,1)} %bitcast), calls=%async_computation | async-start | bytes 2097152 | tf_op jit(solution)/shard_map/all_to_all | solution.py:138
  218.2 13.9 %all-to-all-start.2 = ((bf16[32,2,512]{2,1,0:T(2,128)(2,1)}), bf16[32,2,512]{2,1,0:T(2,128)(2,1)S(1)}, u32[]{:S(2)}, u32[]{:S(2)}) async-start(bf16[32,2,512]{2,1,0:T(2,128)(2,1)} %reshape.225), calls=%async_computation.3 | async-start | bytes 131072 | tf_op jit(solution)/shard_map/all_to_all | solution.py:127
  242.1 2.5 copy-start.3
  246.7 7.2 %copy-start.5 = (bf16[1024]{0:T(1024)(128)(2,1)S(1)}, bf16[1024]{0:T(1024)(128)(2,1)}, u32[]{:S(2)}) copy-start(bf16[1024]{0:T(1024)(128)(2,1)} %param.29) | copy-start | bytes 6148
  246.7 35.9 %copy-start.4 = (bf16[32,1024]{1,0:T(8,128)(2,1)S(1)}, bf16[32,1024]{1,0:T(8,128)(2,1)}, u32[]{:S(2)}) copy-start(bf16[32,1024]{1,0:T(8,128)(2,1)} %param.15) | copy-start | bytes 196612
  246.7 35.5 %all-to-all-start.4 = ((bf16[32,32,1024]{2,1,0:T(8,128)(2,1)}), bf16[32,32,1024]{2,1,0:T(8,128)(2,1)S(1)}, u32[]{:S(2)}, u32[]{:S(2)}) async-start(bf16[32,32,1024]{2,1,0:T(8,128)(2,1)} %bitcast.124), calls=%async_computation.5 | async-start | bytes 4194304 | tf_op jit(solution)/shard_map/all_to_all | solution.py:154
Sparse Core Ops, SparseCore 0:
  45.6 81.5 reduce-scatter.1
  129.4 54.2 all-gather.2
  190.3 31.6 all-gather.4

commit v3 on v2

--- a/solution.py
+++ b/solution.py
@@ -58,7 +58,9 @@
     normed = normalize(full_rows, ln_gain, ln_bias)
     local_rows = normed.shape[0]
     groups_here = prompt_len.shape[0]
-    columns = lax.all_to_all(normed, "grp", split_axis=1, concat_axis=0, tiled=True)
+    gathered = lax.all_gather(normed, "grp", axis=0, tiled=True)
+    block = w_qkv.shape[0]
+    columns = lax.dynamic_slice_in_dim(gathered, lax.axis_index("grp") * block, block, axis=1)
     qkv = lax.psum_scatter(
         jnp.einsum("rf,fch->rch", columns, w_qkv, preferred_element_type=jnp.float32).astype(
             jnp.bfloat16
@@ -140,7 +142,7 @@
     ).reshape(units * head_count, width_here)
     hidden = jax.nn.gelu(
         jnp.dot(
-            lax.all_gather(normed, "grp", axis=0, tiled=True),
+            gathered,
             w_in,
             preferred_element_type=jnp.float32,
         )

time: 291 us -> 263 us (0.904)
  blocking collectives: 40.6 us -> 21.9 us
  waiting for transfers between devices: 173 us -> 155 us
  matrix products: 27.4 us -> 31.8 us
  starting transfers between devices: 21.3 us -> 25.6 us
    reduce_scatter x1, waiting for transfers between devices: 74.7 us -> 48 us  [local(): lax.psum_scatter(jnp.einsum('rf,fch->rch', columns, w_qkv, preferred_elem...]
    all_to_all x1 -> x0, blocking collectives: 19.9 us -> none  [local(): lax.all_to_all(normed, 'grp', split_axis=1, concat_axis=0, tiled=True)]
    all_gather x1, waiting for transfers between devices: 47.2 us -> 57.6 us  [local(): gathered = lax.all_gather(normed, 'grp', axis=0, tiled=True)]
    all_to_all x1, waiting for transfers between devices: 6 us -> 0.26 us  [local(): lax.all_to_all(transposed, 'grp', split_axis=0, concat_axis=2, tiled=True)]
    all_to_all x1, waiting for transfers between devices: 0.01 us -> 4.51 us  [local(): lax.all_to_all(w_attn_out.reshape(dim_here, heads_here, head_count, width...]
    all_to_all x1, waiting for transfers between devices: 16.7 us -> 13 us  [local(): lax.all_to_all(w_down.reshape(units, head_count, width_here), 'head', spl...]
    all_to_all x1, starting transfers between devices: 7.23 us -> 10.7 us  [local(): lax.all_to_all(combined.astype(jnp.bfloat16).reshape(grp_count, local_row...]
  transfers between devices with their start and end apart: 7 -> 7, of which waited for: 5 -> 7; matrix products, arithmetic and copies ran while one was open for 10% -> 12% of each run, Pallas kernels for 0% -> 0%
where the time goes in v3:
time: 263 us; the launch traced here: 262 us
  waiting for transfers between devices  155 us (59%)
  matrix products  31.8 us (12%)
  starting transfers between devices  25.6 us (10%)
  blocking collectives  21.9 us (8%)
  between operations  13.5 us (5%)
  local copies, waits for them, and re-layouts  7.5 us (3%)
  other arithmetic  6.63 us (3%)
    all_gather x1, waiting for transfers between devices, local(): gathered = lax.all_gather(normed, 'grp', axis=0, tiled=True)  57.6 us
    reduce_scatter x1, waiting for transfers between devices, local(): lax.psum_scatter(jnp.einsum('rf,fch->rch', columns, w_qkv, preferred_elem...  48 us
    all_to_all x1, waiting for transfers between devices, local(): lax.all_to_all(combined.astype(jnp.bfloat16).reshape(grp_count, local_row...  28.6 us
    all_to_all x1, waiting for transfers between devices, local(): lax.all_to_all(w_down.reshape(units, head_count, width_here), 'head', spl...  13 us
    all_gather x1, blocking collectives, local(): full_rows = lax.all_gather(activations, 'head', axis=1, tiled=True)  11.3 us
    all_to_all x1, starting transfers between devices, local(): lax.all_to_all(combined.astype(jnp.bfloat16).reshape(grp_count, local_row...  10.7 us
    all_gather x1, blocking collectives, local(): slices = lax.all_gather(slices, 'head', axis=1, tiled=True)  10.6 us
    all_to_all x1, starting transfers between devices, local(): lax.all_to_all(transposed, 'grp', split_axis=0, concat_axis=2, tiled=True)  7.34 us
  transfers between devices with their start and end apart: 7, of which 7 were waited for; matrix products, arithmetic and copies ran while one was open for 12% of the time, Pallas kernels for 0%

profile of v3, /device:TPU:1, one launch (start us, length us, event | category | flops | bytes accessed | tf_op | source)
XLA Modules:
  0.0 261.5 jit_solution(5359865503402456944)
XLA Ops:
  6.5 11.3 %all_gather.12 = bf16[32,4096]{1,0:T(8,128)(2,1)S(1)} all-gather(bf16[32,1024]{1,0:T(8,128)(2,1)} %param.15), channel_id=1, replica_groups=mesh['grp'=32,'head'=4] {'head'}, dimensions={1}, use_global_device_ids=true | all-gather | bytes 327680 | tf_op jit(solution)/shard_map/all_gather | solution.py:57
  19.7 0.9 fusion.30
  20.6 57.6 %all-gather.3.cloned.1.call-done = bf16[1024,4096]{1,0:T(8,128)(2,1)} async-done(((bf16[32,4096]{1,0:T(8,128)(2,1)}), bf16[1024,4096]{1,0:T(8,128)(2,1)}) %all-gather.3.cloned.1.call-update) | async-done | bytes 8388624 | tf_op jit(solution)/shard_map/all_gather | solution.py:61
  78.3 5.7 %convolution_convert_fusion = bf16[1024,3,1024]{2,0,1:T(8,128)(2,1)} fusion(bf16[128,3,1024]{2,0,1:T(8,128)(2,1)} %param.18, bf16[1024,4096]{1,0:T(8,128)(2,1)} %all-gather.3.cloned.1.call-done, s32[]{:T(128)S(6)} %select_n.27), kind=kOutput, calls=%fused_computation.9 | convolution fusion | flops 808452096 | bytes 7340036 | tf_op jit(solution)/shard_map/rf,fch->rch/dot_general | solution.py:65
  84.0 0.9 copy-done.2
  85.7 4.0 %all-to-all-start.2 = ((bf16[8,4,4,1024]{3,1,0,2:T(4,128)(2,1)}), bf16[8,4,4,1024]{3,1,0,2:T(4,128)(2,1)S(1)}, u32[]{:S(2)}, u32[]{:S(2)}) async-start(bf16[8,4,4,1024]{3,1,0,2:T(4,128)(2,1)} %bitcast.111), calls=%async_computation.3 | async-start | bytes 524288 | tf_op jit(solution)/shard_map/all_to_all | solution.py:132
  89.7 1.3 copy.102
  91.1 4.5 %all-to-all-done.2 = bf16[8,4,4,1024]{3,1,0,2:T(4,128)(2,1)S(1)} async-done(((bf16[8,4,4,1024]{3,1,0,2:T(4,128)(2,1)}), bf16[8,4,4,1024]{3,1,0,2:T(4,128)(2,1)S(1)}, u32[]{:S(2)}, u32[]{:S(2)}) %all-to-all-start.2) | async-done | bytes 262176 | tf_op jit(solution)/shard_map/all_to_all | solution.py:132
  95.6 3.5 %all-to-all-start = ((bf16[128,4,1024]{0,2,1:T(8,128)(2,1)}), bf16[128,4,1024]{0,2,1:T(8,128)(2,1)S(1)}, u32[]{:S(2)}, u32[]{:S(2)}) async-start(bf16[128,4,1024]{0,2,1:T(8,128)(2,1)} %bitcast), calls=%async_computation | async-start | bytes 2097152 | tf_op jit(solution)/shard_map/all_to_all | solution.py:140
  99.7 13.0 %all-to-all-done = bf16[128,4,1024]{0,2,1:T(8,128)(2,1)S(1)} async-done(((bf16[128,4,1024]{0,2,1:T(8,128)(2,1)}), bf16[128,4,1024]{0,2,1:T(8,128)(2,1)S(1)}, u32[]{:S(2)}, u32[]{:S(2)}) %all-to-all-start) | async-done | bytes 1048608 | tf_op jit(solution)/shard_map/all_to_all | solution.py:140
  113.2 6.8 %fusion.38 = bf16[1024,128]{1,0:T(8,128)(2,1)} fusion(bf16[1024,4096]{1,0:T(8,128)(2,1)} %all-gather.3.cloned.1.call-done, bf16[4096,128]{1,0:T(8,128)(2,1)S(1)} %copy-done, f32[128]{0:T(128)S(1)} %convert_element_type.74), kind=kOutput, calls=%fused_computation.37 | convolution fusion | flops 1075052544 | bytes 9699840 | tf_op jit(solution)/shard_map/dot_general | solution.py:144
  120.0 48.0 %reduce-scatter.2.cloned.1.call-done = bf16[32,3,1024]{2,0,1:T(8,128)(2,1)} async-done(((bf16[1024,3,1024]{2,0,1:T(8,128)(2,1)}), bf16[32,3,1024]{2,0,1:T(8,128)(2,1)}) %reduce-scatter.2.cloned.1.call-update) | async-done | bytes 196624 | tf_op jit(solution)/shard_map/reduce_scatter | solution.py:64
  168.0 0.9 fusion.63
  171.1 3.5 %fusion.64 = (f32[2,16,4]{1,2,0:T(4,128)S(1)}, f32[2,16,4,1024]{3,1,2,0:T(8,128)S(1)}) fusion(bf16[2,128,4,8,256]{4,3,2,1,0:T(8,128)(2,1)} %bitcast.113, bf16[2,16,4,64]{3,1,2,0:T(8,128)(2,1)S(1)} %copy.106, pred[2,1024]{1,0:T(4,128)(4,1)S(1)} %iota_compare_fusion.1, bf16[2,16,4,192]{3,1,0,2:T(8,128)(2,1)S(1)} %bitcast.120), kind=kOutput, calls=%fused_computation.98 | convolution fusion | flops 67633024 | bytes 4786688 | tf_op jit(solution)/shard_map/gqhd,gjhd->gqhj/dot_general | solution.py:88
  174.6 2.2 fusion.10
  177.4 2.9 %fusion.22 = f32[2,16,4,256]{3,1,2,0:T(8,128)S(1)} fusion(bf16[2,128,4,8,256]{4,3,2,1,0:T(8,128)(2,1)} %bitcast.114, f32[2,16,4,1024]{3,1,2,0:T(8,128)S(1)} %get-tuple-element.20, f32[2,16,4]{1,2,0:T(4,128)S(1)} %copy.113), kind=kOutput, calls=%fused_computation.20 | convolution fusion | flops 67371008 | bytes 4850176 | tf_op jit(solution)/shard_map/gqhj,gjhd->gqhd/dot_general | solution.py:114
  181.5 2.0 fusion.7
  184.7 7.3 %all-to-all-start.1 = ((bf16[32,2,512]{2,1,0:T(2,128)(2,1)}), bf16[32,2,512]{2,1,0:T(2,128)(2,1)S(1)}, u32[]{:S(2)}, u32[]{:S(2)}) async-start(bf16[32,2,512]{2,1,0:T(2,128)(2,1)} %reshape.222), calls=%async_computation.2 | async-start | bytes 131072 | tf_op jit(solution)/shard_map/all_to_all | solution.py:129
  192.0 2.6 %all-gather.5.cloned.1.call-done = bf16[1024,512]{1,0:T(8,128)(2,1)} async-done(((bf16[1024,128]{1,0:T(8,128)(2,1)}), bf16[1024,512]{1,0:T(8,128)(2,1)}) %all-gather.5.cloned.1.call-update) | async-done | bytes 1048592 | tf_op jit(solution)/shard_map/all_gather | solution.py:152
  194.6 4.4 %fusion.65 = f32[1024,1024]{1,0:T(8,128)} fusion(bf16[1024,512]{1,0:T(8,128)(2,1)} %all-gather.5.cloned.1.call-done, bf16[512,1024]{1,0:T(8,128)(2,1)S(1)} %bitcast.117), kind=kOutput, calls=%fused_computation.99 | convolution fusion | flops 1073741824 | bytes 6291456 | tf_op jit(solution)/shard_map/dot_general | solution.py:153
  199.9 10.6 %all_gather.15 = bf16[8,16,1024]{2,0,1:T(8,128)(2,1)S(1)} all-gather(bf16[8,4,1024]{2,0,1:T(8,128)(2,1)S(1)} %all_to_all.44), channel_id=1, replica_groups=mesh['grp'=32,'head'=4] {'head'}, dimensions={1}, use_global_device_ids=true | all-gather | bytes 327680 | tf_op jit(solution)/shard_map/all_gather | solution.py:130
  210.5 4.3 %fusion.6 = bf16[1024,1024]{1,0:T(8,128)(2,1)} fusion(f32[1024,1024]{1,0:T(8,128)} %fusion.65, bf16[8,16,1024]{2,0,1:T(8,128)(2,1)S(1)} %all_gather.15, bf16[8,16,1024]{2,0,1:T(8,128)(2,1)S(1)} %bitcast.127), kind=kOutput, calls=%fused_computation.7 | convolution fusion | flops 270532608 | bytes 6815744 | tf_op jit(solution)/shard_map/dkr,dkf->rf/dot_general | solution.py:154
  214.7 10.7 %all-to-all-start.3 = ((bf16[32,32,1024]{2,1,0:T(8,128)(2,1)}), bf16[32,32,1024]{2,1,0:T(8,128)(2,1)S(1)}, u32[]{:S(2)}, u32[]{:S(2)}) async-start(bf16[32,32,1024]{2,1,0:T(8,128)(2,1)} %bitcast.116), calls=%async_computation.4 | async-start | bytes 4194304 | tf_op jit(solution)/shard_map/all_to_all | solution.py:156
  225.4 28.6 %all-to-all-done.3 = bf16[32,32,1024]{2,1,0:T(8,128)(2,1)S(1)} async-done(((bf16[32,32,1024]{2,1,0:T(8,128)(2,1)}), bf16[32,32,1024]{2,1,0:T(8,128)(2,1)S(1)}, u32[]{:S(2)}, u32[]{:S(2)}) %all-to-all-start.3) | async-done | bytes 2097184 | tf_op jit(solution)/shard_map/all_to_all | solution.py:156
  (83 shorter events, 10.5 us)
Async XLA Ops:
  6.5 106.7 %copy-start = (bf16[4096,128]{1,0:T(8,128)(2,1)S(1)}, bf16[4096,128]{1,0:T(8,128)(2,1)}, u32[]{:S(2)}) copy-start(bf16[4096,128]{1,0:T(8,128)(2,1)} %param.26) | copy-start | bytes 3145732
  6.5 71.7 %all-gather.3.cloned.1.call-start = ((), (), s32[]{:S(2)}) async-start(), calls=%async_computation.5 | async-start | bytes 8650752 | tf_op jit(solution)/shard_map/all_gather | solution.py:61
  20.6 147.4 %reduce-scatter.2.cloned.1.call-start = ((), (), s32[]{:S(2)}) async-start(), calls=%async_computation.7 | async-start | bytes 6488064 | tf_op jit(solution)/shard_map/reduce_scatter | solution.py:64
  84.0 0.9 copy-start.2
  84.0 5.7 %copy-start.1 = (bf16[128,4096]{1,0:T(8,128)(2,1)S(1)}, bf16[128,4096]{1,0:T(8,128)(2,1)}, u32[]{:S(2)}) copy-start(bf16[128,4096]{1,0:T(8,128)(2,1)} %param.28) | copy-start | bytes 3145732
  84.0 7.1 %copy-start.6 = (s32[2]{0:T(128)S(1)}, s32[2]{0:T(128)}, u32[]{:S(2)}) copy-start(s32[2]{0:T(128)} %param.23) | copy-start | bytes 28
  84.0 15.2 %copy-start.5 = (s32[32]{0:T(128)S(1)}, s32[32]{0:T(128)}, u32[]{:S(2)}) copy-start(s32[32]{0:T(128)} %param.24) | copy-start | bytes 388
  84.0 15.2 %copy-start.7 = (bf16[128]{0:T(256)(128)(2,1)S(1)}, bf16[128]{0:T(256)(128)(2,1)}, u32[]{:S(2)}) copy-start(bf16[128]{0:T(256)(128)(2,1)} %param.27) | copy-start | bytes 772
  85.7 9.9 %all-to-all-start.2 = ((bf16[8,4,4,1024]{3,1,0,2:T(4,128)(2,1)}), bf16[8,4,4,1024]{3,1,0,2:T(4,128)(2,1)S(1)}, u32[]{:S(2)}, u32[]{:S(2)}) async-start(bf16[8,4,4,1024]{3,1,0,2:T(4,128)(2,1)} %bitcast.111), calls=%async_computation.3 | async-start | bytes 524288 | tf_op jit(solution)/shard_map/all_to_all | solution.py:132
  95.6 17.0 %all-to-all-start = ((bf16[128,4,1024]{0,2,1:T(8,128)(2,1)}), bf16[128,4,1024]{0,2,1:T(8,128)(2,1)S(1)}, u32[]{:S(2)}, u32[]{:S(2)}) async-start(bf16[128,4,1024]{0,2,1:T(8,128)(2,1)} %bitcast), calls=%async_computation | async-start | bytes 2097152 | tf_op jit(solution)/shard_map/all_to_all | solution.py:140
  99.2 95.4 %all-gather.5.cloned.1.call-start = ((), (), s32[]{:S(2)}) async-start(), calls=%async_computation.6 | async-start | bytes 1310720 | tf_op jit(solution)/shard_map/all_gather | solution.py:152
  184.7 14.7 %all-to-all-start.1 = ((bf16[32,2,512]{2,1,0:T(2,128)(2,1)}), bf16[32,2,512]{2,1,0:T(2,128)(2,1)S(1)}, u32[]{:S(2)}, u32[]{:S(2)}) async-start(bf16[32,2,512]{2,1,0:T(2,128)(2,1)} %reshape.222), calls=%async_computation.2 | async-start | bytes 131072 | tf_op jit(solution)/shard_map/all_to_all | solution.py:129
  214.7 10.7 %copy-start.4 = (bf16[1024]{0:T(1024)(128)(2,1)S(1)}, bf16[1024]{0:T(1024)(128)(2,1)}, u32[]{:S(2)}) copy-start(bf16[1024]{0:T(1024)(128)(2,1)} %param.29) | copy-start | bytes 6148
  214.7 39.6 %copy-start.3 = (bf16[32,1024]{1,0:T(8,128)(2,1)S(1)}, bf16[32,1024]{1,0:T(8,128)(2,1)}, u32[]{:S(2)}) copy-start(bf16[32,1024]{1,0:T(8,128)(2,1)} %param.15) | copy-start | bytes 196612
  214.7 39.3 %all-to-all-start.3 = ((bf16[32,32,1024]{2,1,0:T(8,128)(2,1)}), bf16[32,32,1024]{2,1,0:T(8,128)(2,1)S(1)}, u32[]{:S(2)}, u32[]{:S(2)}) async-start(bf16[32,32,1024]{2,1,0:T(8,128)(2,1)} %bitcast.116), calls=%async_computation.4 | async-start | bytes 4194304 | tf_op jit(solution)/shard_map/all_to_all | solution.py:156
Sparse Core Ops, SparseCore 0:
  20.7 57.5 all-gather.2
  84.1 83.8 reduce-scatter.1
  169.7 24.9 all-gather.4

commit v4 on v3

--- a/solution.py
+++ b/solution.py
@@ -60,15 +60,28 @@
     groups_here = prompt_len.shape[0]
     gathered = lax.all_gather(normed, "grp", axis=0, tiled=True)
     block = w_qkv.shape[0]
-    columns = lax.dynamic_slice_in_dim(gathered, lax.axis_index("grp") * block, block, axis=1)
-    qkv = lax.psum_scatter(
-        jnp.einsum("rf,fch->rch", columns, w_qkv, preferred_element_type=jnp.float32).astype(
-            jnp.bfloat16
-        ),
-        "grp",
-        scatter_dimension=0,
-        tiled=True,
-    ).astype(jnp.float32)
+    pair_rows = normed.reshape(local_rows, grp_count // 2, 2 * block)
+    columns = lax.all_to_all(
+        jnp.repeat(pair_rows, 2, axis=1), "grp", split_axis=1, concat_axis=0, tiled=True
+    ).reshape(grp_count * local_rows, 2 * block)
+    parity = lax.axis_index("grp") % 2
+    half = w_qkv.shape[2] // 2
+    own = lax.dynamic_slice_in_dim(w_qkv, parity * half, half, axis=2)
+    other = lax.dynamic_slice_in_dim(w_qkv, (1 - parity) * half, half, axis=2)
+    sibling = lax.ppermute(other, "grp", [(i, i ^ 1) for i in range(grp_count)])
+    pair_weights = jnp.where(
+        parity == 0,
+        jnp.concatenate([own, sibling], axis=0),
+        jnp.concatenate([sibling, own], axis=0),
+    )
+    term = jnp.einsum(
+        "rf,fch->rch", columns, pair_weights, preferred_element_type=jnp.float32
+    ).astype(jnp.bfloat16)
+    received = lax.all_to_all(
+        term.reshape(grp_count, local_rows, 3, half), "grp", 0, 0, tiled=True
+    ).reshape(grp_count // 2, 2, local_rows, 3, half)
+    qkv = jnp.sum(received.astype(jnp.float32), axis=0)
+    qkv = jnp.transpose(qkv, (1, 2, 0, 3)).reshape(local_rows, 3, 2 * half)
     heads_here = w_qkv.shape[2] // HS
     member = (jnp.arange(local_rows) // GSIZE)[:, None] == jnp.arange(groups_here)[None, :]
     row_prompt = jnp.sum(jnp.where(member, prompt_len[None, :], 0), axis=1)

time: 263 us -> 233 us (0.89)
  waiting for transfers between devices: 155 us -> 120 us
  starting transfers between devices: 25.6 us -> 35.2 us
  matrix products: 31.8 us -> 22.7 us
    all_to_all x0 -> x2, waiting for transfers between devices: none -> 65.9 us  [the longest x1 54.1 us: local(): lax.all_to_all(term.reshape(grp_count, local_rows, 3, half), 'grp', 0, 0,...]
    all_gather x1, waiting for transfers between devices: 57.6 us -> 0.02 us  [local(): gathered = lax.all_gather(normed, 'grp', axis=0, tiled=True)]
    reduce_scatter x1 -> x0, waiting for transfers between devices: 48 us -> none  [local(): lax.psum_scatter(jnp.einsum('rf,fch->rch', columns, w_qkv, preferred_elem...]
    all_to_all x0 -> x2, starting transfers between devices: none -> 16.1 us  [the longest x1 11.2 us: local(): lax.all_to_all(jnp.repeat(pair_rows, 2, axis=1), 'grp', split_axis=1, con...]
    all_to_all x1, waiting for transfers between devices: 0.26 us -> 6.8 us  [local(): lax.all_to_all(transposed, 'grp', split_axis=0, concat_axis=2, tiled=True)]
    dot_general x1, matrix products: 5.71 us -> 1.02 us  [local(): jnp.einsum('rf,fch->rch', columns, pair_weights, preferred_element_type=j...]
    all_to_all x1, waiting for transfers between devices: 4.51 us -> 0.01 us  [local(): lax.all_to_all(w_attn_out.reshape(dim_here, heads_here, head_count, width...]
    all_to_all x1, starting transfers between devices: 10.7 us -> 6.25 us  [local(): lax.all_to_all(combined.astype(jnp.bfloat16).reshape(grp_count, local_row...]
  transfers between devices with their start and end apart: 7 -> 9, of which waited for: 7 -> 6; matrix products, arithmetic and copies ran while one was open for 12% -> 14% of each run, Pallas kernels for 0% -> 0%
where the time goes in v4:
time: 233 us; the launch traced here: 231 us
  waiting for transfers between devices  120 us (52%)
  starting transfers between devices  35.2 us (15%)
  matrix products  22.7 us (10%)
  blocking collectives  21.5 us (9%)
  between operations  13.9 us (6%)
  local copies, waits for them, and re-layouts  9.85 us (4%)
  other arithmetic  8.3 us (4%)
    all_to_all x1, waiting for transfers between devices, local(): lax.all_to_all(term.reshape(grp_count, local_rows, 3, half), 'grp', 0, 0,...  54.1 us
    all_to_all x1, waiting for transfers between devices, local(): lax.all_to_all(combined.astype(jnp.bfloat16).reshape(grp_count, local_row...  28.3 us
    all_to_all x1, waiting for transfers between devices, local(): lax.all_to_all(w_down.reshape(units, head_count, width_here), 'head', spl...  17.1 us
    all_to_all x1, waiting for transfers between devices, local(): lax.all_to_all(jnp.repeat(pair_rows, 2, axis=1), 'grp', split_axis=1, con...  11.8 us
    all_gather x1, blocking collectives, local(): full_rows = lax.all_gather(activations, 'head', axis=1, tiled=True)  11.3 us
    all_to_all x1, starting transfers between devices, local(): lax.all_to_all(jnp.repeat(pair_rows, 2, axis=1), 'grp', split_axis=1, con...  11.2 us
    all_gather x1, blocking collectives, local(): slices = lax.all_gather(slices, 'head', axis=1, tiled=True)  10.2 us
    all_to_all x1, waiting for transfers between devices, local(): lax.all_to_all(transposed, 'grp', split_axis=0, concat_axis=2, tiled=True)  6.8 us
  transfers between devices with their start and end apart: 9, of which 6 were waited for; matrix products, arithmetic and copies ran while one was open for 14% of the time, Pallas kernels for 0%

profile of v4, /device:TPU:1, one launch (start us, length us, event | category | flops | bytes accessed | tf_op | source)
XLA Modules:
  0.0 231.0 jit_solution(7741205132364805250)
XLA Ops:
  6.5 11.3 %all_gather.12 = bf16[32,4096]{1,0:T(8,128)(2,1)S(1)} all-gather(bf16[32,1024]{1,0:T(8,128)(2,1)} %param.15), channel_id=1, replica_groups=mesh['grp'=32,'head'=4] {'head'}, dimensions={1}, use_global_device_ids=true | all-gather | bytes 327680 | tf_op jit(solution)/shard_map/all_gather | solution.py:57
  22.4 11.2 %all-to-all-start.1 = ((bf16[32,32,256]{2,0,1:T(8,128)(2,1)}), bf16[32,32,256]{2,0,1:T(8,128)(2,1)S(1)}, u32[]{:S(2)}, u32[]{:S(2)}) async-start(bf16[32,32,256]{2,0,1:T(8,128)(2,1)} %bitcast.4), calls=%async_computation.1 | async-start | bytes 1048576 | tf_op jit(solution)/shard_map/all_to_all | solution.py:64
  34.1 1.5 collective-permute-done
  35.6 11.8 %all-to-all-done.1 = bf16[32,32,256]{2,0,1:T(8,128)(2,1)S(1)} async-done(((bf16[32,32,256]{2,0,1:T(8,128)(2,1)}), bf16[32,32,256]{2,0,1:T(8,128)(2,1)S(1)}, u32[]{:S(2)}, u32[]{:S(2)}) %all-to-all-start.1) | async-done | bytes 524320 | tf_op jit(solution)/shard_map/all_to_all | solution.py:64
  48.4 2.1 copy.115
  50.6 4.9 %all-to-all-start.2 = ((bf16[32,32,3,512]{3,1,2,0:T(8,128)(2,1)}), bf16[32,32,3,512]{3,1,2,0:T(8,128)(2,1)}, u32[]{:S(2)}, u32[]{:S(2)}) async-start(bf16[32,32,3,512]{3,1,2,0:T(8,128)(2,1)} %copy.115), calls=%async_computation.2 | async-start | bytes 6291456 | tf_op jit(solution)/shard_map/all_to_all | solution.py:80
  55.6 1.3 copy.112
  58.1 54.1 %all-to-all-done.2 = bf16[32,32,3,512]{3,1,2,0:T(8,128)(2,1)} async-done(((bf16[32,32,3,512]{3,1,2,0:T(8,128)(2,1)}), bf16[32,32,3,512]{3,1,2,0:T(8,128)(2,1)}, u32[]{:S(2)}, u32[]{:S(2)}) %all-to-all-start.2) | async-done | bytes 3145760 | tf_op jit(solution)/shard_map/all_to_all | solution.py:80
  112.2 3.4 %all-to-all-start.4 = ((bf16[8,4,4,1024]{3,1,0,2:T(4,128)(2,1)}), bf16[8,4,4,1024]{3,1,0,2:T(4,128)(2,1)S(1)}, u32[]{:S(2)}, u32[]{:S(2)}) async-start(bf16[8,4,4,1024]{3,1,0,2:T(4,128)(2,1)} %bitcast.126), calls=%async_computation.4 | async-start | bytes 524288 | tf_op jit(solution)/shard_map/all_to_all | solution.py:145
  115.6 2.5 %convert_reduce_fusion = f32[2,32,3,512]{3,1,2,0:T(8,128)S(1)} fusion(bf16[16,2,32,3,512]{4,2,3,1,0:T(8,128)(2,1)} %bitcast.36), kind=kLoop, calls=%fused_computation | loop fusion | flops 3047424 | bytes 3538944 | tf_op jit(solution)/shard_map/reduce_sum | solution.py:83
  120.4 3.5 %fusion.69 = (f32[2,16,4]{1,2,0:T(4,128)S(1)}, f32[2,16,4,1024]{3,1,2,0:T(8,128)S(1)}) fusion(bf16[2,128,4,8,256]{4,3,2,1,0:T(8,128)(2,1)} %bitcast.129, bf16[2,16,4,64]{3,1,2,0:T(8,128)(2,1)S(1)} %copy.120, pred[2,1024]{1,0:T(4,128)(4,1)S(1)} %iota_compare_fusion.1, bf16[2,16,4,192]{3,1,0,2:T(8,128)(2,1)S(1)} %bitcast.142), kind=kOutput, calls=%fused_computation.108 | convolution fusion | flops 67633024 | bytes 4786688 | tf_op jit(solution)/shard_map/gqhd,gjhd->gqhj/dot_general | solution.py:101
  124.0 2.2 fusion.10
  126.7 6.5 %fusion.44 = bf16[1024,128]{1,0:T(8,128)(2,1)} fusion(bf16[1024,4096]{1,0:T(8,128)(2,1)} %all-gather.3.cloned.1.call-done, bf16[4096,128]{1,0:T(8,128)(2,1)S(1)} %copy-done, f32[128]{0:T(128)S(1)} %convert_element_type.77), kind=kOutput, calls=%fused_computation.45 | convolution fusion | flops 1075052544 | bytes 9699840 | tf_op jit(solution)/shard_map/dot_general | solution.py:157
  133.2 2.9 %fusion.22 = f32[2,16,4,256]{3,1,2,0:T(8,128)S(1)} fusion(bf16[2,128,4,8,256]{4,3,2,1,0:T(8,128)(2,1)} %bitcast.130, f32[2,16,4,1024]{3,1,2,0:T(8,128)S(1)} %get-tuple-element.22, f32[2,16,4]{1,2,0:T(4,128)S(1)} %copy.127), kind=kOutput, calls=%fused_computation.21 | convolution fusion | flops 67371008 | bytes 4850176 | tf_op jit(solution)/shard_map/gqhj,gjhd->gqhd/dot_general | solution.py:127
  136.1 4.2 %all-to-all-start = ((bf16[128,4,1024]{0,2,1:T(8,128)(2,1)}), bf16[128,4,1024]{0,2,1:T(8,128)(2,1)S(1)}, u32[]{:S(2)}, u32[]{:S(2)}) async-start(bf16[128,4,1024]{0,2,1:T(8,128)(2,1)} %bitcast), calls=%async_computation | async-start | bytes 2097152 | tf_op jit(solution)/shard_map/all_to_all | solution.py:153
  140.7 2.0 fusion.7
  143.9 17.1 %all-to-all-done = bf16[128,4,1024]{0,2,1:T(8,128)(2,1)S(1)} async-done(((bf16[128,4,1024]{0,2,1:T(8,128)(2,1)}), bf16[128,4,1024]{0,2,1:T(8,128)(2,1)S(1)}, u32[]{:S(2)}, u32[]{:S(2)}) %all-to-all-start) | async-done | bytes 1048608 | tf_op jit(solution)/shard_map/all_to_all | solution.py:153
  160.9 4.9 %all-to-all-start.3 = ((bf16[32,2,512]{2,1,0:T(2,128)(2,1)}), bf16[32,2,512]{2,1,0:T(2,128)(2,1)S(1)}, u32[]{:S(2)}, u32[]{:S(2)}) async-start(bf16[32,2,512]{2,1,0:T(2,128)(2,1)} %reshape.247), calls=%async_computation.3 | async-start | bytes 131072 | tf_op jit(solution)/shard_map/all_to_all | solution.py:142
  166.4 6.8 %all-to-all-done.3 = bf16[32,2,512]{2,1,0:T(2,128)(2,1)S(1)} async-done(((bf16[32,2,512]{2,1,0:T(2,128)(2,1)}), bf16[32,2,512]{2,1,0:T(2,128)(2,1)S(1)}, u32[]{:S(2)}, u32[]{:S(2)}) %all-to-all-start.3) | async-done | bytes 65568 | tf_op jit(solution)/shard_map/all_to_all | solution.py:142
  173.8 10.2 %all_gather.15 = bf16[8,16,1024]{2,0,1:T(8,128)(2,1)S(1)} all-gather(bf16[8,4,1024]{2,0,1:T(8,128)(2,1)S(1)} %all_to_all.62), channel_id=1, replica_groups=mesh['grp'=32,'head'=4] {'head'}, dimensions={1}, use_global_device_ids=true | all-gather | bytes 327680 | tf_op jit(solution)/shard_map/all_gather | solution.py:143
  184.0 2.5 %fusion.70 = f32[1024,1024]{1,0:T(8,128)S(1)} fusion(bf16[1024,512]{1,0:T(8,128)(2,1)} %all-gather.5.cloned.1.call-done, bf16[512,1024]{1,0:T(8,128)(2,1)S(1)} %bitcast.139), kind=kOutput, calls=%fused_computation.109 | convolution fusion | flops 1073741824 | bytes 6291456 | tf_op jit(solution)/shard_map/dot_general | solution.py:166
  186.5 2.1 fusion.6
  188.6 6.2 %all-to-all-start.5 = ((bf16[32,32,1024]{2,1,0:T(8,128)(2,1)}), bf16[32,32,1024]{2,1,0:T(8,128)(2,1)S(1)}, u32[]{:S(2)}, u32[]{:S(2)}) async-start(bf16[32,32,1024]{2,1,0:T(8,128)(2,1)} %bitcast.134), calls=%async_computation.5 | async-start | bytes 4194304 | tf_op jit(solution)/shard_map/all_to_all | solution.py:169
  194.9 28.3 %all-to-all-done.5 = bf16[32,32,1024]{2,1,0:T(8,128)(2,1)S(1)} async-done(((bf16[32,32,1024]{2,1,0:T(8,128)(2,1)}), bf16[32,32,1024]{2,1,0:T(8,128)(2,1)S(1)}, u32[]{:S(2)}, u32[]{:S(2)}) %all-to-all-start.5) | async-done | bytes 2097184 | tf_op jit(solution)/shard_map/all_to_all | solution.py:169
  (94 shorter events, 13.6 us)
Async XLA Ops:
  6.5 120.2 %copy-start = (bf16[4096,128]{1,0:T(8,128)(2,1)S(1)}, bf16[4096,128]{1,0:T(8,128)(2,1)}, u32[]{:S(2)}) copy-start(bf16[4096,128]{1,0:T(8,128)(2,1)} %param.26) | copy-start | bytes 3145732
  6.5 27.2 %copy-start.2 = (bf16[128,3,1024]{2,0,1:T(8,128)(2,1)S(1)}, bf16[128,3,1024]{2,0,1:T(8,128)(2,1)}, u32[]{:S(2)}) copy-start(bf16[128,3,1024]{2,0,1:T(8,128)(2,1)} %param.18) | copy-start | bytes 2359300
  6.5 120.2 %all-gather.3.cloned.1.call-start = ((), (), s32[]{:S(2)}) async-start(), calls=%async_computation.6 | async-start | bytes 8650752 | tf_op jit(solution)/shard_map/all_gather | solution.py:61
  22.4 25.0 %all-to-all-start.1 = ((bf16[32,32,256]{2,0,1:T(8,128)(2,1)}), bf16[32,32,256]{2,0,1:T(8,128)(2,1)S(1)}, u32[]{:S(2)}, u32[]{:S(2)}) async-start(bf16[32,32,256]{2,0,1:T(8,128)(2,1)} %bitcast.4), calls=%async_computation.1 | async-start | bytes 1048576 | tf_op jit(solution)/shard_map/all_to_all | solution.py:64
  33.8 1.8 collective-permute-start
  50.6 4.9 %copy-start.8 = (bf16[128]{0:T(256)(128)(2,1)S(1)}, bf16[128]{0:T(256)(128)(2,1)}, u32[]{:S(2)}) copy-start(bf16[128]{0:T(256)(128)(2,1)} %param.27) | copy-start | bytes 772
  50.6 5.0 %copy-start.1 = (bf16[128,4096]{1,0:T(8,128)(2,1)S(1)}, bf16[128,4096]{1,0:T(8,128)(2,1)}, u32[]{:S(2)}) copy-start(bf16[128,4096]{1,0:T(8,128)(2,1)} %param.28) | copy-start | bytes 3145732
  50.6 6.3 %copy-start.3 = (bf16[8,4,4096]{2,1,0:T(4,128)(2,1)S(1)}, bf16[8,4,4096]{2,1,0:T(4,128)(2,1)}, u32[]{:S(2)}) copy-start(bf16[8,4,4096]{2,1,0:T(4,128)(2,1)} %param.25) | copy-start | bytes 786436
  50.6 7.1 %copy-start.7 = (s32[2]{0:T(128)S(1)}, s32[2]{0:T(128)}, u32[]{:S(2)}) copy-start(s32[2]{0:T(128)} %param.23) | copy-start | bytes 28
  50.6 7.2 %copy-start.6 = (s32[32]{0:T(128)S(1)}, s32[32]{0:T(128)}, u32[]{:S(2)}) copy-start(s32[32]{0:T(128)} %param.24) | copy-start | bytes 388
  50.6 61.5 %all-to-all-start.2 = ((bf16[32,32,3,512]{3,1,2,0:T(8,128)(2,1)}), bf16[32,32,3,512]{3,1,2,0:T(8,128)(2,1)}, u32[]{:S(2)}, u32[]{:S(2)}) async-start(bf16[32,32,3,512]{3,1,2,0:T(8,128)(2,1)} %copy.115), calls=%async_computation.2 | async-start | bytes 6291456 | tf_op jit(solution)/shard_map/all_to_all | solution.py:80
  112.2 23.9 %all-to-all-start.4 = ((bf16[8,4,4,1024]{3,1,0,2:T(4,128)(2,1)}), bf16[8,4,4,1024]{3,1,0,2:T(4,128)(2,1)S(1)}, u32[]{:S(2)}, u32[]{:S(2)}) async-start(bf16[8,4,4,1024]{3,1,0,2:T(4,128)(2,1)} %bitcast.126), calls=%async_computation.4 | async-start | bytes 524288 | tf_op jit(solution)/shard_map/all_to_all | solution.py:145
  115.6 68.4 %all-gather.5.cloned.1.call-start = ((), (), s32[]{:S(2)}) async-start(), calls=%async_computation.7 | async-start | bytes 1310720 | tf_op jit(solution)/shard_map/all_gather | solution.py:165
  136.1 24.8 %all-to-all-start = ((bf16[128,4,1024]{0,2,1:T(8,128)(2,1)}), bf16[128,4,1024]{0,2,1:T(8,128)(2,1)S(1)}, u32[]{:S(2)}, u32[]{:S(2)}) async-start(bf16[128,4,1024]{0,2,1:T(8,128)(2,1)} %bitcast), calls=%async_computation | async-start | bytes 2097152 | tf_op jit(solution)/shard_map/all_to_all | solution.py:153
  160.9 12.3 %all-to-all-start.3 = ((bf16[32,2,512]{2,1,0:T(2,128)(2,1)}), bf16[32,2,512]{2,1,0:T(2,128)(2,1)S(1)}, u32[]{:S(2)}, u32[]{:S(2)}) async-start(bf16[32,2,512]{2,1,0:T(2,128)(2,1)} %reshape.247), calls=%async_computation.3 | async-start | bytes 131072 | tf_op jit(solution)/shard_map/all_to_all | solution.py:142
  188.6 6.3 %copy-start.5 = (bf16[1024]{0:T(1024)(128)(2,1)S(1)}, bf16[1024]{0:T(1024)(128)(2,1)}, u32[]{:S(2)}) copy-start(bf16[1024]{0:T(1024)(128)(2,1)} %param.29) | copy-start | bytes 6148
  188.6 34.9 %copy-start.4 = (bf16[32,1024]{1,0:T(8,128)(2,1)S(1)}, bf16[32,1024]{1,0:T(8,128)(2,1)}, u32[]{:S(2)}) copy-start(bf16[32,1024]{1,0:T(8,128)(2,1)} %param.15) | copy-start | bytes 196612
  188.6 34.6 %all-to-all-start.5 = ((bf16[32,32,1024]{2,1,0:T(8,128)(2,1)}), bf16[32,32,1024]{2,1,0:T(8,128)(2,1)S(1)}, u32[]{:S(2)}, u32[]{:S(2)}) async-start(bf16[32,32,1024]{2,1,0:T(8,128)(2,1)} %bitcast.134), calls=%async_computation.5 | async-start | bytes 4194304 | tf_op jit(solution)/shard_map/all_to_all | solution.py:169
Sparse Core Ops, SparseCore 0:
  20.7 91.0 all-gather.2
  133.3 31.1 all-gather.4

commit v5 on v4

--- a/solution.py
+++ b/solution.py
@@ -32,6 +32,29 @@
     turned = jnp.stack([first * cosine - second * sine, second * cosine + first * sine], axis=-1)
     turned = turned.reshape(values.shape[:-1] + (ROT,))
     return jnp.concatenate([turned, values[..., ROT:]], axis=-1)
+
+
+def head_exchange(pieces, axis):
+    count = lax.axis_size("head")
+    here = lax.axis_index("head")
+    received = []
+    for shift in range(count):
+        piece = lax.dynamic_index_in_dim(pieces, (here + shift) % count, axis, keepdims=False)
+        if shift:
+            piece = lax.ppermute(piece, "head", [(i, (i + shift) % count) for i in range(count)])
+        received.append(piece)
+    stacked = jnp.stack(received, axis=0)
+    return jnp.take(stacked, (here - jnp.arange(count)) % count, axis=0)
+
+
+def head_gather(piece):
+    count = lax.axis_size("head")
+    here = lax.axis_index("head")
+    received = [piece]
+    for shift in range(1, count):
+        received.append(lax.ppermute(piece, "head", [(i, (i + shift) % count) for i in range(count)]))
+    stacked = jnp.stack(received, axis=0)
+    return jnp.take(stacked, (here - jnp.arange(count)) % count, axis=0)
 
 
 def local(
@@ -54,7 +77,7 @@
     grp_count = lax.axis_size("grp")
     head_count = lax.axis_size("head")
     width_here = activations.shape[1]
-    full_rows = lax.all_gather(activations, "head", axis=1, tiled=True)
+    full_rows = jnp.moveaxis(head_gather(activations), 0, 1).reshape(activations.shape[0], -1)
     normed = normalize(full_rows, ln_gain, ln_bias)
     local_rows = normed.shape[0]
     groups_here = prompt_len.shape[0]
@@ -140,19 +163,16 @@
     attended = (mixed / denom[..., None]).astype(jnp.bfloat16)
     transposed = jnp.transpose(attended, (2, 1, 0))
     slices = lax.all_to_all(transposed, "grp", split_axis=0, concat_axis=2, tiled=True)
-    slices = lax.all_gather(slices, "head", axis=1, tiled=True)
     dim_here = slices.shape[0]
-    out_blocks = lax.all_to_all(
-        w_attn_out.reshape(dim_here, heads_here, head_count, width_here),
-        "head",
-        split_axis=2,
-        concat_axis=1,
-        tiled=True,
-    ).reshape(dim_here, heads_here * head_count, width_here)
+    slices = jnp.moveaxis(head_gather(slices), 0, 1).reshape(dim_here, heads_here * head_count, -1)
+    out_blocks = head_exchange(
+        w_attn_out.reshape(dim_here, heads_here, head_count, width_here), 2
+    )
+    out_blocks = jnp.moveaxis(out_blocks, 0, 1).reshape(dim_here, heads_here * head_count, width_here)
     units = w_in.shape[1]
-    down_blocks = lax.all_to_all(
-        w_down.reshape(units, head_count, width_here), "head", split_axis=1, concat_axis=0, tiled=True
-    ).reshape(units * head_count, width_here)
+    down_blocks = head_exchange(w_down.reshape(units, head_count, width_here), 1).reshape(
+        units * head_count, width_here
+    )
     hidden = jax.nn.gelu(
         jnp.dot(
             gathered,

time: 233 us -> 203 us (0.87)
  waiting for transfers between devices: 120 us -> 91.9 us
  blocking collectives: 21.5 us -> 0 us
  starting transfers between devices: 35.2 us -> 45.9 us
  local copies, waits for them, and re-layouts: 9.85 us -> 14.9 us
  other arithmetic: 8.3 us -> 12 us
    all_gather x2 -> x0, blocking collectives: 21.5 us -> none  [the longest x1 11.3 us: local(): full_rows = lax.all_gather(activations, 'head', axis=1, tiled=True)]
    ppermute x0 -> x12, starting transfers between devices: none -> 20.5 us  [the longest x6 11.2 us: head_exchange(): lax.ppermute(piece, 'head', [(i, (i + shift) % count) for i in range(coun...]
    all_to_all x1, waiting for transfers between devices: 54.1 us -> 35.2 us  [local(): lax.all_to_all(term.reshape(grp_count, local_rows, 3, half), 'grp', 0, 0,...]
    all_to_all x2 -> x0, waiting for transfers between devices: 17.1 us -> none  [the longest x1 17.1 us: local(): lax.all_to_all(w_down.reshape(units, head_count, width_here), 'head', spl...]
    ppermute x0 -> x12, waiting for transfers between devices: none -> 9.85 us  [the longest x6 5.57 us: head_gather(): lax.ppermute(piece, 'head', [(i, (i + shift) % count) for i in range(coun...]
    all_to_all x2 -> x0, starting transfers between devices: 7.61 us -> none  [the longest x1 4.2 us: local(): lax.all_to_all(w_down.reshape(units, head_count, width_here), 'head', spl...]
    another operation x2 -> x6, other arithmetic: 0.36 us -> 3.41 us  [the longest x2 1.78 us: head_gather(): stacked = jnp.stack(received, axis=0)]
    gather x0 -> x4, local copies, waits for them, and re-layouts: none -> 3 us  [the longest x2 1.87 us: head_exchange(): return jnp.take(stacked, (here - jnp.arange(count)) % count, axis=0)]
  transfers between devices with their start and end apart: 9 -> 19, of which waited for: 6 -> 12; matrix products, arithmetic and copies ran while one was open for 14% -> 20% of each run, Pallas kernels for 0% -> 0%
where the time goes in v5:
time: 203 us; the launch traced here: 202 us
  waiting for transfers between devices  91.9 us (45%)
  starting transfers between devices  45.9 us (23%)
  matrix products  22.8 us (11%)
  local copies, waits for them, and re-layouts  14.9 us (7%)
  between operations  14.2 us (7%)
  other arithmetic  12 us (6%)
    all_to_all x1, waiting for transfers between devices, local(): lax.all_to_all(term.reshape(grp_count, local_rows, 3, half), 'grp', 0, 0,...  35.2 us
    all_to_all x1, waiting for transfers between devices, local(): lax.all_to_all(combined.astype(jnp.bfloat16).reshape(grp_count, local_row...  28.6 us
    all_to_all x1, waiting for transfers between devices, local(): lax.all_to_all(jnp.repeat(pair_rows, 2, axis=1), 'grp', split_axis=1, con...  11.8 us
    ppermute x6, starting transfers between devices, head_exchange(): lax.ppermute(piece, 'head', [(i, (i + shift) % count) for i in range(coun...  11.2 us
    all_to_all x1, starting transfers between devices, local(): lax.all_to_all(jnp.repeat(pair_rows, 2, axis=1), 'grp', split_axis=1, con...  10.1 us
    ppermute x6, starting transfers between devices, head_gather(): lax.ppermute(piece, 'head', [(i, (i + shift) % count) for i in range(coun...  9.33 us
    dot_general x1, matrix products, local(): jnp.dot(gathered, w_in, preferred_element_type=jnp.float32)  6.46 us
    all_to_all x1, starting transfers between devices, local(): lax.all_to_all(combined.astype(jnp.bfloat16).reshape(grp_count, local_row...  6.16 us
  transfers between devices with their start and end apart: 19, of which 12 were waited for; matrix products, arithmetic and copies ran while one was open for 20% of the time, Pallas kernels for 0%

profile of v5, /device:TPU:1, one launch (start us, length us, event | category | flops | bytes accessed | tf_op | source)
XLA Modules:
  0.0 201.6 jit_solution(12807619556974770179)
XLA Ops:
  6.5 2.1 %collective-permute-start = (bf16[32,1024]{1,0:T(8,128)(2,1)}, bf16[32,1024]{1,0:T(8,128)(2,1)S(1)}, u32[]{:S(2)}, u32[]{:S(2)}) collective-permute-start(bf16[32,1024]{1,0:T(8,128)(2,1)} %param.17), channel_id=1, source_target_pairs={{0,1},{1,2},{2,3},{3,0},{4,5},{5,6},{6,7},{7,4},{8,9},{9,10},{10,1... | collective-permute-start | bytes 196616 | tf_op jit(solution)/shard_map/ppermute | solution.py:55
  8.6 2.5 %collective-permute-start.1 = (bf16[32,1024]{1,0:T(8,128)(2,1)}, bf16[32,1024]{1,0:T(8,128)(2,1)S(1)}, u32[]{:S(2)}, u32[]{:S(2)}) collective-permute-start(bf16[32,1024]{1,0:T(8,128)(2,1)} %param.17), channel_id=1, source_target_pairs={{0,2},{1,3},{2,0},{3,1},{4,6},{5,7},{6,4},{7,5},{8,10},{9,11},{10,... | collective-permute-start | bytes 196616 | tf_op jit(solution)/shard_map/ppermute | solution.py:55
  19.8 10.1 %all-to-all-start = ((bf16[32,32,256]{2,0,1:T(8,128)(2,1)}), bf16[32,32,256]{2,0,1:T(8,128)(2,1)S(1)}, u32[]{:S(2)}, u32[]{:S(2)}) async-start(bf16[32,32,256]{2,0,1:T(8,128)(2,1)} %bitcast.16), calls=%async_computation | async-start | bytes 1048576 | tf_op jit(solution)/shard_map/all_to_all | solution.py:87
  31.8 11.8 %all-to-all-done = bf16[32,32,256]{2,0,1:T(8,128)(2,1)S(1)} async-done(((bf16[32,32,256]{2,0,1:T(8,128)(2,1)}), bf16[32,32,256]{2,0,1:T(8,128)(2,1)S(1)}, u32[]{:S(2)}, u32[]{:S(2)}) %all-to-all-start) | async-done | bytes 524320 | tf_op jit(solution)/shard_map/all_to_all | solution.py:87
  44.6 2.2 %copy.105 = bf16[32,32,3,512]{3,1,2,0:T(8,128)(2,1)} copy(bf16[32,32,3,512]{3,1,0,2:T(8,128)(2,1)S(1)} %bitcast.170) | data formatting | bytes 6291456 | tf_op jit(solution)/shard_map/reshape | solution.py:104
  46.8 4.9 %all-to-all-start.1 = ((bf16[32,32,3,512]{3,1,2,0:T(8,128)(2,1)}), bf16[32,32,3,512]{3,1,2,0:T(8,128)(2,1)}, u32[]{:S(2)}, u32[]{:S(2)}) async-start(bf16[32,32,3,512]{3,1,2,0:T(8,128)(2,1)} %copy.105), calls=%async_computation.1 | async-start | bytes 6291456 | tf_op jit(solution)/shard_map/all_to_all | solution.py:103
  53.6 3.6 %collective-permute-start.4 = (bf16[128,1024]{1,0:T(8,128)(2,1)S(1)}, bf16[128,1024]{1,0:T(8,128)(2,1)}, u32[]{:S(2)}, u32[]{:S(2)}) collective-permute-start(bf16[128,1024]{1,0:T(8,128)(2,1)S(1)} %bitcast.185), channel_id=1, source_target_pairs={{0,2},{1,3},{2,0},{3,1},{4,6},{5,7},{6,4},{7,5},{8,10},{9,11},{10,... | collective-permute-start | bytes 786440 | tf_op jit(solution)/shard_map/ppermute | solution.py:44
  58.8 2.4 %collective-permute-start.12 = (bf16[8,4,1024]{2,0,1:T(8,128)(2,1)S(1)}, bf16[8,4,1024]{2,0,1:T(8,128)(2,1)S(1)}, u32[]{:S(2)}, u32[]{:S(2)}) collective-permute-start(bf16[8,4,1024]{2,0,1:T(8,128)(2,1)S(1)} %bitcast.191), channel_id=1, source_target_pairs={{0,3},{1,0},{2,1},{3,2},{4,7},{5,4},{6,5},{7,6},{8,11},{9,8},{10,9... | collective-permute-start | bytes 196616 | tf_op jit(solution)/shard_map/ppermute | solution.py:44
  62.9 3.1 %collective-permute-done.10 = bf16[8,4,1024]{2,0,1:T(8,128)(2,1)S(1)} collective-permute-done((bf16[8,4,1024]{2,0,1:T(8,128)(2,1)S(1)}, bf16[8,4,1024]{2,0,1:T(8,128)(2,1)S(1)}, u32[]{:S(2)}, u32[]{:S(2)}) %collective-permute-start.10) | collective-permute-done | bytes 65568 | tf_op jit(solution)/shard_map/ppermute | solution.py:44
  66.0 4.6 %collective-permute-start.5 = (bf16[128,1024]{1,0:T(8,128)(2,1)}, bf16[128,1024]{1,0:T(8,128)(2,1)S(1)}, u32[]{:S(2)}, u32[]{:S(2)}) collective-permute-start(bf16[128,1024]{1,0:T(8,128)(2,1)} %bitcast.13), channel_id=1, source_target_pairs={{0,3},{1,0},{2,1},{3,2},{4,7},{5,4},{6,5},{7,6},{8,11},{9,8},{10,9... | collective-permute-start | bytes 786440 | tf_op jit(solution)/shard_map/ppermute | solution.py:44
  73.1 35.2 %all-to-all-done.1 = bf16[32,32,3,512]{3,1,2,0:T(8,128)(2,1)} async-done(((bf16[32,32,3,512]{3,1,2,0:T(8,128)(2,1)}), bf16[32,32,3,512]{3,1,2,0:T(8,128)(2,1)}, u32[]{:S(2)}, u32[]{:S(2)}) %all-to-all-start.1) | async-done | bytes 3145760 | tf_op jit(solution)/shard_map/all_to_all | solution.py:103
  108.3 2.5 %convert_reduce_fusion = f32[2,32,3,512]{3,1,2,0:T(8,128)S(1)} fusion(bf16[16,2,32,3,512]{4,2,3,1,0:T(8,128)(2,1)} %bitcast.54), kind=kLoop, calls=%fused_computation.4 | loop fusion | flops 3047424 | bytes 3538944 | tf_op jit(solution)/shard_map/reduce_sum | solution.py:106
  113.1 3.5 %fusion.75 = (f32[2,16,4]{1,2,0:T(4,128)S(1)}, f32[2,16,4,1024]{3,1,2,0:T(8,128)S(1)}) fusion(bf16[2,128,4,8,256]{4,3,2,1,0:T(8,128)(2,1)} %bitcast.167, bf16[2,16,4,64]{3,1,2,0:T(8,128)(2,1)S(1)} %copy.110, pred[2,1024]{1,0:T(4,128)(4,1)S(1)} %iota_compare_fusion.1, bf16[2,16,4,192]{3,1,0,2:T(8,128)(2,1)S(1)} %bitcast.178), kind=kOutput, calls=%fused_computation.150 | convolution fusion | flops 67633024 | bytes 4786688 | tf_op jit(solution)/shard_map/gqhd,gjhd->gqhj/dot_general | solution.py:124
  116.7 2.2 %fusion.10 = f32[32,4,1,32]{3,2,1,0:T(1,128)S(1)} fusion(bf16[32,4,4,8,256]{4,3,2,1,0:T(8,128)(2,1)} %bitcast.199, bf16[32,4,256,1]{2,0,1,3:T(8,128)(2,1)S(1)} %get-tuple-element.26), kind=kOutput, calls=%fused_computation.18 | convolution fusion | flops 2097152 | bytes 2179072 | tf_op jit(solution)/shard_map/rhd,rthd->rht/dot_general | solution.py:132
  119.7 2.0 fusion.7
  121.7 6.5 %fusion.38 = bf16[1024,128]{1,0:T(8,128)(2,1)} fusion(bf16[1024,4096]{1,0:T(8,128)(2,1)} %all-gather.3.cloned.1.call-done, bf16[4096,128]{1,0:T(8,128)(2,1)S(1)} %copy-done, f32[128]{0:T(128)S(1)} %convert_element_type.101), kind=kOutput, calls=%fused_computation.47 | convolution fusion | flops 1075052544 | bytes 9699840 | tf_op jit(solution)/shard_map/dot_general | solution.py:177
  128.2 2.9 %fusion.22 = f32[2,16,4,256]{3,1,2,0:T(8,128)S(1)} fusion(bf16[2,128,4,8,256]{4,3,2,1,0:T(8,128)(2,1)} %bitcast.169, f32[2,16,4,1024]{3,1,2,0:T(8,128)S(1)} %get-tuple-element.33, f32[2,16,4]{1,2,0:T(4,128)S(1)} %copy.117), kind=kOutput, calls=%fused_computation.25 | convolution fusion | flops 67371008 | bytes 4850176 | tf_op jit(solution)/shard_map/gqhj,gjhd->gqhd/dot_general | solution.py:150
  132.3 3.9 %all-to-all-start.2 = ((bf16[32,2,512]{2,1,0:T(2,128)(2,1)}), bf16[32,2,512]{2,1,0:T(2,128)(2,1)S(1)}, u32[]{:S(2)}, u32[]{:S(2)}) async-start(bf16[32,2,512]{2,1,0:T(2,128)(2,1)} %reshape.374), calls=%async_computation.2 | async-start | bytes 131072 | tf_op jit(solution)/shard_map/all_to_all | solution.py:165
  138.9 4.8 %all-to-all-done.2 = bf16[32,2,512]{2,1,0:T(2,128)(2,1)S(1)} async-done(((bf16[32,2,512]{2,1,0:T(2,128)(2,1)}), bf16[32,2,512]{2,1,0:T(2,128)(2,1)S(1)}, u32[]{:S(2)}, u32[]{:S(2)}) %all-to-all-start.2) | async-done | bytes 65568 | tf_op jit(solution)/shard_map/all_to_all | solution.py:165
  144.3 3.5 %collective-permute-start.8 = (bf16[8,4,1024]{2,0,1:T(8,128)(2,1)S(1)}, bf16[8,4,1024]{2,0,1:T(8,128)(2,1)}, u32[]{:S(2)}, u32[]{:S(2)}) collective-permute-start(bf16[8,4,1024]{2,0,1:T(8,128)(2,1)S(1)} %all_to_all.37), channel_id=1, source_target_pairs={{0,2},{1,3},{2,0},{3,1},{4,6},{5,7},{6,4},{7,5},{8,10},{9,11},{10,... | collective-permute-start | bytes 196616 | tf_op jit(solution)/shard_map/ppermute | solution.py:55
  154.3 2.5 %fusion.76 = f32[1024,1024]{1,0:T(8,128)S(1)} fusion(bf16[1024,512]{1,0:T(8,128)(2,1)} %all-gather.5.cloned.1.call-done, bf16[512,1024]{1,0:T(8,128)(2,1)S(1)} %bitcast_select_fusion), kind=kOutput, calls=%fused_computation.151 | convolution fusion | flops 1073741824 | bytes 6291456 | tf_op jit(solution)/shard_map/dot_general | solution.py:186
  156.8 2.2 %fusion.6 = bf16[1024,1024]{1,0:T(8,128)(2,1)} fusion(f32[1024,1024]{1,0:T(8,128)S(1)} %fusion.76, bf16[4,8,4,1024]{3,1,2,0:T(8,128)(2,1)S(1)} %copy-done.3, bf16[4,8,4,1024]{3,1,2,0:T(8,128)(2,1)S(1)} %gather_fusion.2, pred[4]{0:T(512)(128)(4,1)S(1)} %compare_and_fusion), kind=kOutput, calls=%fused_computation.12 | convolution fusion | flops 270794752 | bytes 6815748 | tf_op jit(solution)/shard_map/dkr,dkf->rf/dot_general | solution.py:187
  159.0 6.2 %all-to-all-start.3 = ((bf16[32,32,1024]{2,1,0:T(8,128)(2,1)}), bf16[32,32,1024]{2,1,0:T(8,128)(2,1)S(1)}, u32[]{:S(2)}, u32[]{:S(2)}) async-start(bf16[32,32,1024]{2,1,0:T(8,128)(2,1)} %bitcast.172), calls=%async_computation.3 | async-start | bytes 4194304 | tf_op jit(solution)/shard_map/all_to_all | solution.py:189
  165.2 28.6 %all-to-all-done.3 = bf16[32,32,1024]{2,1,0:T(8,128)(2,1)S(1)} async-done(((bf16[32,32,1024]{2,1,0:T(8,128)(2,1)}), bf16[32,32,1024]{2,1,0:T(8,128)(2,1)S(1)}, u32[]{:S(2)}, u32[]{:S(2)}) %all-to-all-start.3) | async-done | bytes 2097184 | tf_op jit(solution)/shard_map/all_to_all | solution.py:189
  (151 shorter events, 33.6 us)
Async XLA Ops:
  6.5 115.1 %copy-start = (bf16[4096,128]{1,0:T(8,128)(2,1)S(1)}, bf16[4096,128]{1,0:T(8,128)(2,1)}, u32[]{:S(2)}) copy-start(bf16[4096,128]{1,0:T(8,128)(2,1)} %param.28) | copy-start | bytes 3145732
  6.5 11.4 %copy-start.8 = (bf16[4096]{0:T(1024)(128)(2,1)S(1)}, bf16[4096]{0:T(1024)(128)(2,1)}, u32[]{:S(2)}) copy-start(bf16[4096]{0:T(1024)(128)(2,1)} %param.18) | copy-start | bytes 24580
  6.5 11.4 %copy-start.7 = (bf16[4096]{0:T(1024)(128)(2,1)S(1)}, bf16[4096]{0:T(1024)(128)(2,1)}, u32[]{:S(2)}) copy-start(bf16[4096]{0:T(1024)(128)(2,1)} %param.19) | copy-start | bytes 24580
  6.5 115.1 %all-gather.3.cloned.1.call-start = ((), (), s32[]{:S(2)}) async-start(), calls=%async_computation.4 | async-start | bytes 8650752 | tf_op jit(solution)/shard_map/all_gather | solution.py:84
  6.5 7.1 %collective-permute-start = (bf16[32,1024]{1,0:T(8,128)(2,1)}, bf16[32,1024]{1,0:T(8,128)(2,1)S(1)}, u32[]{:S(2)}, u32[]{:S(2)}) collective-permute-start(bf16[32,1024]{1,0:T(8,128)(2,1)} %param.17), channel_id=1, source_target_pairs={{0,1},{1,2},{2,3},{3,0},{4,5},{5,6},{6,7},{7,4},{8,9},{9,10},{10,1... | collective-permute-start | bytes 196616 | tf_op jit(solution)/shard_map/ppermute | solution.py:55
  8.6 5.3 %collective-permute-start.1 = (bf16[32,1024]{1,0:T(8,128)(2,1)}, bf16[32,1024]{1,0:T(8,128)(2,1)S(1)}, u32[]{:S(2)}, u32[]{:S(2)}) collective-permute-start(bf16[32,1024]{1,0:T(8,128)(2,1)} %param.17), channel_id=1, source_target_pairs={{0,2},{1,3},{2,0},{3,1},{4,6},{5,7},{6,4},{7,5},{8,10},{9,11},{10,... | collective-permute-start | bytes 196616 | tf_op jit(solution)/shard_map/ppermute | solution.py:55
  11.1 3.8 %collective-permute-start.2 = (bf16[32,1024]{1,0:T(8,128)(2,1)}, bf16[32,1024]{1,0:T(8,128)(2,1)S(1)}, u32[]{:S(2)}, u32[]{:S(2)}) collective-permute-start(bf16[32,1024]{1,0:T(8,128)(2,1)} %param.17), channel_id=1, source_target_pairs={{0,3},{1,0},{2,1},{3,2},{4,7},{5,4},{6,5},{7,6},{8,11},{9,8},{10,9... | collective-permute-start | bytes 196616 | tf_op jit(solution)/shard_map/ppermute | solution.py:55
  17.0 12.8 %copy-start.2 = (bf16[128,3,1024]{2,0,1:T(8,128)(2,1)S(1)}, bf16[128,3,1024]{2,0,1:T(8,128)(2,1)}, u32[]{:S(2)}) copy-start(bf16[128,3,1024]{2,0,1:T(8,128)(2,1)} %param.20) | copy-start | bytes 2359300
  19.8 23.8 %all-to-all-start = ((bf16[32,32,256]{2,0,1:T(8,128)(2,1)}), bf16[32,32,256]{2,0,1:T(8,128)(2,1)S(1)}, u32[]{:S(2)}, u32[]{:S(2)}) async-start(bf16[32,32,256]{2,0,1:T(8,128)(2,1)} %bitcast.16), calls=%async_computation | async-start | bytes 1048576 | tf_op jit(solution)/shard_map/all_to_all | solution.py:87
  30.0 1.8 collective-permute-start.6
  46.8 61.5 %all-to-all-start.1 = ((bf16[32,32,3,512]{3,1,2,0:T(8,128)(2,1)}), bf16[32,32,3,512]{3,1,2,0:T(8,128)(2,1)}, u32[]{:S(2)}, u32[]{:S(2)}) async-start(bf16[32,32,3,512]{3,1,2,0:T(8,128)(2,1)} %copy.105), calls=%async_computation.1 | async-start | bytes 6291456 | tf_op jit(solution)/shard_map/all_to_all | solution.py:103
  51.7 102.6 %all-gather.5.cloned.1.call-start = ((), (), s32[]{:S(2)}) async-start(), calls=%async_computation.5 | async-start | bytes 1310720 | tf_op jit(solution)/shard_map/all_gather | solution.py:185
  53.5 82.8 %collective-permute-start.3 = (bf16[128,1024]{1,0:T(8,128)(2,1)}, bf16[128,1024]{1,0:T(8,128)(2,1)}, u32[]{:S(2)}, u32[]{:S(2)}) collective-permute-start(bf16[128,1024]{1,0:T(8,128)(2,1)} %bitcast.9), channel_id=1, source_target_pairs={{0,1},{1,2},{2,3},{3,0},{4,5},{5,6},{6,7},{7,4},{8,9},{9,10},{10,1... | collective-permute-start | bytes 786440 | tf_op jit(solution)/shard_map/ppermute | solution.py:44
  53.6 82.6 %collective-permute-start.4 = (bf16[128,1024]{1,0:T(8,128)(2,1)S(1)}, bf16[128,1024]{1,0:T(8,128)(2,1)}, u32[]{:S(2)}, u32[]{:S(2)}) collective-permute-start(bf16[128,1024]{1,0:T(8,128)(2,1)S(1)} %bitcast.185), channel_id=1, source_target_pairs={{0,2},{1,3},{2,0},{3,1},{4,6},{5,7},{6,4},{7,5},{8,10},{9,11},{10,... | collective-permute-start | bytes 786440 | tf_op jit(solution)/shard_map/ppermute | solution.py:44
  58.2 7.8 %collective-permute-start.10 = (bf16[8,4,1024]{2,0,1:T(8,128)(2,1)S(1)}, bf16[8,4,1024]{2,0,1:T(8,128)(2,1)S(1)}, u32[]{:S(2)}, u32[]{:S(2)}) collective-permute-start(bf16[8,4,1024]{2,0,1:T(8,128)(2,1)S(1)} %bitcast.190), channel_id=1, source_target_pairs={{0,1},{1,2},{2,3},{3,0},{4,5},{5,6},{6,7},{7,4},{8,9},{9,10},{10,1... | collective-permute-start | bytes 196616 | tf_op jit(solution)/shard_map/ppermute | solution.py:44
  58.4 13.4 %collective-permute-start.11 = (bf16[8,4,1024]{2,0,1:T(8,128)(2,1)S(1)}, bf16[8,4,1024]{2,0,1:T(8,128)(2,1)S(1)}, u32[]{:S(2)}, u32[]{:S(2)}) collective-permute-start(bf16[8,4,1024]{2,0,1:T(8,128)(2,1)S(1)} %bitcast.189), channel_id=1, source_target_pairs={{0,2},{1,3},{2,0},{3,1},{4,6},{5,7},{6,4},{7,5},{8,10},{9,11},{10,... | collective-permute-start | bytes 196616 | tf_op jit(solution)/shard_map/ppermute | solution.py:44
  58.8 13.0 %collective-permute-start.12 = (bf16[8,4,1024]{2,0,1:T(8,128)(2,1)S(1)}, bf16[8,4,1024]{2,0,1:T(8,128)(2,1)S(1)}, u32[]{:S(2)}, u32[]{:S(2)}) collective-permute-start(bf16[8,4,1024]{2,0,1:T(8,128)(2,1)S(1)} %bitcast.191), channel_id=1, source_target_pairs={{0,3},{1,0},{2,1},{3,2},{4,7},{5,4},{6,5},{7,6},{8,11},{9,8},{10,9... | collective-permute-start | bytes 196616 | tf_op jit(solution)/shard_map/ppermute | solution.py:44
  66.0 70.2 %collective-permute-start.5 = (bf16[128,1024]{1,0:T(8,128)(2,1)}, bf16[128,1024]{1,0:T(8,128)(2,1)S(1)}, u32[]{:S(2)}, u32[]{:S(2)}) collective-permute-start(bf16[128,1024]{1,0:T(8,128)(2,1)} %bitcast.13), channel_id=1, source_target_pairs={{0,3},{1,0},{2,1},{3,2},{4,7},{5,4},{6,5},{7,6},{8,11},{9,8},{10,9... | collective-permute-start | bytes 786440 | tf_op jit(solution)/shard_map/ppermute | solution.py:44
  132.3 11.3 %all-to-all-start.2 = ((bf16[32,2,512]{2,1,0:T(2,128)(2,1)}), bf16[32,2,512]{2,1,0:T(2,128)(2,1)S(1)}, u32[]{:S(2)}, u32[]{:S(2)}) async-start(bf16[32,2,512]{2,1,0:T(2,128)(2,1)} %reshape.374), calls=%async_computation.2 | async-start | bytes 131072 | tf_op jit(solution)/shard_map/all_to_all | solution.py:165
  144.2 6.1 %collective-permute-start.7 = (bf16[8,4,1024]{2,0,1:T(8,128)(2,1)S(1)}, bf16[8,4,1024]{2,0,1:T(8,128)(2,1)S(1)}, u32[]{:S(2)}, u32[]{:S(2)}) collective-permute-start(bf16[8,4,1024]{2,0,1:T(8,128)(2,1)S(1)} %all_to_all.37), channel_id=1, source_target_pairs={{0,1},{1,2},{2,3},{3,0},{4,5},{5,6},{6,7},{7,4},{8,9},{9,10},{10,1... | collective-permute-start | bytes 196616 | tf_op jit(solution)/shard_map/ppermute | solution.py:55
  144.3 7.9 %collective-permute-start.8 = (bf16[8,4,1024]{2,0,1:T(8,128)(2,1)S(1)}, bf16[8,4,1024]{2,0,1:T(8,128)(2,1)}, u32[]{:S(2)}, u32[]{:S(2)}) collective-permute-start(bf16[8,4,1024]{2,0,1:T(8,128)(2,1)S(1)} %all_to_all.37), channel_id=1, source_target_pairs={{0,2},{1,3},{2,0},{3,1},{4,6},{5,7},{6,4},{7,5},{8,10},{9,11},{10,... | collective-permute-start | bytes 196616 | tf_op jit(solution)/shard_map/ppermute | solution.py:55
  147.9 4.9 %collective-permute-start.9 = (bf16[8,4,1024]{2,0,1:T(8,128)(2,1)S(1)}, bf16[8,4,1024]{2,0,1:T(8,128)(2,1)}, u32[]{:S(2)}, u32[]{:S(2)}) collective-permute-start(bf16[8,4,1024]{2,0,1:T(8,128)(2,1)S(1)} %all_to_all.37), channel_id=1, source_target_pairs={{0,3},{1,0},{2,1},{3,2},{4,7},{5,4},{6,5},{7,6},{8,11},{9,8},{10,9... | collective-permute-start | bytes 196616 | tf_op jit(solution)/shard_map/ppermute | solution.py:55
  159.0 35.1 %copy-start.5 = (bf16[32,1024]{1,0:T(8,128)(2,1)S(1)}, bf16[32,1024]{1,0:T(8,128)(2,1)}, u32[]{:S(2)}) copy-start(bf16[32,1024]{1,0:T(8,128)(2,1)} %param.17) | copy-start | bytes 196612
  159.0 34.8 %all-to-all-start.3 = ((bf16[32,32,1024]{2,1,0:T(8,128)(2,1)}), bf16[32,32,1024]{2,1,0:T(8,128)(2,1)S(1)}, u32[]{:S(2)}, u32[]{:S(2)}) async-start(bf16[32,32,1024]{2,1,0:T(8,128)(2,1)} %bitcast.172), calls=%async_computation.3 | async-start | bytes 4194304 | tf_op jit(solution)/shard_map/all_to_all | solution.py:189
  (8 other events, 49.7 us)
Sparse Core Ops, SparseCore 0:
  18.1 89.8 all-gather.2
  128.3 21.6 all-gather.4

commit v6 on v5

--- a/solution.py
+++ b/solution.py
@@ -186,14 +186,18 @@
     mlp_part = jnp.dot(hidden, down_blocks, preferred_element_type=jnp.float32)
     attn_part = jnp.einsum("dkr,dkf->rf", slices, out_blocks, preferred_element_type=jnp.float32)
     combined = mlp_part + attn_part
+    half_width = width_here // 2
+    mine = lax.dynamic_slice_in_dim(combined, parity * half_width, half_width, axis=1)
+    theirs = lax.dynamic_slice_in_dim(combined, (1 - parity) * half_width, half_width, axis=1)
+    got = lax.ppermute(
+        theirs.astype(jnp.bfloat16), "grp", [(i, i ^ 1) for i in range(grp_count)]
+    )
+    pair_sum = (mine + got.astype(jnp.float32)).astype(jnp.bfloat16)
     pieces = lax.all_to_all(
-        combined.astype(jnp.bfloat16).reshape(grp_count, local_rows, width_here),
-        "grp",
-        0,
-        0,
-        tiled=True,
-    )
+        pair_sum.reshape(grp_count, local_rows, half_width), "grp", 0, 0, tiled=True
+    ).reshape(grp_count // 2, 2, local_rows, half_width)
     summed = jnp.sum(pieces.astype(jnp.float32), axis=0)
+    summed = jnp.transpose(summed, (1, 0, 2)).reshape(local_rows, width_here)
     total = activations.astype(jnp.float32) + b_down.astype(jnp.float32)[None, :] + summed
     return total.astype(jnp.bfloat16)
 

time: 203 us -> 194 us (0.956)
  waiting for transfers between devices: 91.9 us -> 84.7 us
  starting transfers between devices: 45.9 us -> 41.8 us
  other arithmetic: 12 us -> 15.7 us
    all_to_all x1, waiting for transfers between devices: 28.6 us -> 17 us  [local(): lax.all_to_all(pair_sum.reshape(grp_count, local_rows, half_width), 'grp'...]
    all_to_all x1, waiting for transfers between devices: 35.2 us -> 39.9 us  [local(): lax.all_to_all(term.reshape(grp_count, local_rows, 3, half), 'grp', 0, 0,...]
    ppermute x6, waiting for transfers between devices: 4.28 us -> 0.02 us  [head_exchange(): lax.ppermute(piece, 'head', [(i, (i + shift) % count) for i in range(coun...]
    ppermute x6, starting transfers between devices: 11.2 us -> 6.93 us  [head_exchange(): lax.ppermute(piece, 'head', [(i, (i + shift) % count) for i in range(coun...]
    ppermute x0 -> x1, waiting for transfers between devices: none -> 2.29 us  [local(): lax.ppermute(theirs.astype(jnp.bfloat16), 'grp', [(i, i ^ 1) for i in ran...]
    ppermute x6, starting transfers between devices: 9.33 us -> 7.16 us  [head_gather(): lax.ppermute(piece, 'head', [(i, (i + shift) % count) for i in range(coun...]
    unnamed x36 -> x34, local copies, waits for them, and re-layouts: 2.98 us -> 4.14 us
  transfers between devices with their start and end apart: 19 -> 20, of which waited for: 12 -> 10; matrix products, arithmetic and copies ran while one was open for 20% -> 22% of each run, Pallas kernels for 0% -> 0%
where the time goes in v6:
time: 194 us; the launch traced here: 193 us
  waiting for transfers between devices  84.7 us (44%)
  starting transfers between devices  41.8 us (22%)
  matrix products  21.4 us (11%)
  other arithmetic  15.7 us (8%)
  local copies, waits for them, and re-layouts  14.8 us (8%)
  between operations  14.2 us (7%)
    all_to_all x1, waiting for transfers between devices, local(): lax.all_to_all(term.reshape(grp_count, local_rows, 3, half), 'grp', 0, 0,...  39.9 us
    all_to_all x1, waiting for transfers between devices, local(): lax.all_to_all(pair_sum.reshape(grp_count, local_rows, half_width), 'grp'...  17 us
    all_to_all x1, waiting for transfers between devices, local(): lax.all_to_all(jnp.repeat(pair_rows, 2, axis=1), 'grp', split_axis=1, con...  12.2 us
    all_to_all x1, starting transfers between devices, local(): lax.all_to_all(jnp.repeat(pair_rows, 2, axis=1), 'grp', split_axis=1, con...  10.6 us
    ppermute x6, starting transfers between devices, head_gather(): lax.ppermute(piece, 'head', [(i, (i + shift) % count) for i in range(coun...  7.16 us
    ppermute x6, starting transfers between devices, head_exchange(): lax.ppermute(piece, 'head', [(i, (i + shift) % count) for i in range(coun...  6.93 us
    all_to_all x1, starting transfers between devices, local(): lax.all_to_all(pair_sum.reshape(grp_count, local_rows, half_width), 'grp'...  6.49 us
    dot_general x1, matrix products, local(): jnp.dot(gathered, w_in, preferred_element_type=jnp.float32)  6.46 us
  transfers between devices with their start and end apart: 20, of which 10 were waited for; matrix products, arithmetic and copies ran while one was open for 22% of the time, Pallas kernels for 0%

profile of v6, /device:TPU:1, one launch (start us, length us, event | category | flops | bytes accessed | tf_op | source)
XLA Modules:
  0.0 192.7 jit_solution(4797078603968507238)
XLA Ops:
  6.5 2.1 %collective-permute-start = (bf16[32,1024]{1,0:T(8,128)(2,1)}, bf16[32,1024]{1,0:T(8,128)(2,1)S(1)}, u32[]{:S(2)}, u32[]{:S(2)}) collective-permute-start(bf16[32,1024]{1,0:T(8,128)(2,1)} %param.17), channel_id=1, source_target_pairs={{0,1},{1,2},{2,3},{3,0},{4,5},{5,6},{6,7},{7,4},{8,9},{9,10},{10,1... | collective-permute-start | bytes 196616 | tf_op jit(solution)/shard_map/ppermute | solution.py:55
  10.0 1.6 collective-permute-start.1
  13.1 1.7 collective-permute-done.1
  19.8 10.6 %all-to-all-start = ((bf16[32,32,256]{2,0,1:T(8,128)(2,1)}), bf16[32,32,256]{2,0,1:T(8,128)(2,1)S(1)}, u32[]{:S(2)}, u32[]{:S(2)}) async-start(bf16[32,32,256]{2,0,1:T(8,128)(2,1)} %bitcast.16), calls=%async_computation | async-start | bytes 1048576 | tf_op jit(solution)/shard_map/all_to_all | solution.py:87
  30.8 1.5 collective-permute-done.6
  32.3 12.2 %all-to-all-done = bf16[32,32,256]{2,0,1:T(8,128)(2,1)S(1)} async-done(((bf16[32,32,256]{2,0,1:T(8,128)(2,1)}), bf16[32,32,256]{2,0,1:T(8,128)(2,1)S(1)}, u32[]{:S(2)}, u32[]{:S(2)}) %all-to-all-start) | async-done | bytes 524320 | tf_op jit(solution)/shard_map/all_to_all | solution.py:87
  45.5 2.2 %copy.137 = bf16[32,32,3,512]{3,1,2,0:T(8,128)(2,1)} copy(bf16[32,32,3,512]{3,1,0,2:T(8,128)(2,1)S(1)} %bitcast.174) | data formatting | bytes 6291456 | tf_op jit(solution)/shard_map/reshape | solution.py:104
  47.6 4.9 %all-to-all-start.1 = ((bf16[32,32,3,512]{3,1,2,0:T(8,128)(2,1)}), bf16[32,32,3,512]{3,1,2,0:T(8,128)(2,1)}, u32[]{:S(2)}, u32[]{:S(2)}) async-start(bf16[32,32,3,512]{3,1,2,0:T(8,128)(2,1)} %copy.137), calls=%async_computation.1 | async-start | bytes 6291456 | tf_op jit(solution)/shard_map/all_to_all | solution.py:103
  59.2 1.6 collective-permute-start.3
  66.1 1.7 collective-permute-start.5
  69.3 39.9 %all-to-all-done.1 = bf16[32,32,3,512]{3,1,2,0:T(8,128)(2,1)} async-done(((bf16[32,32,3,512]{3,1,2,0:T(8,128)(2,1)}), bf16[32,32,3,512]{3,1,2,0:T(8,128)(2,1)}, u32[]{:S(2)}, u32[]{:S(2)}) %all-to-all-start.1) | async-done | bytes 3145760 | tf_op jit(solution)/shard_map/all_to_all | solution.py:103
  109.3 2.5 %convert_reduce_fusion = f32[2,32,3,512]{3,1,2,0:T(8,128)S(1)} fusion(bf16[16,2,32,3,512]{4,2,3,1,0:T(8,128)(2,1)} %bitcast.56), kind=kLoop, calls=%fused_computation.4 | loop fusion | flops 3047424 | bytes 3538944 | tf_op jit(solution)/shard_map/reduce_sum | solution.py:106
  114.1 3.5 %fusion.74 = (f32[2,16,4]{1,2,0:T(4,128)S(1)}, f32[2,16,4,1024]{3,1,2,0:T(8,128)S(1)}) fusion(bf16[2,128,4,8,256]{4,3,2,1,0:T(8,128)(2,1)} %bitcast.170, bf16[2,16,4,64]{3,1,2,0:T(8,128)(2,1)S(1)} %copy.142, pred[2,1024]{1,0:T(4,128)(4,1)S(1)} %iota_compare_fusion.1, bf16[2,16,4,192]{3,1,0,2:T(8,128)(2,1)S(1)} %bitcast.181), kind=kOutput, calls=%fused_computation.151 | convolution fusion | flops 67633024 | bytes 4786688 | tf_op jit(solution)/shard_map/gqhd,gjhd->gqhj/dot_general | solution.py:124
  117.6 2.2 %fusion.9 = f32[32,4,1,32]{3,2,1,0:T(1,128)S(1)} fusion(bf16[32,4,4,8,256]{4,3,2,1,0:T(8,128)(2,1)} %bitcast.200, bf16[32,4,256,1]{2,0,1,3:T(8,128)(2,1)S(1)} %get-tuple-element.26), kind=kOutput, calls=%fused_computation.16 | convolution fusion | flops 2097152 | bytes 2179072 | tf_op jit(solution)/shard_map/rhd,rthd->rht/dot_general | solution.py:132
  120.6 2.0 %fusion.6 = f32[32,4,1,256]{3,2,1,0:T(1,128)S(1)} fusion(bf16[32,4,4,8,256]{4,3,2,1,0:T(8,128)(2,1)} %bitcast.201, bf16[32,4,32,1]{2,0,1,3:T(8,128)(2,1)S(1)} %get-tuple-element.29), kind=kOutput, calls=%fused_computation.13 | convolution fusion | flops 2097152 | bytes 2236416 | tf_op jit(solution)/shard_map/rht,rthd->rhd/dot_general | solution.py:157
  122.6 6.5 %fusion.37 = bf16[1024,128]{1,0:T(8,128)(2,1)} fusion(bf16[1024,4096]{1,0:T(8,128)(2,1)} %all-gather.3.cloned.1.call-done, bf16[4096,128]{1,0:T(8,128)(2,1)S(1)} %copy-done, f32[128]{0:T(128)S(1)} %copy-done.11), kind=kOutput, calls=%fused_computation.48 | convolution fusion | flops 1075052544 | bytes 9699840 | tf_op jit(solution)/shard_map/dot_general | solution.py:177
  129.1 2.9 %fusion.21 = f32[2,16,4,256]{3,1,2,0:T(8,128)S(1)} fusion(bf16[2,128,4,8,256]{4,3,2,1,0:T(8,128)(2,1)} %bitcast.172, f32[2,16,4,1024]{3,1,2,0:T(8,128)S(1)} %get-tuple-element.33, f32[2,16,4]{1,2,0:T(4,128)S(1)} %copy.149), kind=kOutput, calls=%fused_computation.26 | convolution fusion | flops 67371008 | bytes 4850176 | tf_op jit(solution)/shard_map/gqhj,gjhd->gqhd/dot_general | solution.py:150
  133.3 3.9 %all-to-all-start.2 = ((bf16[32,2,512]{2,1,0:T(2,128)(2,1)}), bf16[32,2,512]{2,1,0:T(2,128)(2,1)S(1)}, u32[]{:S(2)}, u32[]{:S(2)}) async-start(bf16[32,2,512]{2,1,0:T(2,128)(2,1)} %reshape.382), calls=%async_computation.2 | async-start | bytes 131072 | tf_op jit(solution)/shard_map/all_to_all | solution.py:165
  139.1 5.5 %all-to-all-done.2 = bf16[32,2,512]{2,1,0:T(2,128)(2,1)S(1)} async-done(((bf16[32,2,512]{2,1,0:T(2,128)(2,1)}), bf16[32,2,512]{2,1,0:T(2,128)(2,1)S(1)}, u32[]{:S(2)}, u32[]{:S(2)}) %all-to-all-start.2) | async-done | bytes 65568 | tf_op jit(solution)/shard_map/all_to_all | solution.py:165
  147.8 2.0 %collective-permute-done.9 = bf16[8,4,1024]{2,0,1:T(8,128)(2,1)S(1)} collective-permute-done((bf16[8,4,1024]{2,0,1:T(8,128)(2,1)S(1)}, bf16[8,4,1024]{2,0,1:T(8,128)(2,1)S(1)}, u32[]{:S(2)}, u32[]{:S(2)}) %collective-permute-start.9) | collective-permute-done | bytes 65568 | tf_op jit(solution)/shard_map/ppermute | solution.py:55
  152.8 2.5 %fusion.75 = f32[1024,1024]{1,0:T(8,128)S(1)} fusion(bf16[1024,512]{1,0:T(8,128)(2,1)} %all-gather.5.cloned.1.call-done, bf16[512,1024]{1,0:T(8,128)(2,1)S(1)} %bitcast_select_fusion), kind=kOutput, calls=%fused_computation.152 | convolution fusion | flops 1073741824 | bytes 6291456 | tf_op jit(solution)/shard_map/dot_general | solution.py:186
  157.8 2.3 %collective-permute-done.13 = bf16[1024,512]{1,0:T(8,128)(2,1)S(1)} collective-permute-done((bf16[1024,512]{1,0:T(8,128)(2,1)S(1)}, bf16[1024,512]{1,0:T(8,128)(2,1)S(1)}, u32[]{:S(2)}, u32[]{:S(2)}) %collective-permute-start.13) | collective-permute-done | bytes 1048608 | tf_op jit(solution)/shard_map/ppermute | solution.py:192
  161.4 6.5 %all-to-all-start.3 = ((bf16[32,32,512]{2,1,0:T(8,128)(2,1)}), bf16[32,32,512]{2,1,0:T(8,128)(2,1)S(1)}, u32[]{:S(2)}, u32[]{:S(2)}) async-start(bf16[32,32,512]{2,1,0:T(8,128)(2,1)} %bitcast.50), calls=%async_computation.3 | async-start | bytes 2097152 | tf_op jit(solution)/shard_map/all_to_all | solution.py:196
  168.0 17.0 %all-to-all-done.3 = bf16[32,32,512]{2,1,0:T(8,128)(2,1)S(1)} async-done(((bf16[32,32,512]{2,1,0:T(8,128)(2,1)}), bf16[32,32,512]{2,1,0:T(8,128)(2,1)S(1)}, u32[]{:S(2)}, u32[]{:S(2)}) %all-to-all-start.3) | async-done | bytes 1048608 | tf_op jit(solution)/shard_map/all_to_all | solution.py:196
  (154 shorter events, 39.0 us)
Async XLA Ops:
  6.5 116.1 %copy-start = (bf16[4096,128]{1,0:T(8,128)(2,1)S(1)}, bf16[4096,128]{1,0:T(8,128)(2,1)}, u32[]{:S(2)}) copy-start(bf16[4096,128]{1,0:T(8,128)(2,1)} %param.28) | copy-start | bytes 3145732
  6.5 116.1 %all-gather.3.cloned.1.call-start = ((), (), s32[]{:S(2)}) async-start(), calls=%async_computation.4 | async-start | bytes 8650752 | tf_op jit(solution)/shard_map/all_gather | solution.py:84
  6.5 6.5 %collective-permute-start = (bf16[32,1024]{1,0:T(8,128)(2,1)}, bf16[32,1024]{1,0:T(8,128)(2,1)S(1)}, u32[]{:S(2)}, u32[]{:S(2)}) collective-permute-start(bf16[32,1024]{1,0:T(8,128)(2,1)} %param.17), channel_id=1, source_target_pairs={{0,1},{1,2},{2,3},{3,0},{4,5},{5,6},{6,7},{7,4},{8,9},{9,10},{10,1... | collective-permute-start | bytes 196616 | tf_op jit(solution)/shard_map/ppermute | solution.py:55
  8.6 4.5 %collective-permute-start.2 = (bf16[32,1024]{1,0:T(8,128)(2,1)}, bf16[32,1024]{1,0:T(8,128)(2,1)S(1)}, u32[]{:S(2)}, u32[]{:S(2)}) collective-permute-start(bf16[32,1024]{1,0:T(8,128)(2,1)} %param.17), channel_id=1, source_target_pairs={{0,3},{1,0},{2,1},{3,2},{4,7},{5,4},{6,5},{7,6},{8,11},{9,8},{10,9... | collective-permute-start | bytes 196616 | tf_op jit(solution)/shard_map/ppermute | solution.py:55
  10.0 4.8 %collective-permute-start.1 = (bf16[32,1024]{1,0:T(8,128)(2,1)}, bf16[32,1024]{1,0:T(8,128)(2,1)S(1)}, u32[]{:S(2)}, u32[]{:S(2)}) collective-permute-start(bf16[32,1024]{1,0:T(8,128)(2,1)} %param.17), channel_id=1, source_target_pairs={{0,2},{1,3},{2,0},{3,1},{4,6},{5,7},{6,4},{7,5},{8,10},{9,11},{10,... | collective-permute-start | bytes 196616 | tf_op jit(solution)/shard_map/ppermute | solution.py:55
  17.0 13.4 %copy-start.3 = (bf16[128,3,1024]{2,0,1:T(8,128)(2,1)S(1)}, bf16[128,3,1024]{2,0,1:T(8,128)(2,1)}, u32[]{:S(2)}) copy-start(bf16[128,3,1024]{2,0,1:T(8,128)(2,1)} %param.20) | copy-start | bytes 2359300
  19.8 24.7 %all-to-all-start = ((bf16[32,32,256]{2,0,1:T(8,128)(2,1)}), bf16[32,32,256]{2,0,1:T(8,128)(2,1)S(1)}, u32[]{:S(2)}, u32[]{:S(2)}) async-start(bf16[32,32,256]{2,0,1:T(8,128)(2,1)} %bitcast.16), calls=%async_computation | async-start | bytes 1048576 | tf_op jit(solution)/shard_map/all_to_all | solution.py:87
  30.5 1.8 collective-permute-start.6
  47.6 61.6 %all-to-all-start.1 = ((bf16[32,32,3,512]{3,1,2,0:T(8,128)(2,1)}), bf16[32,32,3,512]{3,1,2,0:T(8,128)(2,1)}, u32[]{:S(2)}, u32[]{:S(2)}) async-start(bf16[32,32,3,512]{3,1,2,0:T(8,128)(2,1)} %copy.137), calls=%async_computation.1 | async-start | bytes 6291456 | tf_op jit(solution)/shard_map/all_to_all | solution.py:103
  52.6 100.2 %all-gather.5.cloned.1.call-start = ((), (), s32[]{:S(2)}) async-start(), calls=%async_computation.5 | async-start | bytes 1310720 | tf_op jit(solution)/shard_map/all_gather | solution.py:185
  54.3 11.8 %collective-permute-start.12 = (bf16[8,4,1024]{2,0,1:T(8,128)(2,1)}, bf16[8,4,1024]{2,0,1:T(8,128)(2,1)}, u32[]{:S(2)}, u32[]{:S(2)}) collective-permute-start(bf16[8,4,1024]{2,0,1:T(8,128)(2,1)} %bitcast.166), channel_id=1, source_target_pairs={{0,3},{1,0},{2,1},{3,2},{4,7},{5,4},{6,5},{7,6},{8,11},{9,8},{10,9... | collective-permute-start | bytes 196616 | tf_op jit(solution)/shard_map/ppermute | solution.py:44
  55.9 12.0 %collective-permute-start.10 = (bf16[8,4,1024]{2,0,1:T(8,128)(2,1)}, bf16[8,4,1024]{2,0,1:T(8,128)(2,1)}, u32[]{:S(2)}, u32[]{:S(2)}) collective-permute-start(bf16[8,4,1024]{2,0,1:T(8,128)(2,1)} %bitcast.168), channel_id=1, source_target_pairs={{0,1},{1,2},{2,3},{3,0},{4,5},{5,6},{6,7},{7,4},{8,9},{9,10},{10,1... | collective-permute-start | bytes 196616 | tf_op jit(solution)/shard_map/ppermute | solution.py:44
  57.2 10.7 %collective-permute-start.11 = (bf16[8,4,1024]{2,0,1:T(8,128)(2,1)}, bf16[8,4,1024]{2,0,1:T(8,128)(2,1)}, u32[]{:S(2)}, u32[]{:S(2)}) collective-permute-start(bf16[8,4,1024]{2,0,1:T(8,128)(2,1)} %bitcast.167), channel_id=1, source_target_pairs={{0,2},{1,3},{2,0},{3,1},{4,6},{5,7},{6,4},{7,5},{8,10},{9,11},{10,... | collective-permute-start | bytes 196616 | tf_op jit(solution)/shard_map/ppermute | solution.py:44
  59.2 78.0 %collective-permute-start.3 = (bf16[128,1024]{1,0:T(8,128)(2,1)S(1)}, bf16[128,1024]{1,0:T(8,128)(2,1)}, u32[]{:S(2)}, u32[]{:S(2)}) collective-permute-start(bf16[128,1024]{1,0:T(8,128)(2,1)S(1)} %bitcast.190), channel_id=1, source_target_pairs={{0,1},{1,2},{2,3},{3,0},{4,5},{5,6},{6,7},{7,4},{8,9},{9,10},{10,1... | collective-permute-start | bytes 786440 | tf_op jit(solution)/shard_map/ppermute | solution.py:44
  60.9 76.3 %collective-permute-start.4 = (bf16[128,1024]{1,0:T(8,128)(2,1)S(1)}, bf16[128,1024]{1,0:T(8,128)(2,1)}, u32[]{:S(2)}, u32[]{:S(2)}) collective-permute-start(bf16[128,1024]{1,0:T(8,128)(2,1)S(1)} %bitcast.191), channel_id=1, source_target_pairs={{0,2},{1,3},{2,0},{3,1},{4,6},{5,7},{6,4},{7,5},{8,10},{9,11},{10,... | collective-permute-start | bytes 786440 | tf_op jit(solution)/shard_map/ppermute | solution.py:44
  66.1 71.1 %collective-permute-start.5 = (bf16[128,1024]{1,0:T(8,128)(2,1)}, bf16[128,1024]{1,0:T(8,128)(2,1)}, u32[]{:S(2)}, u32[]{:S(2)}) collective-permute-start(bf16[128,1024]{1,0:T(8,128)(2,1)} %bitcast.13), channel_id=1, source_target_pairs={{0,3},{1,0},{2,1},{3,2},{4,7},{5,4},{6,5},{7,6},{8,11},{9,8},{10,9... | collective-permute-start | bytes 786440 | tf_op jit(solution)/shard_map/ppermute | solution.py:44
  133.3 11.3 %all-to-all-start.2 = ((bf16[32,2,512]{2,1,0:T(2,128)(2,1)}), bf16[32,2,512]{2,1,0:T(2,128)(2,1)S(1)}, u32[]{:S(2)}, u32[]{:S(2)}) async-start(bf16[32,2,512]{2,1,0:T(2,128)(2,1)} %reshape.382), calls=%async_computation.2 | async-start | bytes 131072 | tf_op jit(solution)/shard_map/all_to_all | solution.py:165
  145.2 4.6 %collective-permute-start.9 = (bf16[8,4,1024]{2,0,1:T(8,128)(2,1)S(1)}, bf16[8,4,1024]{2,0,1:T(8,128)(2,1)S(1)}, u32[]{:S(2)}, u32[]{:S(2)}) collective-permute-start(bf16[8,4,1024]{2,0,1:T(8,128)(2,1)S(1)} %all_to_all.37), channel_id=1, source_target_pairs={{0,3},{1,0},{2,1},{3,2},{4,7},{5,4},{6,5},{7,6},{8,11},{9,8},{10,9... | collective-permute-start | bytes 196616 | tf_op jit(solution)/shard_map/ppermute | solution.py:55
  146.1 4.7 %collective-permute-start.8 = (bf16[8,4,1024]{2,0,1:T(8,128)(2,1)S(1)}, bf16[8,4,1024]{2,0,1:T(8,128)(2,1)S(1)}, u32[]{:S(2)}, u32[]{:S(2)}) collective-permute-start(bf16[8,4,1024]{2,0,1:T(8,128)(2,1)S(1)} %all_to_all.37), channel_id=1, source_target_pairs={{0,2},{1,3},{2,0},{3,1},{4,6},{5,7},{6,4},{7,5},{8,10},{9,11},{10,... | collective-permute-start | bytes 196616 | tf_op jit(solution)/shard_map/ppermute | solution.py:55
  146.7 5.5 %collective-permute-start.7 = (bf16[8,4,1024]{2,0,1:T(8,128)(2,1)S(1)}, bf16[8,4,1024]{2,0,1:T(8,128)(2,1)S(1)}, u32[]{:S(2)}, u32[]{:S(2)}) collective-permute-start(bf16[8,4,1024]{2,0,1:T(8,128)(2,1)S(1)} %all_to_all.37), channel_id=1, source_target_pairs={{0,1},{1,2},{2,3},{3,0},{4,5},{5,6},{6,7},{7,4},{8,9},{9,10},{10,1... | collective-permute-start | bytes 196616 | tf_op jit(solution)/shard_map/ppermute | solution.py:55
  156.1 29.7 %copy-start.1 = (bf16[4096,128]{1,0:T(8,128)(2,1)S(1)}, bf16[4096,128]{1,0:T(8,128)(2,1)}, u32[]{:S(2)}) copy-start(bf16[4096,128]{1,0:T(8,128)(2,1)} %param.28) | copy-start | bytes 3145732
  156.3 28.8 %copy-start.5 = (bf16[32,1024]{1,0:T(8,128)(2,1)S(1)}, bf16[32,1024]{1,0:T(8,128)(2,1)}, u32[]{:S(2)}) copy-start(bf16[32,1024]{1,0:T(8,128)(2,1)} %param.17) | copy-start | bytes 196612
  156.3 3.7 %collective-permute-start.13 = (bf16[1024,512]{1,0:T(8,128)(2,1)S(1)}, bf16[1024,512]{1,0:T(8,128)(2,1)S(1)}, u32[]{:S(2)}, u32[]{:S(2)}) collective-permute-start(bf16[1024,512]{1,0:T(8,128)(2,1)S(1)} %dynamic-slice_convert_fusion), channel_id=1, source_target_pairs={{0,4},{4,0},{8,12},{12,8},{16,20},{20,16},{24,28},{28,24},{32,36},... | collective-permute-start | bytes 3145736 | tf_op jit(solution)/shard_map/ppermute | solution.py:192
  161.4 23.5 %all-to-all-start.3 = ((bf16[32,32,512]{2,1,0:T(8,128)(2,1)}), bf16[32,32,512]{2,1,0:T(8,128)(2,1)S(1)}, u32[]{:S(2)}, u32[]{:S(2)}) async-start(bf16[32,32,512]{2,1,0:T(8,128)(2,1)} %bitcast.50), calls=%async_computation.3 | async-start | bytes 2097152 | tf_op jit(solution)/shard_map/all_to_all | solution.py:196
  (8 other events, 70.1 us)
Sparse Core Ops, SparseCore 0:
  18.0 90.7 all-gather.2
  129.2 22.1 all-gather.4

commit v7 on v6

--- a/solution.py
+++ b/solution.py
@@ -81,7 +81,8 @@
     normed = normalize(full_rows, ln_gain, ln_bias)
     local_rows = normed.shape[0]
     groups_here = prompt_len.shape[0]
-    gathered = lax.all_gather(normed, "grp", axis=0, tiled=True)
+    quarter = lax.dynamic_slice_in_dim(normed, lax.axis_index("head") * width_here, width_here, axis=1)
+    gathered = lax.all_gather(quarter, "grp", axis=0, tiled=True)
     block = w_qkv.shape[0]
     pair_rows = normed.reshape(local_rows, grp_count // 2, 2 * block)
     columns = lax.all_to_all(
@@ -173,13 +174,12 @@
     down_blocks = head_exchange(w_down.reshape(units, head_count, width_here), 1).reshape(
         units * head_count, width_here
     )
+    in_blocks = head_exchange(w_in.reshape(head_count, width_here, units), 0)
+    in_blocks = jnp.moveaxis(in_blocks, 0, 1).reshape(width_here, head_count * units)
+    partial = jnp.dot(gathered, in_blocks, preferred_element_type=jnp.float32)
+    partial = head_exchange(partial.astype(jnp.bfloat16).reshape(-1, head_count, units), 1)
     hidden = jax.nn.gelu(
-        jnp.dot(
-            gathered,
-            w_in,
-            preferred_element_type=jnp.float32,
-        )
-        + b_in.astype(jnp.float32),
+        jnp.sum(partial.astype(jnp.float32), axis=0) + b_in.astype(jnp.float32),
         approximate=True,
     ).astype(jnp.bfloat16)
     hidden = lax.all_gather(hidden, "head", axis=1, tiled=True)

time: 194 us -> 204 us (1.052)
  waiting for transfers between devices: 84.7 us -> 54.1 us
  local copies, waits for them, and re-layouts: 14.8 us -> 37.6 us
  starting transfers between devices: 41.8 us -> 54.6 us
  other arithmetic: 15.7 us -> 24.8 us
  matrix products: 21.4 us -> 17.1 us
    all_to_all x1, waiting for transfers between devices: 39.9 us -> 0.01 us  [local(): lax.all_to_all(term.reshape(grp_count, local_rows, 3, half), 'grp', 0, 0,...]
    dynamic_slice x6 -> x7, local copies, waits for them, and re-layouts: 1.98 us -> 11.9 us  [head_exchange(): lax.dynamic_index_in_dim(pieces, (here + shift) % count, axis, keepdims=F...]
    ppermute x6 -> x12, waiting for transfers between devices: 0.02 us -> 9.58 us  [head_exchange(): lax.ppermute(piece, 'head', [(i, (i + shift) % count) for i in range(coun...]
    ppermute x6 -> x12, starting transfers between devices: 6.93 us -> 15 us  [head_exchange(): lax.ppermute(piece, 'head', [(i, (i + shift) % count) for i in range(coun...]
    all_gather x1, waiting for transfers between devices: 0.02 us -> 5.94 us  [local(): gathered = lax.all_gather(quarter, 'grp', axis=0, tiled=True)]
    gather x2 -> x4, local copies, waits for them, and re-layouts: 1.18 us -> 5.62 us  [head_exchange(): return jnp.take(stacked, (here - jnp.arange(count)) % count, axis=0)]
    dot_general x1, matrix products: 6.46 us -> 2.87 us  [local(): partial = jnp.dot(gathered, in_blocks, preferred_element_type=jnp.float32)]
    ppermute x6, waiting for transfers between devices: 6.15 us -> 2.84 us  [head_gather(): lax.ppermute(piece, 'head', [(i, (i + shift) % count) for i in range(coun...]
  transfers between devices with their start and end apart: 20 -> 26, of which waited for: 10 -> 14; matrix products, arithmetic and copies ran while one was open for 22% -> 32% of each run, Pallas kernels for 0% -> 0%
where the time goes in v7:
time: 204 us; the launch traced here: 203 us
  starting transfers between devices  54.6 us (27%)
  waiting for transfers between devices  54.1 us (27%)
  local copies, waits for them, and re-layouts  37.6 us (18%)
  other arithmetic  24.8 us (12%)
  matrix products  17.1 us (8%)
  between operations  14.3 us (7%)
    all_to_all x1, waiting for transfers between devices, local(): lax.all_to_all(pair_sum.reshape(grp_count, local_rows, half_width), 'grp'...  17 us
    ppermute x12, starting transfers between devices, head_exchange(): lax.ppermute(piece, 'head', [(i, (i + shift) % count) for i in range(coun...  15 us
    dynamic_slice x7, local copies, waits for them, and re-layouts, head_exchange(): lax.dynamic_index_in_dim(pieces, (here + shift) % count, axis, keepdims=F...  11.9 us
    ppermute x6, starting transfers between devices, head_gather(): lax.ppermute(piece, 'head', [(i, (i + shift) % count) for i in range(coun...  10.4 us
    all_to_all x1, starting transfers between devices, local(): lax.all_to_all(jnp.repeat(pair_rows, 2, axis=1), 'grp', split_axis=1, con...  10.1 us
    ppermute x12, waiting for transfers between devices, head_exchange(): lax.ppermute(piece, 'head', [(i, (i + shift) % count) for i in range(coun...  9.58 us
    all_to_all x1, waiting for transfers between devices, local(): lax.all_to_all(jnp.repeat(pair_rows, 2, axis=1), 'grp', split_axis=1, con...  9.53 us
    all_to_all x1, starting transfers between devices, local(): lax.all_to_all(transposed, 'grp', split_axis=0, concat_axis=2, tiled=True)  6.81 us
  transfers between devices with their start and end apart: 26, of which 14 were waited for; matrix products, arithmetic and copies ran while one was open for 32% of the time, Pallas kernels for 0%

profile of v7, /device:TPU:1, one launch (start us, length us, event | category | flops | bytes accessed | tf_op | source)
XLA Modules:
  0.0 202.6 jit_solution(2363949606909611677)
XLA Ops:
  8.6 2.5 %collective-permute-start.1 = (bf16[32,1024]{1,0:T(8,128)(2,1)}, bf16[32,1024]{1,0:T(8,128)(2,1)S(1)}, u32[]{:S(2)}, u32[]{:S(2)}) collective-permute-start(bf16[32,1024]{1,0:T(8,128)(2,1)} %param.19), channel_id=1, source_target_pairs={{0,2},{1,3},{2,0},{3,1},{4,6},{5,7},{6,4},{7,5},{8,10},{9,11},{10,... | collective-permute-start | bytes 196616 | tf_op jit(solution)/shard_map/ppermute | solution.py:55
  19.5 10.1 %all-to-all-start = ((bf16[32,32,256]{2,0,1:T(8,128)(2,1)}), bf16[32,32,256]{2,0,1:T(8,128)(2,1)S(1)}, u32[]{:S(2)}, u32[]{:S(2)}) async-start(bf16[32,32,256]{2,0,1:T(8,128)(2,1)} %bitcast.33), calls=%async_computation | async-start | bytes 1048576 | tf_op jit(solution)/shard_map/all_to_all | solution.py:88
  31.4 9.5 %all-to-all-done = bf16[32,32,256]{2,0,1:T(8,128)(2,1)S(1)} async-done(((bf16[32,32,256]{2,0,1:T(8,128)(2,1)}), bf16[32,32,256]{2,0,1:T(8,128)(2,1)S(1)}, u32[]{:S(2)}, u32[]{:S(2)}) %all-to-all-start) | async-done | bytes 524320 | tf_op jit(solution)/shard_map/all_to_all | solution.py:88
  44.1 4.1 %all-to-all-start.1 = ((bf16[32,32,3,512]{3,1,2,0:T(8,128)(2,1)}), bf16[32,32,3,512]{3,1,2,0:T(8,128)(2,1)S(1)}, u32[]{:S(2)}, u32[]{:S(2)}) async-start(bf16[32,32,3,512]{3,1,2,0:T(8,128)(2,1)} %copy.141), calls=%async_computation.1 | async-start | bytes 6291456 | tf_op jit(solution)/shard_map/all_to_all | solution.py:104
  48.3 2.2 %constant_dynamic-slice_fusion.10 = (bf16[1,1024,128]{2,1,0:T(8,128)(2,1)}, bf16[1024,128]{1,0:T(8,128)(2,1)}, bf16[1024,128]{1,0:T(8,128)(2,1)}, bf16[1024,128]{1,0:T(8,128)(2,1)}) fusion(bf16[4,1024,128]{2,1,0:T(8,128)(2,1)} %bitcast.204, s32[]{:T(128)S(6)} %select_n.193, s32[]{:T(128)S(6)} %select_n.199, s32[]{:T(128)S(6)} %select_n.197, s32[]{:T(128)S(6)} %select_n.195), kind=kLoop, calls=%fused_computation.135 | loop fusion | bytes 2097168 | tf_op jit(solution)/shard_map/jit(dynamic_index_in_dim)/dynamic_slice | solution.py:42
  61.5 2.3 %copy.134 = bf16[128,4096]{0,1:T(8,128)(2,1)} copy(bf16[128,4096]{1,0:T(8,128)(2,1)} %param.32) | data formatting | bytes 2097152 | tf_op args[13]
  87.6 2.3 %pad_maximum_fusion = bf16[4,1024,128]{2,1,0:T(8,128)(2,1)} fusion(bf16[1,1024,128]{2,1,0:T(8,128)(2,1)} %bitcast.12, bf16[1,1024,128]{2,1,0:T(8,128)(2,1)} %bitcast.10, bf16[1,1024,128]{2,1,0:T(8,128)(2,1)} %bitcast.8, bf16[1,1024,128]{2,1,0:T(8,128)(2,1)} %get-tuple-element.17), kind=kLoop, calls=%fused_computation.30 | loop fusion | flops 1572864 | bytes 2097152 | tf_op jit(solution)/shard_map/stack | solution.py:46
  89.9 2.9 %gather_fusion.2 = bf16[4,1024,128]{2,1,0:T(8,128)(2,1)} fusion(bf16[4,1024,128]{2,1,0:T(8,128)(2,1)} %pad_maximum_fusion, s32[1024]{0:T(1024)S(1)} %pad_clamp_fusion), kind=kCustom, calls=%fused_computation.clone | custom fusion | bytes 2097168 | tf_op jit(solution)/shard_map/jit(_take)/gather | solution.py:47
  92.8 2.4 %select_bitcast_fusion = bf16[1024,4,128]{2,0,1:T(8,128)(2,1)} fusion(bf16[4,1024,128]{2,1,0:T(8,128)(2,1)} %gather_fusion.2, pred[4]{0:T(512)(128)(4,1)S(1)} %copy-done.16), kind=kLoop, calls=%fused_computation.34 | loop fusion | flops 524288 | bytes 2097156 | tf_op jit(solution)/shard_map/transpose | solution.py:178
  95.2 2.3 %copy.133 = bf16[1024,4,128]{0,2,1:T(8,128)(2,1)} copy(bf16[1024,4,128]{2,0,1:T(8,128)(2,1)} %select_bitcast_fusion) | data formatting | bytes 2097152 | tf_op jit(solution)/shard_map/transpose | solution.py:178
  100.4 3.5 %fusion.78 = (f32[2,16,4]{1,2,0:T(4,128)S(1)}, f32[2,16,4,1024]{3,1,2,0:T(8,128)S(1)}) fusion(bf16[2,128,4,8,256]{4,3,2,1,0:T(8,128)(2,1)} %bitcast.196, bf16[2,16,4,64]{3,1,2,0:T(8,128)(2,1)S(1)} %copy.146, pred[2,1024]{1,0:T(4,128)(4,1)S(1)} %copy-done.12, bf16[2,16,4,192]{3,1,0,2:T(8,128)(2,1)S(1)} %bitcast.210), kind=kOutput, calls=%fused_computation.169 | convolution fusion | flops 67633024 | bytes 4786688 | tf_op jit(solution)/shard_map/gqhd,gjhd->gqhj/dot_general | solution.py:125
  104.0 2.4 %fusion.9 = f32[32,4,1,32]{3,2,1,0:T(1,128)S(1)} fusion(bf16[32,4,4,8,256]{4,3,2,1,0:T(8,128)(2,1)} %bitcast.236, bf16[32,4,256,1]{2,0,1,3:T(8,128)(2,1)S(1)} %get-tuple-element.35), kind=kOutput, calls=%fused_computation.18 | convolution fusion | flops 2097152 | bytes 2179072 | tf_op jit(solution)/shard_map/rhd,rthd->rht/dot_general | solution.py:133
  108.8 5.9 %all-gather.3.cloned.1.call-done = bf16[1024,1024]{1,0:T(8,128)(2,1)} async-done(((bf16[32,1024]{1,0:T(8,128)(2,1)}), bf16[1024,1024]{1,0:T(8,128)(2,1)}) %all-gather.3.cloned.1.call-update) | async-done | bytes 2097168 | tf_op jit(solution)/shard_map/all_gather | solution.py:85
  114.8 2.9 %convolution_convert_fusion.1 = bf16[1024,512]{0,1:T(8,128)(2,1)S(1)} fusion(bf16[1024,1024]{1,0:T(8,128)(2,1)} %all-gather.3.cloned.1.call-done, bf16[1024,512]{0,1:T(8,128)(2,1)S(1)} %bitcast.206), kind=kOutput, calls=%fused_computation.25 | convolution fusion | flops 1074266112 | bytes 4194304 | tf_op jit(solution)/shard_map/dot_general | solution.py:179
  119.1 2.4 %collective-permute-start.7 = (bf16[1024,128]{0,1:T(8,128)(2,1)S(1)}, bf16[1024,128]{0,1:T(8,128)(2,1)S(1)}, u32[]{:S(2)}, u32[]{:S(2)}) collective-permute-start(bf16[1024,128]{0,1:T(8,128)(2,1)S(1)} %get-tuple-element.15), channel_id=1, source_target_pairs={{0,2},{1,3},{2,0},{3,1},{4,6},{5,7},{6,4},{7,5},{8,10},{9,11},{10,... | collective-permute-start | bytes 786440 | tf_op jit(solution)/shard_map/ppermute | solution.py:44
  123.7 2.9 %collective-permute-done.6 = bf16[1024,128]{0,1:T(8,128)(2,1)S(1)} collective-permute-done((bf16[1024,128]{0,1:T(8,128)(2,1)S(1)}, bf16[1024,128]{0,1:T(8,128)(2,1)S(1)}, u32[]{:S(2)}, u32[]{:S(2)}) %collective-permute-start.6) | collective-permute-done | bytes 262176 | tf_op jit(solution)/shard_map/ppermute | solution.py:44
  127.9 5.3 %collective-permute-done.7 = bf16[1024,128]{0,1:T(8,128)(2,1)S(1)} collective-permute-done((bf16[1024,128]{0,1:T(8,128)(2,1)S(1)}, bf16[1024,128]{0,1:T(8,128)(2,1)S(1)}, u32[]{:S(2)}, u32[]{:S(2)}) %collective-permute-start.7) | collective-permute-done | bytes 262176 | tf_op jit(solution)/shard_map/ppermute | solution.py:44
  136.1 2.9 %fusion.21 = f32[2,16,4,256]{3,1,2,0:T(8,128)S(1)} fusion(bf16[2,128,4,8,256]{4,3,2,1,0:T(8,128)(2,1)} %bitcast.198, f32[2,16,4,1024]{3,1,2,0:T(8,128)S(1)} %get-tuple-element.42, f32[2,16,4]{1,2,0:T(4,128)S(1)} %copy.153), kind=kOutput, calls=%fused_computation.29 | convolution fusion | flops 67371008 | bytes 4850176 | tf_op jit(solution)/shard_map/gqhj,gjhd->gqhd/dot_general | solution.py:151
  140.3 6.8 %all-to-all-start.2 = ((bf16[32,2,512]{2,1,0:T(2,128)(2,1)}), bf16[32,2,512]{2,1,0:T(2,128)(2,1)S(1)}, u32[]{:S(2)}, u32[]{:S(2)}) async-start(bf16[32,2,512]{2,1,0:T(2,128)(2,1)} %reshape.422), calls=%async_computation.2 | async-start | bytes 131072 | tf_op jit(solution)/shard_map/all_to_all | solution.py:166
  149.1 5.4 %all-to-all-done.2 = bf16[32,2,512]{2,1,0:T(2,128)(2,1)S(1)} async-done(((bf16[32,2,512]{2,1,0:T(2,128)(2,1)}), bf16[32,2,512]{2,1,0:T(2,128)(2,1)S(1)}, u32[]{:S(2)}, u32[]{:S(2)}) %all-to-all-start.2) | async-done | bytes 65568 | tf_op jit(solution)/shard_map/all_to_all | solution.py:166
  162.8 2.6 %fusion.79 = f32[1024,1024]{1,0:T(8,128)S(1)} fusion(bf16[1024,512]{0,1:T(8,128)(2,1)} %all-gather.5.cloned.1.call-done, bf16[512,1024]{1,0:T(8,128)(2,1)S(1)} %bitcast_select_fusion), kind=kOutput, calls=%fused_computation.170 | convolution fusion | flops 1073741824 | bytes 6291456 | tf_op jit(solution)/shard_map/dot_general | solution.py:186
  167.6 2.3 %collective-permute-done.19 = bf16[1024,512]{1,0:T(8,128)(2,1)S(1)} collective-permute-done((bf16[1024,512]{1,0:T(8,128)(2,1)S(1)}, bf16[1024,512]{1,0:T(8,128)(2,1)S(1)}, u32[]{:S(2)}, u32[]{:S(2)}) %collective-permute-start.19) | collective-permute-done | bytes 1048608 | tf_op jit(solution)/shard_map/ppermute | solution.py:192
  171.2 6.6 %all-to-all-start.3 = ((bf16[32,32,512]{2,1,0:T(8,128)(2,1)}), bf16[32,32,512]{2,1,0:T(8,128)(2,1)S(1)}, u32[]{:S(2)}, u32[]{:S(2)}) async-start(bf16[32,32,512]{2,1,0:T(8,128)(2,1)} %bitcast.67), calls=%async_computation.3 | async-start | bytes 2097152 | tf_op jit(solution)/shard_map/all_to_all | solution.py:196
  177.9 17.0 %all-to-all-done.3 = bf16[32,32,512]{2,1,0:T(8,128)(2,1)S(1)} async-done(((bf16[32,32,512]{2,1,0:T(8,128)(2,1)}), bf16[32,32,512]{2,1,0:T(8,128)(2,1)S(1)}, u32[]{:S(2)}, u32[]{:S(2)}) %all-to-all-start.3) | async-done | bytes 1048608 | tf_op jit(solution)/shard_map/all_to_all | solution.py:196
  (216 shorter events, 78.9 us)
Async XLA Ops:
  6.5 7.1 %collective-permute-start = (bf16[32,1024]{1,0:T(8,128)(2,1)}, bf16[32,1024]{1,0:T(8,128)(2,1)S(1)}, u32[]{:S(2)}, u32[]{:S(2)}) collective-permute-start(bf16[32,1024]{1,0:T(8,128)(2,1)} %param.19), channel_id=1, source_target_pairs={{0,1},{1,2},{2,3},{3,0},{4,5},{5,6},{6,7},{7,4},{8,9},{9,10},{10,1... | collective-permute-start | bytes 196616 | tf_op jit(solution)/shard_map/ppermute | solution.py:55
  8.6 5.3 %collective-permute-start.1 = (bf16[32,1024]{1,0:T(8,128)(2,1)}, bf16[32,1024]{1,0:T(8,128)(2,1)S(1)}, u32[]{:S(2)}, u32[]{:S(2)}) collective-permute-start(bf16[32,1024]{1,0:T(8,128)(2,1)} %param.19), channel_id=1, source_target_pairs={{0,2},{1,3},{2,0},{3,1},{4,6},{5,7},{6,4},{7,5},{8,10},{9,11},{10,... | collective-permute-start | bytes 196616 | tf_op jit(solution)/shard_map/ppermute | solution.py:55
  11.0 3.8 %collective-permute-start.2 = (bf16[32,1024]{1,0:T(8,128)(2,1)}, bf16[32,1024]{1,0:T(8,128)(2,1)S(1)}, u32[]{:S(2)}, u32[]{:S(2)}) collective-permute-start(bf16[32,1024]{1,0:T(8,128)(2,1)} %param.19), channel_id=1, source_target_pairs={{0,3},{1,0},{2,1},{3,2},{4,7},{5,4},{6,5},{7,6},{8,11},{9,8},{10,9... | collective-permute-start | bytes 196616 | tf_op jit(solution)/shard_map/ppermute | solution.py:55
  19.5 21.5 %all-to-all-start = ((bf16[32,32,256]{2,0,1:T(8,128)(2,1)}), bf16[32,32,256]{2,0,1:T(8,128)(2,1)S(1)}, u32[]{:S(2)}, u32[]{:S(2)}) async-start(bf16[32,32,256]{2,0,1:T(8,128)(2,1)} %bitcast.33), calls=%async_computation | async-start | bytes 1048576 | tf_op jit(solution)/shard_map/all_to_all | solution.py:88
  44.1 53.4 %all-to-all-start.1 = ((bf16[32,32,3,512]{3,1,2,0:T(8,128)(2,1)}), bf16[32,32,3,512]{3,1,2,0:T(8,128)(2,1)S(1)}, u32[]{:S(2)}, u32[]{:S(2)}) async-start(bf16[32,32,3,512]{3,1,2,0:T(8,128)(2,1)} %copy.141), calls=%async_computation.1 | async-start | bytes 6291456 | tf_op jit(solution)/shard_map/all_to_all | solution.py:104
  48.2 66.6 %all-gather.3.cloned.1.call-start = ((), (), s32[]{:S(2)}) async-start(), calls=%async_computation.4 | async-start | bytes 2162688 | tf_op jit(solution)/shard_map/all_gather | solution.py:85
  50.5 37.1 %collective-permute-start.4 = (bf16[1024,128]{1,0:T(8,128)(2,1)}, bf16[1024,128]{1,0:T(8,128)(2,1)}, u32[]{:S(2)}, u32[]{:S(2)}) collective-permute-start(bf16[1024,128]{1,0:T(8,128)(2,1)} %get-tuple-element.19), channel_id=1, source_target_pairs={{0,2},{1,3},{2,0},{3,1},{4,6},{5,7},{6,4},{7,5},{8,10},{9,11},{10,... | collective-permute-start | bytes 786440 | tf_op jit(solution)/shard_map/ppermute | solution.py:44
  51.8 35.8 %collective-permute-start.5 = (bf16[1024,128]{1,0:T(8,128)(2,1)}, bf16[1024,128]{1,0:T(8,128)(2,1)}, u32[]{:S(2)}, u32[]{:S(2)}) collective-permute-start(bf16[1024,128]{1,0:T(8,128)(2,1)} %get-tuple-element.18), channel_id=1, source_target_pairs={{0,3},{1,0},{2,1},{3,2},{4,7},{5,4},{6,5},{7,6},{8,11},{9,8},{10,9... | collective-permute-start | bytes 786440 | tf_op jit(solution)/shard_map/ppermute | solution.py:44
  53.2 34.4 %collective-permute-start.3 = (bf16[1024,128]{1,0:T(8,128)(2,1)}, bf16[1024,128]{1,0:T(8,128)(2,1)}, u32[]{:S(2)}, u32[]{:S(2)}) collective-permute-start(bf16[1024,128]{1,0:T(8,128)(2,1)} %get-tuple-element.20), channel_id=1, source_target_pairs={{0,1},{1,2},{2,3},{3,0},{4,5},{5,6},{6,7},{7,4},{8,9},{9,10},{10,1... | collective-permute-start | bytes 786440 | tf_op jit(solution)/shard_map/ppermute | solution.py:44
  56.6 24.5 %collective-permute-start.16 = (bf16[8,4,1024]{2,0,1:T(8,128)(2,1)}, bf16[8,4,1024]{2,0,1:T(8,128)(2,1)}, u32[]{:S(2)}, u32[]{:S(2)}) collective-permute-start(bf16[8,4,1024]{2,0,1:T(8,128)(2,1)} %bitcast.193), channel_id=1, source_target_pairs={{0,1},{1,2},{2,3},{3,0},{4,5},{5,6},{6,7},{7,4},{8,9},{9,10},{10,1... | collective-permute-start | bytes 196616 | tf_op jit(solution)/shard_map/ppermute | solution.py:44
  58.8 23.3 %collective-permute-start.17 = (bf16[8,4,1024]{2,0,1:T(8,128)(2,1)}, bf16[8,4,1024]{2,0,1:T(8,128)(2,1)}, u32[]{:S(2)}, u32[]{:S(2)}) collective-permute-start(bf16[8,4,1024]{2,0,1:T(8,128)(2,1)} %bitcast.192), channel_id=1, source_target_pairs={{0,2},{1,3},{2,0},{3,1},{4,6},{5,7},{6,4},{7,5},{8,10},{9,11},{10,... | collective-permute-start | bytes 196616 | tf_op jit(solution)/shard_map/ppermute | solution.py:44
  69.3 93.5 %all-gather.5.cloned.1.call-start = ((), (), s32[]{:S(2)}) async-start(), calls=%async_computation.5 | async-start | bytes 1310720 | tf_op jit(solution)/shard_map/all_gather | solution.py:185
  81.1 3.6 %collective-permute-start.18 = (bf16[8,4,1024]{2,0,1:T(8,128)(2,1)S(1)}, bf16[8,4,1024]{2,0,1:T(8,128)(2,1)S(1)}, u32[]{:S(2)}, u32[]{:S(2)}) collective-permute-start(bf16[8,4,1024]{2,0,1:T(8,128)(2,1)S(1)} %bitcast.228), channel_id=1, source_target_pairs={{0,3},{1,0},{2,1},{3,2},{4,7},{5,4},{6,5},{7,6},{8,11},{9,8},{10,9... | collective-permute-start | bytes 196616 | tf_op jit(solution)/shard_map/ppermute | solution.py:44
  82.1 65.0 %collective-permute-start.9 = (bf16[128,1024]{1,0:T(8,128)(2,1)}, bf16[128,1024]{1,0:T(8,128)(2,1)}, u32[]{:S(2)}, u32[]{:S(2)}) collective-permute-start(bf16[128,1024]{1,0:T(8,128)(2,1)} %bitcast.221), channel_id=1, source_target_pairs={{0,1},{1,2},{2,3},{3,0},{4,5},{5,6},{6,7},{7,4},{8,9},{9,10},{10,1... | collective-permute-start | bytes 786440 | tf_op jit(solution)/shard_map/ppermute | solution.py:44
  84.7 62.4 %collective-permute-start.10 = (bf16[128,1024]{1,0:T(8,128)(2,1)}, bf16[128,1024]{1,0:T(8,128)(2,1)}, u32[]{:S(2)}, u32[]{:S(2)}) collective-permute-start(bf16[128,1024]{1,0:T(8,128)(2,1)} %bitcast.220), channel_id=1, source_target_pairs={{0,2},{1,3},{2,0},{3,1},{4,6},{5,7},{6,4},{7,5},{8,10},{9,11},{10,... | collective-permute-start | bytes 786440 | tf_op jit(solution)/shard_map/ppermute | solution.py:44
  117.8 8.9 %collective-permute-start.6 = (bf16[1024,128]{0,1:T(8,128)(2,1)S(1)}, bf16[1024,128]{0,1:T(8,128)(2,1)S(1)}, u32[]{:S(2)}, u32[]{:S(2)}) collective-permute-start(bf16[1024,128]{0,1:T(8,128)(2,1)S(1)} %get-tuple-element.16), channel_id=1, source_target_pairs={{0,1},{1,2},{2,3},{3,0},{4,5},{5,6},{6,7},{7,4},{8,9},{9,10},{10,1... | collective-permute-start | bytes 786440 | tf_op jit(solution)/shard_map/ppermute | solution.py:44
  119.1 14.1 %collective-permute-start.7 = (bf16[1024,128]{0,1:T(8,128)(2,1)S(1)}, bf16[1024,128]{0,1:T(8,128)(2,1)S(1)}, u32[]{:S(2)}, u32[]{:S(2)}) collective-permute-start(bf16[1024,128]{0,1:T(8,128)(2,1)S(1)} %get-tuple-element.15), channel_id=1, source_target_pairs={{0,2},{1,3},{2,0},{3,1},{4,6},{5,7},{6,4},{7,5},{8,10},{9,11},{10,... | collective-permute-start | bytes 786440 | tf_op jit(solution)/shard_map/ppermute | solution.py:44
  121.5 11.7 %collective-permute-start.8 = (bf16[1024,128]{0,1:T(8,128)(2,1)S(1)}, bf16[1024,128]{0,1:T(8,128)(2,1)S(1)}, u32[]{:S(2)}, u32[]{:S(2)}) collective-permute-start(bf16[1024,128]{0,1:T(8,128)(2,1)S(1)} %get-tuple-element.14), channel_id=1, source_target_pairs={{0,3},{1,0},{2,1},{3,2},{4,7},{5,4},{6,5},{7,6},{8,11},{9,8},{10,9... | collective-permute-start | bytes 786440 | tf_op jit(solution)/shard_map/ppermute | solution.py:44
  126.6 20.5 %collective-permute-start.11 = (bf16[128,1024]{1,0:T(8,128)(2,1)S(1)}, bf16[128,1024]{1,0:T(8,128)(2,1)S(1)}, u32[]{:S(2)}, u32[]{:S(2)}) collective-permute-start(bf16[128,1024]{1,0:T(8,128)(2,1)S(1)} %bitcast.219), channel_id=1, source_target_pairs={{0,3},{1,0},{2,1},{3,2},{4,7},{5,4},{6,5},{7,6},{8,11},{9,8},{10,9... | collective-permute-start | bytes 786440 | tf_op jit(solution)/shard_map/ppermute | solution.py:44
  140.3 14.1 %all-to-all-start.2 = ((bf16[32,2,512]{2,1,0:T(2,128)(2,1)}), bf16[32,2,512]{2,1,0:T(2,128)(2,1)S(1)}, u32[]{:S(2)}, u32[]{:S(2)}) async-start(bf16[32,2,512]{2,1,0:T(2,128)(2,1)} %reshape.422), calls=%async_computation.2 | async-start | bytes 131072 | tf_op jit(solution)/shard_map/all_to_all | solution.py:166
  155.0 5.5 %collective-permute-start.13 = (bf16[8,4,1024]{2,0,1:T(8,128)(2,1)S(1)}, bf16[8,4,1024]{2,0,1:T(8,128)(2,1)S(1)}, u32[]{:S(2)}, u32[]{:S(2)}) collective-permute-start(bf16[8,4,1024]{2,0,1:T(8,128)(2,1)S(1)} %all_to_all.37), channel_id=1, source_target_pairs={{0,1},{1,2},{2,3},{3,0},{4,5},{5,6},{6,7},{7,4},{8,9},{9,10},{10,1... | collective-permute-start | bytes 196616 | tf_op jit(solution)/shard_map/ppermute | solution.py:55
  156.2 5.0 %collective-permute-start.14 = (bf16[8,4,1024]{2,0,1:T(8,128)(2,1)S(1)}, bf16[8,4,1024]{2,0,1:T(8,128)(2,1)S(1)}, u32[]{:S(2)}, u32[]{:S(2)}) collective-permute-start(bf16[8,4,1024]{2,0,1:T(8,128)(2,1)S(1)} %all_to_all.37), channel_id=1, source_target_pairs={{0,2},{1,3},{2,0},{3,1},{4,6},{5,7},{6,4},{7,5},{8,10},{9,11},{10,... | collective-permute-start | bytes 196616 | tf_op jit(solution)/shard_map/ppermute | solution.py:55
  157.9 4.2 %collective-permute-start.15 = (bf16[8,4,1024]{2,0,1:T(8,128)(2,1)S(1)}, bf16[8,4,1024]{2,0,1:T(8,128)(2,1)S(1)}, u32[]{:S(2)}, u32[]{:S(2)}) collective-permute-start(bf16[8,4,1024]{2,0,1:T(8,128)(2,1)S(1)} %all_to_all.37), channel_id=1, source_target_pairs={{0,3},{1,0},{2,1},{3,2},{4,7},{5,4},{6,5},{7,6},{8,11},{9,8},{10,9... | collective-permute-start | bytes 196616 | tf_op jit(solution)/shard_map/ppermute | solution.py:55
  171.2 23.7 %all-to-all-start.3 = ((bf16[32,32,512]{2,1,0:T(8,128)(2,1)}), bf16[32,32,512]{2,1,0:T(8,128)(2,1)S(1)}, u32[]{:S(2)}, u32[]{:S(2)}) async-start(bf16[32,32,512]{2,1,0:T(8,128)(2,1)} %bitcast.67), calls=%async_computation.3 | async-start | bytes 2097152 | tf_op jit(solution)/shard_map/all_to_all | solution.py:196
  (34 other events, 207.2 us)
Sparse Core Ops, SparseCore 0:
  69.4 45.3 all-gather.2
  136.1 22.3 all-gather.4

commit v8 on v7

--- a/solution.py
+++ b/solution.py
@@ -81,8 +81,20 @@
     normed = normalize(full_rows, ln_gain, ln_bias)
     local_rows = normed.shape[0]
     groups_here = prompt_len.shape[0]
-    quarter = lax.dynamic_slice_in_dim(normed, lax.axis_index("head") * width_here, width_here, axis=1)
-    gathered = lax.all_gather(quarter, "grp", axis=0, tiled=True)
+    floats = full_rows.astype(jnp.float32)
+    mean = jnp.mean(floats, axis=-1, keepdims=True)
+    center = floats - mean
+    scale_of_row = lax.rsqrt(jnp.mean(center * center, axis=-1, keepdims=True) + 1e-05)
+    row_stats = lax.all_gather(
+        jnp.concatenate([mean, scale_of_row], axis=1), "grp", axis=0, tiled=True
+    )
+    raw_quarter = lax.all_gather(activations, "grp", axis=0, tiled=True).astype(jnp.float32)
+    feature_start = lax.axis_index("head") * width_here
+    gain_quarter = lax.dynamic_slice_in_dim(ln_gain, feature_start, width_here).astype(jnp.float32)
+    bias_quarter = lax.dynamic_slice_in_dim(ln_bias, feature_start, width_here).astype(jnp.float32)
+    gathered = (
+        (raw_quarter - row_stats[:, :1]) * row_stats[:, 1:] * gain_quarter + bias_quarter
+    ).astype(jnp.bfloat16)
     block = w_qkv.shape[0]
     pair_rows = normed.reshape(local_rows, grp_count // 2, 2 * block)
     columns = lax.all_to_all(

time: 204 us -> 217 us (1.064)
  blocking collectives: 0 us -> 30.9 us
  waiting for transfers between devices: 54.1 us -> 48.4 us
  other arithmetic: 24.8 us -> 19.7 us
  local copies, waits for them, and re-layouts: 37.6 us -> 33.8 us
  starting transfers between devices: 54.6 us -> 51.1 us
    all_gather x0 -> x1, blocking collectives: none -> 30.9 us  [local(): lax.all_gather(jnp.concatenate([mean, scale_of_row], axis=1), 'grp', axis...]
    all_gather x1, waiting for transfers between devices: 5.94 us -> 0.01 us  [local(): lax.all_gather(activations, 'grp', axis=0, tiled=True).astype(jnp.float32)]
    unnamed x74 -> x51, local copies, waits for them, and re-layouts: 6.23 us -> 3.7 us
  transfers between devices with their start and end apart: 26 -> 26, of which waited for: 14 -> 10; matrix products, arithmetic and copies ran while one was open for 32% -> 28% of each run, Pallas kernels for 0% -> 0%
where the time goes in v8:
time: 217 us; the launch traced here: 216 us
  starting transfers between devices  51.1 us (24%)
  waiting for transfers between devices  48.4 us (22%)
  local copies, waits for them, and re-layouts  33.8 us (16%)
  blocking collectives  30.9 us (14%)
  other arithmetic  19.7 us (9%)
  matrix products  17.4 us (8%)
  between operations  14.3 us (7%)
    all_gather x1, blocking collectives, local(): lax.all_gather(jnp.concatenate([mean, scale_of_row], axis=1), 'grp', axis...  30.9 us
    all_to_all x1, waiting for transfers between devices, local(): lax.all_to_all(pair_sum.reshape(grp_count, local_rows, half_width), 'grp'...  17 us
    ppermute x12, starting transfers between devices, head_exchange(): lax.ppermute(piece, 'head', [(i, (i + shift) % count) for i in range(coun...  15.9 us
    dynamic_slice x7, local copies, waits for them, and re-layouts, head_exchange(): lax.dynamic_index_in_dim(pieces, (here + shift) % count, axis, keepdims=F...  11.3 us
    all_to_all x1, starting transfers between devices, local(): lax.all_to_all(jnp.repeat(pair_rows, 2, axis=1), 'grp', split_axis=1, con...  10.1 us
    ppermute x12, waiting for transfers between devices, head_exchange(): lax.ppermute(piece, 'head', [(i, (i + shift) % count) for i in range(coun...  9.57 us
    all_to_all x1, waiting for transfers between devices, local(): lax.all_to_all(jnp.repeat(pair_rows, 2, axis=1), 'grp', split_axis=1, con...  9.29 us
    ppermute x6, starting transfers between devices, head_gather(): lax.ppermute(piece, 'head', [(i, (i + shift) % count) for i in range(coun...  8.41 us
  transfers between devices with their start and end apart: 26, of which 10 were waited for; matrix products, arithmetic and copies ran while one was open for 28% of the time, Pallas kernels for 0%

profile of v8, /device:TPU:1, one launch (start us, length us, event | category | flops | bytes accessed | tf_op | source)
XLA Modules:
  0.0 215.6 jit_solution(5442348813475220614)
XLA Ops:
  8.6 2.5 %collective-permute-start.1 = (bf16[32,1024]{1,0:T(8,128)(2,1)}, bf16[32,1024]{1,0:T(8,128)(2,1)S(1)}, u32[]{:S(2)}, u32[]{:S(2)}) collective-permute-start(bf16[32,1024]{1,0:T(8,128)(2,1)} %param.19), channel_id=1, source_target_pairs={{0,2},{1,3},{2,0},{3,1},{4,6},{5,7},{6,4},{7,5},{8,10},{9,11},{10,... | collective-permute-start | bytes 196616 | tf_op jit(solution)/shard_map/ppermute | solution.py:55
  19.7 10.1 %all-to-all-start = ((bf16[32,32,256]{2,0,1:T(8,128)(2,1)}), bf16[32,32,256]{2,0,1:T(8,128)(2,1)S(1)}, u32[]{:S(2)}, u32[]{:S(2)}) async-start(bf16[32,32,256]{2,0,1:T(8,128)(2,1)} %bitcast.38), calls=%async_computation | async-start | bytes 1048576 | tf_op jit(solution)/shard_map/all_to_all | solution.py:100
  31.9 9.3 %all-to-all-done = bf16[32,32,256]{2,0,1:T(8,128)(2,1)S(1)} async-done(((bf16[32,32,256]{2,0,1:T(8,128)(2,1)}), bf16[32,32,256]{2,0,1:T(8,128)(2,1)S(1)}, u32[]{:S(2)}, u32[]{:S(2)}) %all-to-all-start) | async-done | bytes 524320 | tf_op jit(solution)/shard_map/all_to_all | solution.py:100
  44.3 4.1 %all-to-all-start.1 = ((bf16[32,32,3,512]{3,1,2,0:T(8,128)(2,1)}), bf16[32,32,3,512]{3,1,2,0:T(8,128)(2,1)S(1)}, u32[]{:S(2)}, u32[]{:S(2)}) async-start(bf16[32,32,3,512]{3,1,2,0:T(8,128)(2,1)} %copy.141), calls=%async_computation.1 | async-start | bytes 6291456 | tf_op jit(solution)/shard_map/all_to_all | solution.py:116
  53.6 3.2 %collective-permute-start.10 = (bf16[128,1024]{1,0:T(8,128)(2,1)}, bf16[128,1024]{1,0:T(8,128)(2,1)}, u32[]{:S(2)}, u32[]{:S(2)}) collective-permute-start(bf16[128,1024]{1,0:T(8,128)(2,1)} %bitcast.226), channel_id=1, source_target_pairs={{0,2},{1,3},{2,0},{3,1},{4,6},{5,7},{6,4},{7,5},{8,10},{9,11},{10,... | collective-permute-start | bytes 786440 | tf_op jit(solution)/shard_map/ppermute | solution.py:44
  76.7 30.9 %all-gather = f32[32,32,2]{1,2,0:T(2,128)S(1)} all-gather(f32[1,32,2]{1,2,0:T(2,128)S(1)} %maximum_bitcast_fusion), channel_id=1, replica_groups=mesh['grp'=32,'head'=4] {'grp'}, dimensions={0}, use_global_device_ids=true | all-gather | bytes 8448 | tf_op jit(solution)/shard_map/all_gather | solution.py:88
  109.1 2.3 %pad_maximum_fusion = bf16[4,1024,128]{2,1,0:T(8,128)(2,1)} fusion(bf16[1,1024,128]{2,1,0:T(8,128)(2,1)} %bitcast.16, bf16[1,1024,128]{2,1,0:T(8,128)(2,1)} %bitcast.14, bf16[1,1024,128]{2,1,0:T(8,128)(2,1)} %bitcast.12, bf16[1,1024,128]{2,1,0:T(8,128)(2,1)} %get-tuple-element.17), kind=kLoop, calls=%fused_computation.36 | loop fusion | flops 1572864 | bytes 2097152 | tf_op jit(solution)/shard_map/stack | solution.py:46
  111.4 2.9 %gather_fusion.2 = bf16[4,1024,128]{2,1,0:T(8,128)(2,1)} fusion(bf16[4,1024,128]{2,1,0:T(8,128)(2,1)} %pad_maximum_fusion, s32[1024]{0:T(1024)S(1)} %pad_clamp_fusion), kind=kCustom, calls=%fused_computation.clone | custom fusion | bytes 2097168 | tf_op jit(solution)/shard_map/jit(_take)/gather | solution.py:47
  114.3 2.4 %select_bitcast_fusion = bf16[1024,4,128]{2,0,1:T(8,128)(2,1)} fusion(bf16[4,1024,128]{2,1,0:T(8,128)(2,1)} %gather_fusion.2, pred[4]{0:T(512)(128)(4,1)S(1)} %compare_and_fusion), kind=kLoop, calls=%fused_computation.40 | loop fusion | flops 524288 | bytes 2097156 | tf_op jit(solution)/shard_map/transpose | solution.py:190
  116.6 2.3 %copy.133 = bf16[1024,4,128]{0,2,1:T(8,128)(2,1)} copy(bf16[1024,4,128]{2,0,1:T(8,128)(2,1)} %select_bitcast_fusion) | data formatting | bytes 2097152 | tf_op jit(solution)/shard_map/transpose | solution.py:190
  121.8 3.6 %fusion.83 = (f32[2,16,4]{1,2,0:T(4,128)S(1)}, f32[2,16,4,1024]{3,1,2,0:T(8,128)S(1)}) fusion(bf16[2,128,4,8,256]{4,3,2,1,0:T(8,128)(2,1)} %bitcast.202, bf16[2,16,4,64]{3,1,2,0:T(8,128)(2,1)S(1)} %copy.146, pred[2,1024]{1,0:T(4,128)(4,1)S(1)} %iota_compare_fusion.1, bf16[2,16,4,192]{3,1,0,2:T(8,128)(2,1)S(1)} %bitcast.215), kind=kOutput, calls=%fused_computation.175 | convolution fusion | flops 67633024 | bytes 4786688 | tf_op jit(solution)/shard_map/gqhd,gjhd->gqhj/dot_general | solution.py:137
  130.1 3.2 %fusion.17 = bf16[1024,512]{0,1:T(8,128)(2,1)S(1)} fusion(bf16[1024,512]{0,1:T(8,128)(2,1)S(1)} %bitcast.212, bf16[1024,1024]{1,0:T(8,128)(2,1)} %all-gather.4.cloned.1.call-done, f32[1024]{0:T(1024)S(1)} %get-tuple-element.47, f32[1024]{0:T(1024)S(1)} %get-tuple-element.48, f32[1024]{0:T(1024)S(1)} %bitcast.244, f32[1024]{0:T(1024)S(1)} %bitcast.243), kind=kOutput, calls=%fused_computation.31 | convolution fusion | flops 1080557568 | bytes 4210688 | tf_op jit(solution)/shard_map/dot_general | solution.py:191
  133.5 3.6 %collective-permute-start.7 = (bf16[1024,128]{0,1:T(8,128)(2,1)S(1)}, bf16[1024,128]{0,1:T(8,128)(2,1)S(1)}, u32[]{:S(2)}, u32[]{:S(2)}) collective-permute-start(bf16[1024,128]{0,1:T(8,128)(2,1)S(1)} %get-tuple-element.15), channel_id=1, source_target_pairs={{0,2},{1,3},{2,0},{3,1},{4,6},{5,7},{6,4},{7,5},{8,10},{9,11},{10,... | collective-permute-start | bytes 786440 | tf_op jit(solution)/shard_map/ppermute | solution.py:44
  138.2 4.2 %collective-permute-done.6 = bf16[1024,128]{0,1:T(8,128)(2,1)S(1)} collective-permute-done((bf16[1024,128]{0,1:T(8,128)(2,1)S(1)}, bf16[1024,128]{0,1:T(8,128)(2,1)S(1)}, u32[]{:S(2)}, u32[]{:S(2)}) %collective-permute-start.6) | collective-permute-done | bytes 262176 | tf_op jit(solution)/shard_map/ppermute | solution.py:44
  143.7 5.3 %collective-permute-done.7 = bf16[1024,128]{0,1:T(8,128)(2,1)S(1)} collective-permute-done((bf16[1024,128]{0,1:T(8,128)(2,1)S(1)}, bf16[1024,128]{0,1:T(8,128)(2,1)S(1)}, u32[]{:S(2)}, u32[]{:S(2)}) %collective-permute-start.7) | collective-permute-done | bytes 262176 | tf_op jit(solution)/shard_map/ppermute | solution.py:44
  151.8 2.9 %fusion.27 = f32[2,16,4,256]{3,1,2,0:T(8,128)S(1)} fusion(bf16[2,128,4,8,256]{4,3,2,1,0:T(8,128)(2,1)} %bitcast.204, f32[2,16,4,1024]{3,1,2,0:T(8,128)S(1)} %get-tuple-element.46, f32[2,16,4]{1,2,0:T(4,128)S(1)} %copy.153), kind=kOutput, calls=%fused_computation.35 | convolution fusion | flops 67371008 | bytes 4850176 | tf_op jit(solution)/shard_map/gqhj,gjhd->gqhd/dot_general | solution.py:163
  156.1 5.4 %all-to-all-start.2 = ((bf16[32,2,512]{2,1,0:T(2,128)(2,1)}), bf16[32,2,512]{2,1,0:T(2,128)(2,1)S(1)}, u32[]{:S(2)}, u32[]{:S(2)}) async-start(bf16[32,2,512]{2,1,0:T(2,128)(2,1)} %reshape.448), calls=%async_computation.2 | async-start | bytes 131072 | tf_op jit(solution)/shard_map/all_to_all | solution.py:178
  163.4 5.4 %all-to-all-done.2 = bf16[32,2,512]{2,1,0:T(2,128)(2,1)S(1)} async-done(((bf16[32,2,512]{2,1,0:T(2,128)(2,1)}), bf16[32,2,512]{2,1,0:T(2,128)(2,1)S(1)}, u32[]{:S(2)}, u32[]{:S(2)}) %all-to-all-start.2) | async-done | bytes 65568 | tf_op jit(solution)/shard_map/all_to_all | solution.py:178
  169.4 2.7 %collective-permute-start.14 = (bf16[8,4,1024]{2,0,1:T(8,128)(2,1)S(1)}, bf16[8,4,1024]{2,0,1:T(8,128)(2,1)S(1)}, u32[]{:S(2)}, u32[]{:S(2)}) collective-permute-start(bf16[8,4,1024]{2,0,1:T(8,128)(2,1)S(1)} %all_to_all.37), channel_id=1, source_target_pairs={{0,2},{1,3},{2,0},{3,1},{4,6},{5,7},{6,4},{7,5},{8,10},{9,11},{10,... | collective-permute-start | bytes 196616 | tf_op jit(solution)/shard_map/ppermute | solution.py:55
  172.6 2.6 %collective-permute-done.13 = bf16[8,4,1024]{2,0,1:T(8,128)(2,1)S(1)} collective-permute-done((bf16[8,4,1024]{2,0,1:T(8,128)(2,1)S(1)}, bf16[8,4,1024]{2,0,1:T(8,128)(2,1)S(1)}, u32[]{:S(2)}, u32[]{:S(2)}) %collective-permute-start.13) | collective-permute-done | bytes 65568 | tf_op jit(solution)/shard_map/ppermute | solution.py:55
  176.8 2.5 %fusion.84 = f32[1024,1024]{1,0:T(8,128)S(1)} fusion(bf16[1024,512]{0,1:T(8,128)(2,1)} %all-gather.6.cloned.1.call-done, bf16[512,1024]{1,0:T(8,128)(2,1)S(1)} %bitcast_select_fusion), kind=kOutput, calls=%fused_computation.176 | convolution fusion | flops 1073741824 | bytes 6291456 | tf_op jit(solution)/shard_map/dot_general | solution.py:198
  181.8 2.3 %collective-permute-done.19 = bf16[1024,512]{1,0:T(8,128)(2,1)S(1)} collective-permute-done((bf16[1024,512]{1,0:T(8,128)(2,1)S(1)}, bf16[1024,512]{1,0:T(8,128)(2,1)S(1)}, u32[]{:S(2)}, u32[]{:S(2)}) %collective-permute-start.19) | collective-permute-done | bytes 1048608 | tf_op jit(solution)/shard_map/ppermute | solution.py:204
  185.4 5.4 %all-to-all-start.3 = ((bf16[32,32,512]{2,1,0:T(8,128)(2,1)}), bf16[32,32,512]{2,1,0:T(8,128)(2,1)S(1)}, u32[]{:S(2)}, u32[]{:S(2)}) async-start(bf16[32,32,512]{2,1,0:T(8,128)(2,1)} %bitcast.72), calls=%async_computation.3 | async-start | bytes 2097152 | tf_op jit(solution)/shard_map/all_to_all | solution.py:208
  190.9 17.0 %all-to-all-done.3 = bf16[32,32,512]{2,1,0:T(8,128)(2,1)S(1)} async-done(((bf16[32,32,512]{2,1,0:T(8,128)(2,1)}), bf16[32,32,512]{2,1,0:T(8,128)(2,1)S(1)}, u32[]{:S(2)}, u32[]{:S(2)}) %all-to-all-start.3) | async-done | bytes 1048608 | tf_op jit(solution)/shard_map/all_to_all | solution.py:208
  (194 shorter events, 65.1 us)
Async XLA Ops:
  6.5 7.1 %collective-permute-start = (bf16[32,1024]{1,0:T(8,128)(2,1)}, bf16[32,1024]{1,0:T(8,128)(2,1)S(1)}, u32[]{:S(2)}, u32[]{:S(2)}) collective-permute-start(bf16[32,1024]{1,0:T(8,128)(2,1)} %param.19), channel_id=1, source_target_pairs={{0,1},{1,2},{2,3},{3,0},{4,5},{5,6},{6,7},{7,4},{8,9},{9,10},{10,1... | collective-permute-start | bytes 196616 | tf_op jit(solution)/shard_map/ppermute | solution.py:55
  8.6 5.3 %collective-permute-start.1 = (bf16[32,1024]{1,0:T(8,128)(2,1)}, bf16[32,1024]{1,0:T(8,128)(2,1)S(1)}, u32[]{:S(2)}, u32[]{:S(2)}) collective-permute-start(bf16[32,1024]{1,0:T(8,128)(2,1)} %param.19), channel_id=1, source_target_pairs={{0,2},{1,3},{2,0},{3,1},{4,6},{5,7},{6,4},{7,5},{8,10},{9,11},{10,... | collective-permute-start | bytes 196616 | tf_op jit(solution)/shard_map/ppermute | solution.py:55
  11.0 3.8 %collective-permute-start.2 = (bf16[32,1024]{1,0:T(8,128)(2,1)}, bf16[32,1024]{1,0:T(8,128)(2,1)S(1)}, u32[]{:S(2)}, u32[]{:S(2)}) collective-permute-start(bf16[32,1024]{1,0:T(8,128)(2,1)} %param.19), channel_id=1, source_target_pairs={{0,3},{1,0},{2,1},{3,2},{4,7},{5,4},{6,5},{7,6},{8,11},{9,8},{10,9... | collective-permute-start | bytes 196616 | tf_op jit(solution)/shard_map/ppermute | solution.py:55
  19.7 21.5 %all-to-all-start = ((bf16[32,32,256]{2,0,1:T(8,128)(2,1)}), bf16[32,32,256]{2,0,1:T(8,128)(2,1)S(1)}, u32[]{:S(2)}, u32[]{:S(2)}) async-start(bf16[32,32,256]{2,0,1:T(8,128)(2,1)} %bitcast.38), calls=%async_computation | async-start | bytes 1048576 | tf_op jit(solution)/shard_map/all_to_all | solution.py:100
  29.8 100.3 %all-gather.4.cloned.1.call-start = ((), (), s32[]{:S(2)}) async-start(), calls=%async_computation.4 | async-start | bytes 2162688 | tf_op jit(solution)/shard_map/all_gather | solution.py:91
  44.3 74.6 %all-to-all-start.1 = ((bf16[32,32,3,512]{3,1,2,0:T(8,128)(2,1)}), bf16[32,32,3,512]{3,1,2,0:T(8,128)(2,1)S(1)}, u32[]{:S(2)}, u32[]{:S(2)}) async-start(bf16[32,32,3,512]{3,1,2,0:T(8,128)(2,1)} %copy.141), calls=%async_computation.1 | async-start | bytes 6291456 | tf_op jit(solution)/shard_map/all_to_all | solution.py:116
  48.4 128.4 %all-gather.6.cloned.1.call-start = ((), (), s32[]{:S(2)}) async-start(), calls=%async_computation.5 | async-start | bytes 1310720 | tf_op jit(solution)/shard_map/all_gather | solution.py:197
  52.5 109.0 %collective-permute-start.9 = (bf16[128,1024]{1,0:T(8,128)(2,1)}, bf16[128,1024]{1,0:T(8,128)(2,1)}, u32[]{:S(2)}, u32[]{:S(2)}) collective-permute-start(bf16[128,1024]{1,0:T(8,128)(2,1)} %bitcast.225), channel_id=1, source_target_pairs={{0,1},{1,2},{2,3},{3,0},{4,5},{5,6},{6,7},{7,4},{8,9},{9,10},{10,1... | collective-permute-start | bytes 786440 | tf_op jit(solution)/shard_map/ppermute | solution.py:44
  53.6 107.8 %collective-permute-start.10 = (bf16[128,1024]{1,0:T(8,128)(2,1)}, bf16[128,1024]{1,0:T(8,128)(2,1)}, u32[]{:S(2)}, u32[]{:S(2)}) collective-permute-start(bf16[128,1024]{1,0:T(8,128)(2,1)} %bitcast.226), channel_id=1, source_target_pairs={{0,2},{1,3},{2,0},{3,1},{4,6},{5,7},{6,4},{7,5},{8,10},{9,11},{10,... | collective-permute-start | bytes 786440 | tf_op jit(solution)/shard_map/ppermute | solution.py:44
  58.8 11.8 %collective-permute-start.16 = (bf16[8,4,1024]{2,0,1:T(8,128)(2,1)S(1)}, bf16[8,4,1024]{2,0,1:T(8,128)(2,1)S(1)}, u32[]{:S(2)}, u32[]{:S(2)}) collective-permute-start(bf16[8,4,1024]{2,0,1:T(8,128)(2,1)S(1)} %bitcast.235), channel_id=1, source_target_pairs={{0,1},{1,2},{2,3},{3,0},{4,5},{5,6},{6,7},{7,4},{8,9},{9,10},{10,1... | collective-permute-start | bytes 196616 | tf_op jit(solution)/shard_map/ppermute | solution.py:44
  58.9 12.3 %collective-permute-start.17 = (bf16[8,4,1024]{2,0,1:T(8,128)(2,1)S(1)}, bf16[8,4,1024]{2,0,1:T(8,128)(2,1)}, u32[]{:S(2)}, u32[]{:S(2)}) collective-permute-start(bf16[8,4,1024]{2,0,1:T(8,128)(2,1)S(1)} %bitcast.234), channel_id=1, source_target_pairs={{0,2},{1,3},{2,0},{3,1},{4,6},{5,7},{6,4},{7,5},{8,10},{9,11},{10,... | collective-permute-start | bytes 196616 | tf_op jit(solution)/shard_map/ppermute | solution.py:44
  60.1 13.0 %collective-permute-start.18 = (bf16[8,4,1024]{2,0,1:T(8,128)(2,1)S(1)}, bf16[8,4,1024]{2,0,1:T(8,128)(2,1)}, u32[]{:S(2)}, u32[]{:S(2)}) collective-permute-start(bf16[8,4,1024]{2,0,1:T(8,128)(2,1)S(1)} %bitcast.233), channel_id=1, source_target_pairs={{0,3},{1,0},{2,1},{3,2},{4,7},{5,4},{6,5},{7,6},{8,11},{9,8},{10,9... | collective-permute-start | bytes 196616 | tf_op jit(solution)/shard_map/ppermute | solution.py:44
  70.6 38.5 %collective-permute-start.3 = (bf16[1024,128]{1,0:T(8,128)(2,1)}, bf16[1024,128]{1,0:T(8,128)(2,1)}, u32[]{:S(2)}, u32[]{:S(2)}) collective-permute-start(bf16[1024,128]{1,0:T(8,128)(2,1)} %get-tuple-element.20), channel_id=1, source_target_pairs={{0,1},{1,2},{2,3},{3,0},{4,5},{5,6},{6,7},{7,4},{8,9},{9,10},{10,1... | collective-permute-start | bytes 786440 | tf_op jit(solution)/shard_map/ppermute | solution.py:44
  71.2 37.8 %collective-permute-start.4 = (bf16[1024,128]{1,0:T(8,128)(2,1)}, bf16[1024,128]{1,0:T(8,128)(2,1)}, u32[]{:S(2)}, u32[]{:S(2)}) collective-permute-start(bf16[1024,128]{1,0:T(8,128)(2,1)} %get-tuple-element.19), channel_id=1, source_target_pairs={{0,2},{1,3},{2,0},{3,1},{4,6},{5,7},{6,4},{7,5},{8,10},{9,11},{10,... | collective-permute-start | bytes 786440 | tf_op jit(solution)/shard_map/ppermute | solution.py:44
  73.1 36.0 %collective-permute-start.5 = (bf16[1024,128]{1,0:T(8,128)(2,1)}, bf16[1024,128]{1,0:T(8,128)(2,1)}, u32[]{:S(2)}, u32[]{:S(2)}) collective-permute-start(bf16[1024,128]{1,0:T(8,128)(2,1)} %get-tuple-element.18), channel_id=1, source_target_pairs={{0,3},{1,0},{2,1},{3,2},{4,7},{5,4},{6,5},{7,6},{8,11},{9,8},{10,9... | collective-permute-start | bytes 786440 | tf_op jit(solution)/shard_map/ppermute | solution.py:44
  133.4 9.0 %collective-permute-start.6 = (bf16[1024,128]{0,1:T(8,128)(2,1)S(1)}, bf16[1024,128]{0,1:T(8,128)(2,1)S(1)}, u32[]{:S(2)}, u32[]{:S(2)}) collective-permute-start(bf16[1024,128]{0,1:T(8,128)(2,1)S(1)} %get-tuple-element.16), channel_id=1, source_target_pairs={{0,1},{1,2},{2,3},{3,0},{4,5},{5,6},{6,7},{7,4},{8,9},{9,10},{10,1... | collective-permute-start | bytes 786440 | tf_op jit(solution)/shard_map/ppermute | solution.py:44
  133.5 15.5 %collective-permute-start.7 = (bf16[1024,128]{0,1:T(8,128)(2,1)S(1)}, bf16[1024,128]{0,1:T(8,128)(2,1)S(1)}, u32[]{:S(2)}, u32[]{:S(2)}) collective-permute-start(bf16[1024,128]{0,1:T(8,128)(2,1)S(1)} %get-tuple-element.15), channel_id=1, source_target_pairs={{0,2},{1,3},{2,0},{3,1},{4,6},{5,7},{6,4},{7,5},{8,10},{9,11},{10,... | collective-permute-start | bytes 786440 | tf_op jit(solution)/shard_map/ppermute | solution.py:44
  137.1 11.9 %collective-permute-start.8 = (bf16[1024,128]{0,1:T(8,128)(2,1)S(1)}, bf16[1024,128]{0,1:T(8,128)(2,1)S(1)}, u32[]{:S(2)}, u32[]{:S(2)}) collective-permute-start(bf16[1024,128]{0,1:T(8,128)(2,1)S(1)} %get-tuple-element.14), channel_id=1, source_target_pairs={{0,3},{1,0},{2,1},{3,2},{4,7},{5,4},{6,5},{7,6},{8,11},{9,8},{10,9... | collective-permute-start | bytes 786440 | tf_op jit(solution)/shard_map/ppermute | solution.py:44
  142.4 19.1 %collective-permute-start.11 = (bf16[128,1024]{1,0:T(8,128)(2,1)S(1)}, bf16[128,1024]{1,0:T(8,128)(2,1)S(1)}, u32[]{:S(2)}, u32[]{:S(2)}) collective-permute-start(bf16[128,1024]{1,0:T(8,128)(2,1)S(1)} %bitcast.227), channel_id=1, source_target_pairs={{0,3},{1,0},{2,1},{3,2},{4,7},{5,4},{6,5},{7,6},{8,11},{9,8},{10,9... | collective-permute-start | bytes 786440 | tf_op jit(solution)/shard_map/ppermute | solution.py:44
  156.1 12.7 %all-to-all-start.2 = ((bf16[32,2,512]{2,1,0:T(2,128)(2,1)}), bf16[32,2,512]{2,1,0:T(2,128)(2,1)S(1)}, u32[]{:S(2)}, u32[]{:S(2)}) async-start(bf16[32,2,512]{2,1,0:T(2,128)(2,1)} %reshape.448), calls=%async_computation.2 | async-start | bytes 131072 | tf_op jit(solution)/shard_map/all_to_all | solution.py:178
  169.3 5.9 %collective-permute-start.13 = (bf16[8,4,1024]{2,0,1:T(8,128)(2,1)S(1)}, bf16[8,4,1024]{2,0,1:T(8,128)(2,1)S(1)}, u32[]{:S(2)}, u32[]{:S(2)}) collective-permute-start(bf16[8,4,1024]{2,0,1:T(8,128)(2,1)S(1)} %all_to_all.37), channel_id=1, source_target_pairs={{0,1},{1,2},{2,3},{3,0},{4,5},{5,6},{6,7},{7,4},{8,9},{9,10},{10,1... | collective-permute-start | bytes 196616 | tf_op jit(solution)/shard_map/ppermute | solution.py:55
  169.4 5.8 %collective-permute-start.14 = (bf16[8,4,1024]{2,0,1:T(8,128)(2,1)S(1)}, bf16[8,4,1024]{2,0,1:T(8,128)(2,1)S(1)}, u32[]{:S(2)}, u32[]{:S(2)}) collective-permute-start(bf16[8,4,1024]{2,0,1:T(8,128)(2,1)S(1)} %all_to_all.37), channel_id=1, source_target_pairs={{0,2},{1,3},{2,0},{3,1},{4,6},{5,7},{6,4},{7,5},{8,10},{9,11},{10,... | collective-permute-start | bytes 196616 | tf_op jit(solution)/shard_map/ppermute | solution.py:55
  172.1 3.9 %collective-permute-start.15 = (bf16[8,4,1024]{2,0,1:T(8,128)(2,1)S(1)}, bf16[8,4,1024]{2,0,1:T(8,128)(2,1)S(1)}, u32[]{:S(2)}, u32[]{:S(2)}) collective-permute-start(bf16[8,4,1024]{2,0,1:T(8,128)(2,1)S(1)} %all_to_all.37), channel_id=1, source_target_pairs={{0,3},{1,0},{2,1},{3,2},{4,7},{5,4},{6,5},{7,6},{8,11},{9,8},{10,9... | collective-permute-start | bytes 196616 | tf_op jit(solution)/shard_map/ppermute | solution.py:55
  185.4 22.5 %all-to-all-start.3 = ((bf16[32,32,512]{2,1,0:T(8,128)(2,1)}), bf16[32,32,512]{2,1,0:T(8,128)(2,1)S(1)}, u32[]{:S(2)}, u32[]{:S(2)}) async-start(bf16[32,32,512]{2,1,0:T(8,128)(2,1)} %bitcast.72), calls=%async_computation.3 | async-start | bytes 2097152 | tf_op jit(solution)/shard_map/all_to_all | solution.py:208
  (22 other events, 253.0 us)
Sparse Core Ops, SparseCore 0:
  32.9 64.1 all-gather.3
  151.9 19.7 all-gather.5

commit v9 on v7

--- a/solution.py
+++ b/solution.py
@@ -82,12 +82,20 @@
     local_rows = normed.shape[0]
     groups_here = prompt_len.shape[0]
     quarter = lax.dynamic_slice_in_dim(normed, lax.axis_index("head") * width_here, width_here, axis=1)
-    gathered = lax.all_gather(quarter, "grp", axis=0, tiled=True)
     block = w_qkv.shape[0]
     pair_rows = normed.reshape(local_rows, grp_count // 2, 2 * block)
-    columns = lax.all_to_all(
-        jnp.repeat(pair_rows, 2, axis=1), "grp", split_axis=1, concat_axis=0, tiled=True
-    ).reshape(grp_count * local_rows, 2 * block)
+    outgoing = jnp.concatenate(
+        [
+            jnp.repeat(pair_rows, 2, axis=1),
+            jnp.broadcast_to(quarter[:, None, :], (local_rows, grp_count, width_here)),
+        ],
+        axis=2,
+    )
+    incoming = lax.all_to_all(outgoing, "grp", split_axis=1, concat_axis=0, tiled=True).reshape(
+        grp_count * local_rows, 2 * block + width_here
+    )
+    columns = incoming[:, : 2 * block]
+    gathered = incoming[:, 2 * block :]
     parity = lax.axis_index("grp") % 2
     half = w_qkv.shape[2] // 2
     own = lax.dynamic_slice_in_dim(w_qkv, parity * half, half, axis=2)
@@ -182,7 +190,7 @@
         jnp.sum(partial.astype(jnp.float32), axis=0) + b_in.astype(jnp.float32),
         approximate=True,
     ).astype(jnp.bfloat16)
-    hidden = lax.all_gather(hidden, "head", axis=1, tiled=True)
+    hidden = jnp.moveaxis(head_gather(hidden), 0, 1).reshape(hidden.shape[0], -1)
     mlp_part = jnp.dot(hidden, down_blocks, preferred_element_type=jnp.float32)
     attn_part = jnp.einsum("dkr,dkf->rf", slices, out_blocks, preferred_element_type=jnp.float32)
     combined = mlp_part + attn_part

time: 204 us -> 200 us (0.980)
  between operations: 14.3 us -> 0.81 us
  matrix products: 17.1 us -> 22.2 us
  starting transfers between devices: 54.6 us -> 59.1 us
  waiting for transfers between devices: 54.1 us -> 49.7 us
  other arithmetic: 24.8 us -> 27.5 us
    all_to_all x1, waiting for transfers between devices: 9.53 us -> 21.8 us  [local(): lax.all_to_all(outgoing, 'grp', split_axis=1, concat_axis=0, tiled=True)]
    ppermute x12, waiting for transfers between devices: 9.58 us -> 3.31 us  [head_exchange(): lax.ppermute(piece, 'head', [(i, (i + shift) % count) for i in range(coun...]
    all_gather x2 -> x0, waiting for transfers between devices: 5.96 us -> none  [the longest x1 5.94 us: local(): gathered = lax.all_gather(quarter, 'grp', axis=0, tiled=True)]
    gather x4, local copies, waits for them, and re-layouts: 5.62 us -> 10.3 us  [head_exchange(): return jnp.take(stacked, (here - jnp.arange(count)) % count, axis=0)]
    dynamic_slice x7, local copies, waits for them, and re-layouts: 11.9 us -> 7.48 us  [head_exchange(): lax.dynamic_index_in_dim(pieces, (here + shift) % count, axis, keepdims=F...]
    all_to_all x1, starting transfers between devices: 6.81 us -> 11.1 us  [local(): lax.all_to_all(transposed, 'grp', split_axis=0, concat_axis=2, tiled=True)]
    another operation x4, other arithmetic: 4.49 us -> 7.91 us  [head_exchange(): stacked = jnp.stack(received, axis=0)]
    ppermute x6 -> x9, waiting for transfers between devices: 2.84 us -> 0.02 us  [head_gather(): lax.ppermute(piece, 'head', [(i, (i + shift) % count) for i in range(coun...]
  transfers between devices with their start and end apart: 26 -> 27, of which waited for: 14 -> 5; matrix products, arithmetic and copies ran while one was open for 32% -> 39% of each run, Pallas kernels for 0% -> 0%
where the time goes in v9:
time: 200 us; the launch traced here: 199 us
  starting transfers between devices  59.1 us (30%)
  waiting for transfers between devices  49.7 us (25%)
  local copies, waits for them, and re-layouts  39.2 us (20%)
  other arithmetic  27.5 us (14%)
  matrix products  22.2 us (11%)
    all_to_all x1, waiting for transfers between devices, local(): lax.all_to_all(outgoing, 'grp', split_axis=1, concat_axis=0, tiled=True)  21.8 us
    all_to_all x1, waiting for transfers between devices, local(): lax.all_to_all(pair_sum.reshape(grp_count, local_rows, half_width), 'grp'...  17.1 us
    ppermute x12, starting transfers between devices, head_exchange(): lax.ppermute(piece, 'head', [(i, (i + shift) % count) for i in range(coun...  13.9 us
    ppermute x9, starting transfers between devices, head_gather(): lax.ppermute(piece, 'head', [(i, (i + shift) % count) for i in range(coun...  12 us
    all_to_all x1, starting transfers between devices, local(): lax.all_to_all(transposed, 'grp', split_axis=0, concat_axis=2, tiled=True)  11.1 us
    gather x4, local copies, waits for them, and re-layouts, head_exchange(): return jnp.take(stacked, (here - jnp.arange(count)) % count, axis=0)  10.3 us
    all_to_all x1, starting transfers between devices, local(): lax.all_to_all(outgoing, 'grp', split_axis=1, concat_axis=0, tiled=True)  9.96 us
    another operation x4, other arithmetic, head_exchange(): stacked = jnp.stack(received, axis=0)  7.91 us
  transfers between devices with their start and end apart: 27, of which 5 were waited for; matrix products, arithmetic and copies ran while one was open for 39% of the time, Pallas kernels for 0%

profile of v9, /device:TPU:1, one launch (start us, length us, event | category | flops | bytes accessed | tf_op | source)
XLA Modules:
  0.0 198.5 jit_solution(5905626774490545957)
XLA Ops:
  2.0 2.5 %collective-permute-start.1 = (bf16[32,1024]{1,0:T(8,128)(2,1)}, bf16[32,1024]{1,0:T(8,128)(2,1)S(1)}, u32[]{:S(2)}, u32[]{:S(2)}) collective-permute-start(bf16[32,1024]{1,0:T(8,128)(2,1)} %param.19), channel_id=1, source_target_pairs={{0,2},{1,3},{2,0},{3,1},{4,6},{5,7},{6,4},{7,5},{8,10},{9,11},{10,... | collective-permute-start | bytes 196616 | tf_op jit(solution)/shard_map/ppermute | solution.py:55
  13.8 10.0 %all-to-all-start = ((bf16[32,32,1280]{2,0,1:T(8,128)(2,1)}), bf16[32,32,1280]{2,0,1:T(8,128)(2,1)}, u32[]{:S(2)}, u32[]{:S(2)}) async-start(bf16[32,32,1280]{2,0,1:T(8,128)(2,1)} %pad_maximum_fusion), calls=%async_computation | async-start | bytes 5242880 | tf_op jit(solution)/shard_map/all_to_all | solution.py:94
  26.3 3.3 %collective-permute-start.4 = (bf16[1024,128]{1,0:T(8,128)(2,1)}, bf16[1024,128]{1,0:T(8,128)(2,1)}, u32[]{:S(2)}, u32[]{:S(2)}) collective-permute-start(bf16[1024,128]{1,0:T(8,128)(2,1)} %get-tuple-element.19), channel_id=1, source_target_pairs={{0,2},{1,3},{2,0},{3,1},{4,6},{5,7},{6,4},{7,5},{8,10},{9,11},{10,... | collective-permute-start | bytes 786440 | tf_op jit(solution)/shard_map/ppermute | solution.py:44
  36.0 21.8 %all-to-all-done = bf16[32,32,1280]{2,0,1:T(8,128)(2,1)} async-done(((bf16[32,32,1280]{2,0,1:T(8,128)(2,1)}), bf16[32,32,1280]{2,0,1:T(8,128)(2,1)}, u32[]{:S(2)}, u32[]{:S(2)}) %all-to-all-start) | async-done | bytes 2621472 | tf_op jit(solution)/shard_map/all_to_all | solution.py:94
  61.8 6.3 %all-to-all-start.1 = ((bf16[32,32,3,512]{3,1,2,0:T(8,128)(2,1)}), bf16[32,32,3,512]{3,1,2,0:T(8,128)(2,1)S(1)}, u32[]{:S(2)}, u32[]{:S(2)}) async-start(bf16[32,32,3,512]{3,1,2,0:T(8,128)(2,1)} %copy.144), calls=%async_computation.1 | async-start | bytes 6291456 | tf_op jit(solution)/shard_map/all_to_all | solution.py:112
  78.9 3.3 %collective-permute-start.20 = (bf16[8,4,1024]{2,0,1:T(8,128)(2,1)}, bf16[8,4,1024]{2,0,1:T(8,128)(2,1)}, u32[]{:S(2)}, u32[]{:S(2)}) collective-permute-start(bf16[8,4,1024]{2,0,1:T(8,128)(2,1)} %bitcast.197), channel_id=1, source_target_pairs={{0,2},{1,3},{2,0},{3,1},{4,6},{5,7},{6,4},{7,5},{8,10},{9,11},{10,... | collective-permute-start | bytes 196616 | tf_op jit(solution)/shard_map/ppermute | solution.py:44
  82.1 2.3 %pad_maximum_fusion.1 = bf16[4,1024,128]{2,1,0:T(8,128)(2,1)} fusion(bf16[1,1024,128]{2,1,0:T(8,128)(2,1)} %bitcast.16, bf16[1,1024,128]{2,1,0:T(8,128)(2,1)} %bitcast.14, bf16[1,1024,128]{2,1,0:T(8,128)(2,1)} %bitcast.12, bf16[1,1024,128]{2,1,0:T(8,128)(2,1)} %get-tuple-element.17), kind=kLoop, calls=%fused_computation.34 | loop fusion | flops 1572864 | bytes 2097152 | tf_op jit(solution)/shard_map/stack | solution.py:46
  84.5 3.0 %gather_fusion.2 = bf16[4,1024,128]{2,1,0:T(8,128)(2,1)} fusion(bf16[4,1024,128]{2,1,0:T(8,128)(2,1)} %pad_maximum_fusion.1, s32[1024]{0:T(1024)} %pad_clamp_fusion), kind=kCustom, calls=%fused_computation.clone | custom fusion | bytes 2097168 | tf_op jit(solution)/shard_map/jit(_take)/gather | solution.py:47
  87.5 2.4 %select_bitcast_fusion = bf16[1024,4,128]{2,0,1:T(8,128)(2,1)} fusion(bf16[4,1024,128]{2,1,0:T(8,128)(2,1)} %gather_fusion.2, pred[4]{0:T(512)(128)(4,1)} %copy-done.12), kind=kLoop, calls=%fused_computation.41 | loop fusion | flops 524288 | bytes 2097156 | tf_op jit(solution)/shard_map/transpose | solution.py:186
  92.1 3.2 %fusion.14 = bf16[1024,512]{0,1:T(8,128)(2,1)S(1)} fusion(bf16[1024,512]{0,1:T(8,128)(2,1)} %bitcast.212, bf16[1024,1280]{1,0:T(8,128)(2,1)} %bitcast.9), kind=kOutput, calls=%fused_computation.29 | convolution fusion | flops 1074266112 | bytes 4194304 | tf_op jit(solution)/shard_map/dot_general | solution.py:187
  106.2 2.4 %pad_maximum_fusion.4 = bf16[4,128,1024]{2,1,0:T(8,128)(2,1)} fusion(bf16[1,128,1024]{2,1,0:T(8,128)(2,1)} %bitcast.39, bf16[1,128,1024]{2,1,0:T(8,128)(2,1)} %bitcast.37, bf16[1,128,1024]{2,1,0:T(8,128)(2,1)} %bitcast.35, bf16[1,128,1024]{2,1,0:T(8,128)(2,1)} %bitcast.214), kind=kLoop, calls=%fused_computation.37 | loop fusion | flops 1572864 | bytes 2097152 | tf_op jit(solution)/shard_map/stack | solution.py:46
  108.6 2.9 %gather_fusion.1 = bf16[4,128,1024]{2,1,0:T(8,128)(2,1)} fusion(bf16[4,128,1024]{2,1,0:T(8,128)(2,1)} %pad_maximum_fusion.4, s32[1024]{0:T(1024)} %copy-done.14), kind=kCustom, calls=%fused_computation.6 | custom fusion | bytes 2097168 | tf_op jit(solution)/shard_map/jit(_take)/gather | solution.py:47
  111.5 3.3 %collective-permute-done.8 = bf16[1024,128]{0,1:T(8,128)(2,1)} collective-permute-done((bf16[1024,128]{0,1:T(8,128)(2,1)}, bf16[1024,128]{0,1:T(8,128)(2,1)}, u32[]{:S(2)}, u32[]{:S(2)}) %collective-permute-start.8) | collective-permute-done | bytes 262176 | tf_op jit(solution)/shard_map/ppermute | solution.py:44
  117.1 3.0 %gather_fusion.3 = bf16[4,1024,128]{1,2,0:T(8,128)(2,1)} fusion(bf16[4,1024,128]{1,2,0:T(8,128)(2,1)} %pad_maximum_fusion.2, s32[1024]{0:T(1024)} %pad_clamp_fusion), kind=kCustom, calls=%fused_computation.2.clone | custom fusion | bytes 2097168 | tf_op jit(solution)/shard_map/jit(_take)/gather | solution.py:47
  123.8 2.3 %collective-permute-start.10 = (bf16[1024,128]{0,1:T(8,128)(2,1)}, bf16[1024,128]{0,1:T(8,128)(2,1)}, u32[]{:S(2)}, u32[]{:S(2)}) collective-permute-start(bf16[1024,128]{0,1:T(8,128)(2,1)} %fusion.56), channel_id=1, source_target_pairs={{0,2},{1,3},{2,0},{3,1},{4,6},{5,7},{6,4},{7,5},{8,10},{9,11},{10,... | collective-permute-start | bytes 786440 | tf_op jit(solution)/shard_map/ppermute | solution.py:55
  129.3 3.5 %fusion.100 = (f32[2,16,4]{1,2,0:T(4,128)S(1)}, f32[2,16,4,1024]{3,1,2,0:T(8,128)S(1)}) fusion(bf16[2,128,4,8,256]{4,3,2,1,0:T(8,128)(2,1)} %bitcast.201, bf16[2,16,4,64]{3,1,2,0:T(8,128)(2,1)S(1)} %copy.149, pred[2,1024]{1,0:T(4,128)(4,1)S(1)} %copy-done.11, bf16[2,16,4,192]{3,1,0,2:T(8,128)(2,1)S(1)} %bitcast.216), kind=kOutput, calls=%fused_computation.192 | convolution fusion | flops 67633024 | bytes 4786688 | tf_op jit(solution)/shard_map/gqhd,gjhd->gqhj/dot_general | solution.py:133
  135.9 2.9 %fusion.26 = f32[2,16,4,256]{3,1,2,0:T(8,128)S(1)} fusion(bf16[2,128,4,8,256]{4,3,2,1,0:T(8,128)(2,1)} %bitcast.203, f32[2,16,4,1024]{3,1,2,0:T(8,128)S(1)} %get-tuple-element.42, f32[2,16,4]{1,2,0:T(4,128)S(1)} %copy.156), kind=kOutput, calls=%fused_computation.33 | convolution fusion | flops 67371008 | bytes 4850176 | tf_op jit(solution)/shard_map/gqhj,gjhd->gqhd/dot_general | solution.py:159
  142.0 11.1 %all-to-all-start.2 = ((bf16[32,2,512]{2,1,0:T(2,128)(2,1)}), bf16[32,2,512]{2,1,0:T(2,128)(2,1)S(1)}, u32[]{:S(2)}, u32[]{:S(2)}) async-start(bf16[32,2,512]{2,1,0:T(2,128)(2,1)} %reshape.494), calls=%async_computation.2 | async-start | bytes 131072 | tf_op jit(solution)/shard_map/all_to_all | solution.py:174
  155.3 5.2 %all-to-all-done.2 = bf16[32,2,512]{2,1,0:T(2,128)(2,1)S(1)} async-done(((bf16[32,2,512]{2,1,0:T(2,128)(2,1)}), bf16[32,2,512]{2,1,0:T(2,128)(2,1)S(1)}, u32[]{:S(2)}, u32[]{:S(2)}) %all-to-all-start.2) | async-done | bytes 65568 | tf_op jit(solution)/shard_map/all_to_all | solution.py:174
  161.1 2.3 %collective-permute-start.17 = (bf16[8,4,1024]{2,0,1:T(8,128)(2,1)S(1)}, bf16[8,4,1024]{2,0,1:T(8,128)(2,1)S(1)}, u32[]{:S(2)}, u32[]{:S(2)}) collective-permute-start(bf16[8,4,1024]{2,0,1:T(8,128)(2,1)S(1)} %all_to_all.37), channel_id=1, source_target_pairs={{0,2},{1,3},{2,0},{3,1},{4,6},{5,7},{6,4},{7,5},{8,10},{9,11},{10,... | collective-permute-start | bytes 196616 | tf_op jit(solution)/shard_map/ppermute | solution.py:55
  163.8 3.3 %fusion.29 = f32[1024,1024,1]{1,0,2:T(8,128)} fusion(bf16[4,1024,128]{1,2,0:T(8,128)(2,1)S(1)} %gather_fusion.4, bf16[4,128,1024]{2,1,0:T(8,128)(2,1)S(1)} %copy-done.1, pred[4]{0:T(512)(128)(4,1)S(1)} %copy-done.13), kind=kOutput, calls=%fused_computation.38 | convolution fusion | flops 1074790400 | bytes 6291460 | tf_op jit(solution)/shard_map/dot_general | solution.py:194
  168.2 3.0 %bitcast_add_fusion = f32[1024,1024]{1,0:T(8,128)S(1)} fusion(f32[1024,1024,1]{1,0,2:T(8,128)} %fusion.29, bf16[4,8,4,1024]{3,1,2,0:T(8,128)(2,1)S(1)} %copy-done.6, bf16[4,8,4,1024]{3,1,2,0:T(8,128)(2,1)S(1)} %gather_fusion.5, pred[4]{0:T(512)(128)(4,1)S(1)} %copy-done.13), kind=kOutput, calls=%fused_computation.14 | convolution fusion | flops 269746176 | bytes 8912900 | tf_op jit(solution)/shard_map/dkr,dkf->rf/dot_general | solution.py:195
  176.5 4.1 %all-to-all-start.3 = ((bf16[32,32,512]{2,1,0:T(8,128)(2,1)}), bf16[32,32,512]{2,1,0:T(8,128)(2,1)S(1)}, u32[]{:S(2)}, u32[]{:S(2)}) async-start(bf16[32,32,512]{2,1,0:T(8,128)(2,1)} %bitcast.73), calls=%async_computation.3 | async-start | bytes 2097152 | tf_op jit(solution)/shard_map/all_to_all | solution.py:204
  180.6 17.1 %all-to-all-done.3 = bf16[32,32,512]{2,1,0:T(8,128)(2,1)S(1)} async-done(((bf16[32,32,512]{2,1,0:T(8,128)(2,1)}), bf16[32,32,512]{2,1,0:T(8,128)(2,1)S(1)}, u32[]{:S(2)}, u32[]{:S(2)}) %all-to-all-start.3) | async-done | bytes 1048608 | tf_op jit(solution)/shard_map/all_to_all | solution.py:204
  (197 shorter events, 73.5 us)
Async XLA Ops:
  0.0 8.5 %collective-permute-start = (bf16[32,1024]{1,0:T(8,128)(2,1)}, bf16[32,1024]{1,0:T(8,128)(2,1)S(1)}, u32[]{:S(2)}, u32[]{:S(2)}) collective-permute-start(bf16[32,1024]{1,0:T(8,128)(2,1)} %param.19), channel_id=1, source_target_pairs={{0,1},{1,2},{2,3},{3,0},{4,5},{5,6},{6,7},{7,4},{8,9},{9,10},{10,1... | collective-permute-start | bytes 196616 | tf_op jit(solution)/shard_map/ppermute | solution.py:55
  2.0 6.5 %collective-permute-start.1 = (bf16[32,1024]{1,0:T(8,128)(2,1)}, bf16[32,1024]{1,0:T(8,128)(2,1)S(1)}, u32[]{:S(2)}, u32[]{:S(2)}) collective-permute-start(bf16[32,1024]{1,0:T(8,128)(2,1)} %param.19), channel_id=1, source_target_pairs={{0,2},{1,3},{2,0},{3,1},{4,6},{5,7},{6,4},{7,5},{8,10},{9,11},{10,... | collective-permute-start | bytes 196616 | tf_op jit(solution)/shard_map/ppermute | solution.py:55
  13.8 44.0 %all-to-all-start = ((bf16[32,32,1280]{2,0,1:T(8,128)(2,1)}), bf16[32,32,1280]{2,0,1:T(8,128)(2,1)}, u32[]{:S(2)}, u32[]{:S(2)}) async-start(bf16[32,32,1280]{2,0,1:T(8,128)(2,1)} %pad_maximum_fusion), calls=%async_computation | async-start | bytes 5242880 | tf_op jit(solution)/shard_map/all_to_all | solution.py:94
  24.7 11.2 %collective-permute-start.15 = (bf16[128,3,512]{2,0,1:T(8,128)(2,1)}, bf16[128,3,512]{2,0,1:T(8,128)(2,1)S(1)}, u32[]{:S(2)}, u32[]{:S(2)}) collective-permute-start(bf16[128,3,512]{2,0,1:T(8,128)(2,1)} %get-tuple-element.22), channel_id=1, source_target_pairs={{0,4},{4,0},{8,12},{12,8},{16,20},{20,16},{24,28},{28,24},{32,36},... | collective-permute-start | bytes 1179656 | tf_op jit(solution)/shard_map/ppermute | solution.py:103
  26.0 52.5 %collective-permute-start.3 = (bf16[1024,128]{1,0:T(8,128)(2,1)}, bf16[1024,128]{1,0:T(8,128)(2,1)}, u32[]{:S(2)}, u32[]{:S(2)}) collective-permute-start(bf16[1024,128]{1,0:T(8,128)(2,1)} %get-tuple-element.20), channel_id=1, source_target_pairs={{0,1},{1,2},{2,3},{3,0},{4,5},{5,6},{6,7},{7,4},{8,9},{9,10},{10,1... | collective-permute-start | bytes 786440 | tf_op jit(solution)/shard_map/ppermute | solution.py:44
  26.3 52.5 %collective-permute-start.4 = (bf16[1024,128]{1,0:T(8,128)(2,1)}, bf16[1024,128]{1,0:T(8,128)(2,1)}, u32[]{:S(2)}, u32[]{:S(2)}) collective-permute-start(bf16[1024,128]{1,0:T(8,128)(2,1)} %get-tuple-element.19), channel_id=1, source_target_pairs={{0,2},{1,3},{2,0},{3,1},{4,6},{5,7},{6,4},{7,5},{8,10},{9,11},{10,... | collective-permute-start | bytes 786440 | tf_op jit(solution)/shard_map/ppermute | solution.py:44
  29.6 52.5 %collective-permute-start.5 = (bf16[1024,128]{1,0:T(8,128)(2,1)}, bf16[1024,128]{1,0:T(8,128)(2,1)}, u32[]{:S(2)}, u32[]{:S(2)}) collective-permute-start(bf16[1024,128]{1,0:T(8,128)(2,1)} %get-tuple-element.18), channel_id=1, source_target_pairs={{0,3},{1,0},{2,1},{3,2},{4,7},{5,4},{6,5},{7,6},{8,11},{9,8},{10,9... | collective-permute-start | bytes 786440 | tf_op jit(solution)/shard_map/ppermute | solution.py:44
  32.0 67.7 %collective-permute-start.12 = (bf16[128,1024]{1,0:T(8,128)(2,1)}, bf16[128,1024]{1,0:T(8,128)(2,1)}, u32[]{:S(2)}, u32[]{:S(2)}) collective-permute-start(bf16[128,1024]{1,0:T(8,128)(2,1)} %bitcast.34), channel_id=1, source_target_pairs={{0,1},{1,2},{2,3},{3,0},{4,5},{5,6},{6,7},{7,4},{8,9},{9,10},{10,1... | collective-permute-start | bytes 786440 | tf_op jit(solution)/shard_map/ppermute | solution.py:44
  35.9 70.3 %collective-permute-start.13 = (bf16[128,1024]{1,0:T(8,128)(2,1)}, bf16[128,1024]{1,0:T(8,128)(2,1)}, u32[]{:S(2)}, u32[]{:S(2)}) collective-permute-start(bf16[128,1024]{1,0:T(8,128)(2,1)} %bitcast.36), channel_id=1, source_target_pairs={{0,2},{1,3},{2,0},{3,1},{4,6},{5,7},{6,4},{7,5},{8,10},{9,11},{10,... | collective-permute-start | bytes 786440 | tf_op jit(solution)/shard_map/ppermute | solution.py:44
  61.8 64.6 %all-to-all-start.1 = ((bf16[32,32,3,512]{3,1,2,0:T(8,128)(2,1)}), bf16[32,32,3,512]{3,1,2,0:T(8,128)(2,1)S(1)}, u32[]{:S(2)}, u32[]{:S(2)}) async-start(bf16[32,32,3,512]{3,1,2,0:T(8,128)(2,1)} %copy.144), calls=%async_computation.1 | async-start | bytes 6291456 | tf_op jit(solution)/shard_map/all_to_all | solution.py:112
  78.6 17.8 %collective-permute-start.19 = (bf16[8,4,1024]{2,0,1:T(8,128)(2,1)}, bf16[8,4,1024]{2,0,1:T(8,128)(2,1)}, u32[]{:S(2)}, u32[]{:S(2)}) collective-permute-start(bf16[8,4,1024]{2,0,1:T(8,128)(2,1)} %bitcast.198), channel_id=1, source_target_pairs={{0,1},{1,2},{2,3},{3,0},{4,5},{5,6},{6,7},{7,4},{8,9},{9,10},{10,1... | collective-permute-start | bytes 196616 | tf_op jit(solution)/shard_map/ppermute | solution.py:44
  78.9 18.0 %collective-permute-start.20 = (bf16[8,4,1024]{2,0,1:T(8,128)(2,1)}, bf16[8,4,1024]{2,0,1:T(8,128)(2,1)}, u32[]{:S(2)}, u32[]{:S(2)}) collective-permute-start(bf16[8,4,1024]{2,0,1:T(8,128)(2,1)} %bitcast.197), channel_id=1, source_target_pairs={{0,2},{1,3},{2,0},{3,1},{4,6},{5,7},{6,4},{7,5},{8,10},{9,11},{10,... | collective-permute-start | bytes 196616 | tf_op jit(solution)/shard_map/ppermute | solution.py:44
  82.1 15.7 %collective-permute-start.21 = (bf16[8,4,1024]{2,0,1:T(8,128)(2,1)}, bf16[8,4,1024]{2,0,1:T(8,128)(2,1)}, u32[]{:S(2)}, u32[]{:S(2)}) collective-permute-start(bf16[8,4,1024]{2,0,1:T(8,128)(2,1)} %bitcast.196), channel_id=1, source_target_pairs={{0,3},{1,0},{2,1},{3,2},{4,7},{5,4},{6,5},{7,6},{8,11},{9,8},{10,9... | collective-permute-start | bytes 196616 | tf_op jit(solution)/shard_map/ppermute | solution.py:44
  96.3 9.9 %collective-permute-start.14 = (bf16[128,1024]{1,0:T(8,128)(2,1)}, bf16[128,1024]{1,0:T(8,128)(2,1)}, u32[]{:S(2)}, u32[]{:S(2)}) collective-permute-start(bf16[128,1024]{1,0:T(8,128)(2,1)} %bitcast.38), channel_id=1, source_target_pairs={{0,3},{1,0},{2,1},{3,2},{4,7},{5,4},{6,5},{7,6},{8,11},{9,8},{10,9... | collective-permute-start | bytes 786440 | tf_op jit(solution)/shard_map/ppermute | solution.py:44
  96.9 14.6 %collective-permute-start.6 = (bf16[1024,128]{0,1:T(8,128)(2,1)}, bf16[1024,128]{0,1:T(8,128)(2,1)}, u32[]{:S(2)}, u32[]{:S(2)}) collective-permute-start(bf16[1024,128]{0,1:T(8,128)(2,1)} %get-tuple-element.16), channel_id=1, source_target_pairs={{0,1},{1,2},{2,3},{3,0},{4,5},{5,6},{6,7},{7,4},{8,9},{9,10},{10,1... | collective-permute-start | bytes 786440 | tf_op jit(solution)/shard_map/ppermute | solution.py:44
  97.9 13.6 %collective-permute-start.7 = (bf16[1024,128]{0,1:T(8,128)(2,1)}, bf16[1024,128]{0,1:T(8,128)(2,1)}, u32[]{:S(2)}, u32[]{:S(2)}) collective-permute-start(bf16[1024,128]{0,1:T(8,128)(2,1)} %get-tuple-element.15), channel_id=1, source_target_pairs={{0,2},{1,3},{2,0},{3,1},{4,6},{5,7},{6,4},{7,5},{8,10},{9,11},{10,... | collective-permute-start | bytes 786440 | tf_op jit(solution)/shard_map/ppermute | solution.py:44
  99.7 15.1 %collective-permute-start.8 = (bf16[1024,128]{0,1:T(8,128)(2,1)}, bf16[1024,128]{0,1:T(8,128)(2,1)}, u32[]{:S(2)}, u32[]{:S(2)}) collective-permute-start(bf16[1024,128]{0,1:T(8,128)(2,1)} %get-tuple-element.14), channel_id=1, source_target_pairs={{0,3},{1,0},{2,1},{3,2},{4,7},{5,4},{6,5},{7,6},{8,11},{9,8},{10,9... | collective-permute-start | bytes 786440 | tf_op jit(solution)/shard_map/ppermute | solution.py:44
  122.6 30.6 %collective-permute-start.9 = (bf16[1024,128]{0,1:T(8,128)(2,1)}, bf16[1024,128]{0,1:T(8,128)(2,1)}, u32[]{:S(2)}, u32[]{:S(2)}) collective-permute-start(bf16[1024,128]{0,1:T(8,128)(2,1)} %fusion.56), channel_id=1, source_target_pairs={{0,1},{1,2},{2,3},{3,0},{4,5},{5,6},{6,7},{7,4},{8,9},{9,10},{10,1... | collective-permute-start | bytes 786440 | tf_op jit(solution)/shard_map/ppermute | solution.py:55
  123.8 29.4 %collective-permute-start.10 = (bf16[1024,128]{0,1:T(8,128)(2,1)}, bf16[1024,128]{0,1:T(8,128)(2,1)}, u32[]{:S(2)}, u32[]{:S(2)}) collective-permute-start(bf16[1024,128]{0,1:T(8,128)(2,1)} %fusion.56), channel_id=1, source_target_pairs={{0,2},{1,3},{2,0},{3,1},{4,6},{5,7},{6,4},{7,5},{8,10},{9,11},{10,... | collective-permute-start | bytes 786440 | tf_op jit(solution)/shard_map/ppermute | solution.py:55
  126.1 27.1 %collective-permute-start.11 = (bf16[1024,128]{0,1:T(8,128)(2,1)}, bf16[1024,128]{0,1:T(8,128)(2,1)}, u32[]{:S(2)}, u32[]{:S(2)}) collective-permute-start(bf16[1024,128]{0,1:T(8,128)(2,1)} %fusion.56), channel_id=1, source_target_pairs={{0,3},{1,0},{2,1},{3,2},{4,7},{5,4},{6,5},{7,6},{8,11},{9,8},{10,9... | collective-permute-start | bytes 786440 | tf_op jit(solution)/shard_map/ppermute | solution.py:55
  142.0 18.4 %all-to-all-start.2 = ((bf16[32,2,512]{2,1,0:T(2,128)(2,1)}), bf16[32,2,512]{2,1,0:T(2,128)(2,1)S(1)}, u32[]{:S(2)}, u32[]{:S(2)}) async-start(bf16[32,2,512]{2,1,0:T(2,128)(2,1)} %reshape.494), calls=%async_computation.2 | async-start | bytes 131072 | tf_op jit(solution)/shard_map/all_to_all | solution.py:174
  161.0 6.4 %collective-permute-start.16 = (bf16[8,4,1024]{2,0,1:T(8,128)(2,1)S(1)}, bf16[8,4,1024]{2,0,1:T(8,128)(2,1)S(1)}, u32[]{:S(2)}, u32[]{:S(2)}) collective-permute-start(bf16[8,4,1024]{2,0,1:T(8,128)(2,1)S(1)} %all_to_all.37), channel_id=1, source_target_pairs={{0,1},{1,2},{2,3},{3,0},{4,5},{5,6},{6,7},{7,4},{8,9},{9,10},{10,1... | collective-permute-start | bytes 196616 | tf_op jit(solution)/shard_map/ppermute | solution.py:55
  161.1 6.3 %collective-permute-start.17 = (bf16[8,4,1024]{2,0,1:T(8,128)(2,1)S(1)}, bf16[8,4,1024]{2,0,1:T(8,128)(2,1)S(1)}, u32[]{:S(2)}, u32[]{:S(2)}) collective-permute-start(bf16[8,4,1024]{2,0,1:T(8,128)(2,1)S(1)} %all_to_all.37), channel_id=1, source_target_pairs={{0,2},{1,3},{2,0},{3,1},{4,6},{5,7},{6,4},{7,5},{8,10},{9,11},{10,... | collective-permute-start | bytes 196616 | tf_op jit(solution)/shard_map/ppermute | solution.py:55
  176.5 21.3 %all-to-all-start.3 = ((bf16[32,32,512]{2,1,0:T(8,128)(2,1)}), bf16[32,32,512]{2,1,0:T(8,128)(2,1)S(1)}, u32[]{:S(2)}, u32[]{:S(2)}) async-start(bf16[32,32,512]{2,1,0:T(8,128)(2,1)} %bitcast.73), calls=%async_computation.3 | async-start | bytes 2097152 | tf_op jit(solution)/shard_map/all_to_all | solution.py:204
  (24 other events, 185.2 us)

commit v10 on v9

--- a/solution.py
+++ b/solution.py
@@ -34,7 +34,7 @@
     return jnp.concatenate([turned, values[..., ROT:]], axis=-1)
 
 
-def head_exchange(pieces, axis):
+def head_exchange(pieces, axis, ordered=True):
     count = lax.axis_size("head")
     here = lax.axis_index("head")
     received = []
@@ -44,17 +44,32 @@
             piece = lax.ppermute(piece, "head", [(i, (i + shift) % count) for i in range(count)])
         received.append(piece)
     stacked = jnp.stack(received, axis=0)
+    if not ordered:
+        return stacked
     return jnp.take(stacked, (here - jnp.arange(count)) % count, axis=0)
 
 
-def head_gather(piece):
+def head_gather(piece, ordered=True):
     count = lax.axis_size("head")
     here = lax.axis_index("head")
     received = [piece]
     for shift in range(1, count):
         received.append(lax.ppermute(piece, "head", [(i, (i + shift) % count) for i in range(count)]))
     stacked = jnp.stack(received, axis=0)
+    if not ordered:
+        return stacked
     return jnp.take(stacked, (here - jnp.arange(count)) % count, axis=0)
+
+
+def head_scatter_unordered(pieces, axis):
+    count = lax.axis_size("head")
+    received = []
+    for shift in range(count):
+        piece = lax.index_in_dim(pieces, (-shift) % count, axis, keepdims=False)
+        if shift:
+            piece = lax.ppermute(piece, "head", [(i, (i + shift) % count) for i in range(count)])
+        received.append(piece)
+    return jnp.stack(received, axis=0)
 
 
 def local(
@@ -173,24 +188,24 @@
     transposed = jnp.transpose(attended, (2, 1, 0))
     slices = lax.all_to_all(transposed, "grp", split_axis=0, concat_axis=2, tiled=True)
     dim_here = slices.shape[0]
-    slices = jnp.moveaxis(head_gather(slices), 0, 1).reshape(dim_here, heads_here * head_count, -1)
+    slices = jnp.moveaxis(head_gather(slices, ordered=False), 0, 1).reshape(dim_here, heads_here * head_count, -1)
     out_blocks = head_exchange(
-        w_attn_out.reshape(dim_here, heads_here, head_count, width_here), 2
+        w_attn_out.reshape(dim_here, heads_here, head_count, width_here), 2, ordered=False
     )
     out_blocks = jnp.moveaxis(out_blocks, 0, 1).reshape(dim_here, heads_here * head_count, width_here)
     units = w_in.shape[1]
-    down_blocks = head_exchange(w_down.reshape(units, head_count, width_here), 1).reshape(
+    down_blocks = head_exchange(w_down.reshape(units, head_count, width_here), 1, ordered=False).reshape(
         units * head_count, width_here
     )
-    in_blocks = head_exchange(w_in.reshape(head_count, width_here, units), 0)
+    in_blocks = head_exchange(w_in.reshape(head_count, width_here, units), 0, ordered=False)
     in_blocks = jnp.moveaxis(in_blocks, 0, 1).reshape(width_here, head_count * units)
     partial = jnp.dot(gathered, in_blocks, preferred_element_type=jnp.float32)
-    partial = head_exchange(partial.astype(jnp.bfloat16).reshape(-1, head_count, units), 1)
+    partial = head_scatter_unordered(partial.astype(jnp.bfloat16).reshape(-1, head_count, units), 1)
     hidden = jax.nn.gelu(
         jnp.sum(partial.astype(jnp.float32), axis=0) + b_in.astype(jnp.float32),
         approximate=True,
     ).astype(jnp.bfloat16)
-    hidden = jnp.moveaxis(head_gather(hidden), 0, 1).reshape(hidden.shape[0], -1)
+    hidden = jnp.moveaxis(head_gather(hidden, ordered=False), 0, 1).reshape(hidden.shape[0], -1)
     mlp_part = jnp.dot(hidden, down_blocks, preferred_element_type=jnp.float32)
     attn_part = jnp.einsum("dkr,dkf->rf", slices, out_blocks, preferred_element_type=jnp.float32)
     combined = mlp_part + attn_part

time: 200 us -> 197 us (0.985)
  other arithmetic: 27.5 us -> 13.1 us
  waiting for transfers between devices: 49.7 us -> 63.7 us
  local copies, waits for them, and re-layouts: 39.2 us -> 34 us
    gather x4 -> x0, local copies, waits for them, and re-layouts: 10.3 us -> none  [head_exchange(): return jnp.take(stacked, (here - jnp.arange(count)) % count, axis=0)]
    all_to_all x1, waiting for transfers between devices: 21.8 us -> 31 us  [local(): lax.all_to_all(outgoing, 'grp', split_axis=1, concat_axis=0, tiled=True)]
    another operation x6 -> x2, other arithmetic: 8.26 us -> 0.36 us  [the longest x4 7.91 us: head_exchange(): stacked = jnp.stack(received, axis=0)]
    ppermute x12 -> x9, starting transfers between devices: 13.9 us -> 6.71 us  [head_exchange(): lax.ppermute(piece, 'head', [(i, (i + shift) % count) for i in range(coun...]
    ppermute x0 -> x3, starting transfers between devices: none -> 5.08 us  [head_scatter_unordered(): lax.ppermute(piece, 'head', [(i, (i + shift) % count) for i in range(coun...]
    ppermute x0 -> x3, waiting for transfers between devices: none -> 4.44 us  [head_scatter_unordered(): lax.ppermute(piece, 'head', [(i, (i + shift) % count) for i in range(coun...]
    ppermute x12 -> x9, waiting for transfers between devices: 3.31 us -> 0.02 us  [head_exchange(): lax.ppermute(piece, 'head', [(i, (i + shift) % count) for i in range(coun...]
    reshape x0 -> x1, local copies, waits for them, and re-layouts: none -> 2.62 us  [local(): w_down.reshape(units, head_count, width_here)]
  transfers between devices with their start and end apart: 27 -> 27, of which waited for: 5 -> 6; matrix products, arithmetic and copies ran while one was open for 39% -> 28% of each run, Pallas kernels for 0% -> 0%
where the time goes in v10:
time: 197 us; the launch traced here: 196 us
  waiting for transfers between devices  63.7 us (32%)
  starting transfers between devices  60.7 us (31%)
  local copies, waits for them, and re-layouts  34 us (17%)
  matrix products  24 us (12%)
  other arithmetic  13.1 us (7%)
    all_to_all x1, waiting for transfers between devices, local(): lax.all_to_all(outgoing, 'grp', split_axis=1, concat_axis=0, tiled=True)  31 us
    all_to_all x1, waiting for transfers between devices, local(): lax.all_to_all(pair_sum.reshape(grp_count, local_rows, half_width), 'grp'...  17.1 us
    ppermute x9, starting transfers between devices, head_gather(): lax.ppermute(piece, 'head', [(i, (i + shift) % count) for i in range(coun...  13.9 us
    all_to_all x1, starting transfers between devices, local(): lax.all_to_all(transposed, 'grp', split_axis=0, concat_axis=2, tiled=True)  13 us
    all_to_all x1, starting transfers between devices, local(): lax.all_to_all(outgoing, 'grp', split_axis=1, concat_axis=0, tiled=True)  9.93 us
    dynamic_slice x3, local copies, waits for them, and re-layouts, head_exchange(): lax.dynamic_index_in_dim(pieces, (here + shift) % count, axis, keepdims=F...  8.99 us
    unnamed x47, local copies, waits for them, and re-layouts  7.23 us
    all_to_all x1, waiting for transfers between devices, local(): lax.all_to_all(transposed, 'grp', split_axis=0, concat_axis=2, tiled=True)  7.11 us
  transfers between devices with their start and end apart: 27, of which 6 were waited for; matrix products, arithmetic and copies ran while one was open for 28% of the time, Pallas kernels for 0%

profile of v10, /device:TPU:1, one launch (start us, length us, event | category | flops | bytes accessed | tf_op | source)
XLA Modules:
  0.0 196.4 jit_solution(10027949848067682480)
XLA Ops:
  2.0 2.5 %collective-permute-start.1 = (bf16[32,1024]{1,0:T(8,128)(2,1)}, bf16[32,1024]{1,0:T(8,128)(2,1)S(1)}, u32[]{:S(2)}, u32[]{:S(2)}) collective-permute-start(bf16[32,1024]{1,0:T(8,128)(2,1)} %param.15), channel_id=1, source_target_pairs={{0,2},{1,3},{2,0},{3,1},{4,6},{5,7},{6,4},{7,5},{8,10},{9,11},{10,... | collective-permute-start | bytes 196616 | tf_op jit(solution)/shard_map/ppermute | solution.py:57
  13.7 9.9 %all-to-all-start = ((bf16[32,32,1280]{2,0,1:T(8,128)(2,1)}), bf16[32,32,1280]{2,0,1:T(8,128)(2,1)S(1)}, u32[]{:S(2)}, u32[]{:S(2)}) async-start(bf16[32,32,1280]{2,0,1:T(8,128)(2,1)} %pad_maximum_fusion), calls=%async_computation | async-start | bytes 5242880 | tf_op jit(solution)/shard_map/all_to_all | solution.py:109
  26.6 31.0 %all-to-all-done = bf16[32,32,1280]{2,0,1:T(8,128)(2,1)S(1)} async-done(((bf16[32,32,1280]{2,0,1:T(8,128)(2,1)}), bf16[32,32,1280]{2,0,1:T(8,128)(2,1)S(1)}, u32[]{:S(2)}, u32[]{:S(2)}) %all-to-all-start) | async-done | bytes 2621472 | tf_op jit(solution)/shard_map/all_to_all | solution.py:109
  57.6 2.7 %convolution_convert_fusion = bf16[1024,3,512]{2,0,1:T(8,128)(2,1)S(1)} fusion(bf16[128,3,512]{2,0,1:T(8,128)(2,1)S(1)} %collective-permute-done.15, bf16[128,3,512]{2,0,1:T(8,128)(2,1)} %get-tuple-element.19, pred[]{:T(512)S(6)} %eq.32, bf16[1024,1280]{1,0:T(8,128)(2,1)S(1)} %bitcast.208), kind=kOutput, calls=%fused_computation.10 | convolution fusion | flops 810418176 | bytes 4456449 | tf_op jit(solution)/shard_map/rf,fch->rch/dot_general | solution.py:124
  62.4 6.2 %all-to-all-start.1 = ((bf16[32,32,3,512]{3,1,2,0:T(8,128)(2,1)}), bf16[32,32,3,512]{3,1,2,0:T(8,128)(2,1)S(1)}, u32[]{:S(2)}, u32[]{:S(2)}) async-start(bf16[32,32,3,512]{3,1,2,0:T(8,128)(2,1)} %copy.168), calls=%async_computation.1 | async-start | bytes 6291456 | tf_op jit(solution)/shard_map/all_to_all | solution.py:127
  71.1 3.3 %collective-permute-start.4 = (bf16[1024,128]{1,0:T(8,128)(2,1)}, bf16[1024,128]{1,0:T(8,128)(2,1)}, u32[]{:S(2)}, u32[]{:S(2)}) collective-permute-start(bf16[1024,128]{1,0:T(8,128)(2,1)} %get-tuple-element.17), channel_id=1, source_target_pairs={{0,2},{1,3},{2,0},{3,1},{4,6},{5,7},{6,4},{7,5},{8,10},{9,11},{10,... | collective-permute-start | bytes 786440 | tf_op jit(solution)/shard_map/ppermute | solution.py:44
  74.4 2.6 %reshape.376 = bf16[128,4,1024]{2,1,0:T(4,128)(2,1)} reshape(bf16[128,4096]{1,0:T(8,128)(2,1)} %param.28) | data formatting | bytes 2097152 | tf_op jit(solution)/shard_map/reshape | solution.py:197
  77.0 5.5 %constant_dynamic-slice_fusion.9 = (bf16[128,1,1024]{2,1,0:T(2,128)(2,1)}, bf16[128,1,1024]{2,1,0:T(2,128)(2,1)S(1)}, bf16[128,1,1024]{2,1,0:T(2,128)(2,1)S(1)}, bf16[128,1,1024]{2,1,0:T(2,128)(2,1)}) fusion(bf16[128,4,1024]{2,1,0:T(4,128)(2,1)} %reshape.376, s32[]{:T(128)S(6)} %select_n.151, s32[]{:T(128)S(6)} %select_n.155, s32[]{:T(128)S(6)} %select_n.153, ...), kind=kLoop, calls=%fused_computation.164 | loop fusion | bytes 2097168 | tf_op jit(solution)/shard_map/jit(dynamic_index_in_dim)/dynamic_slice | solution.py:42
  88.3 2.3 %maximum_bitcast_fusion = bf16[1024,4,128]{2,0,1:T(8,128)(2,1)} fusion(bf16[1,1024,128]{2,1,0:T(8,128)(2,1)} %bitcast.16, bf16[1,1024,128]{2,1,0:T(8,128)(2,1)} %bitcast.14, bf16[1,1024,128]{2,1,0:T(8,128)(2,1)} %bitcast.12, bf16[1,1024,128]{2,1,0:T(8,128)(2,1)} %get-tuple-element.15), kind=kLoop, calls=%fused_computation.28 | loop fusion | flops 1572864 | bytes 2097152 | tf_op jit(solution)/shard_map/transpose | solution.py:201
  90.6 2.3 %copy.161 = bf16[1024,4,128]{0,2,1:T(8,128)(2,1)} copy(bf16[1024,4,128]{2,0,1:T(8,128)(2,1)} %maximum_bitcast_fusion) | data formatting | bytes 2097152 | tf_op jit(solution)/shard_map/transpose | solution.py:201
  92.9 3.2 %fusion.14 = bf16[1024,512]{0,1:T(8,128)(2,1)S(1)} fusion(bf16[1024,512]{0,1:T(8,128)(2,1)} %bitcast.216, bf16[1024,1280]{1,0:T(8,128)(2,1)} %bitcast.209), kind=kOutput, calls=%fused_computation.23 | convolution fusion | flops 1074266112 | bytes 4194304 | tf_op jit(solution)/shard_map/dot_general | solution.py:202
  106.0 4.4 %collective-permute-done.7 = bf16[1024,128]{0,1:T(8,128)(2,1)S(1)} collective-permute-done((bf16[1024,128]{0,1:T(8,128)(2,1)S(1)}, bf16[1024,128]{0,1:T(8,128)(2,1)S(1)}, u32[]{:S(2)}, u32[]{:S(2)}) %collective-permute-start.7) | collective-permute-done | bytes 262176 | tf_op jit(solution)/shard_map/ppermute | solution.py:70
  119.7 3.5 %fusion.112 = (f32[2,16,4]{1,2,0:T(4,128)S(1)}, f32[2,16,4,1024]{3,1,2,0:T(8,128)S(1)}) fusion(bf16[2,128,4,8,256]{4,3,2,1,0:T(8,128)(2,1)} %bitcast.204, bf16[2,16,4,64]{3,1,2,0:T(8,128)(2,1)S(1)} %copy.173, pred[2,1024]{1,0:T(4,128)(4,1)S(1)} %iota_compare_fusion.1, bf16[2,16,4,192]{3,1,0,2:T(8,128)(2,1)S(1)} %bitcast.219), kind=kOutput, calls=%fused_computation.198 | convolution fusion | flops 67633024 | bytes 4786688 | tf_op jit(solution)/shard_map/gqhd,gjhd->gqhj/dot_general | solution.py:148
  123.3 2.2 %fusion.9 = f32[32,4,1,32]{3,2,1,0:T(1,128)S(1)} fusion(bf16[32,4,4,8,256]{4,3,2,1,0:T(8,128)(2,1)} %bitcast.238, bf16[32,4,256,1]{2,0,1,3:T(8,128)(2,1)S(1)} %get-tuple-element.33), kind=kOutput, calls=%fused_computation.14 | convolution fusion | flops 2097152 | bytes 2179072 | tf_op jit(solution)/shard_map/rhd,rthd->rht/dot_general | solution.py:156
  127.9 2.9 %fusion.26 = f32[2,16,4,256]{3,1,2,0:T(8,128)S(1)} fusion(bf16[2,128,4,8,256]{4,3,2,1,0:T(8,128)(2,1)} %bitcast.205, f32[2,16,4,1024]{3,1,2,0:T(8,128)S(1)} %get-tuple-element.40, f32[2,16,4]{1,2,0:T(4,128)S(1)} %copy.180), kind=kOutput, calls=%fused_computation.27 | convolution fusion | flops 67371008 | bytes 4850176 | tf_op jit(solution)/shard_map/gqhj,gjhd->gqhd/dot_general | solution.py:174
  131.3 2.5 %collective-permute-start.10 = (bf16[1024,128]{1,0:T(8,128)(2,1)S(1)}, bf16[1024,128]{1,0:T(8,128)(2,1)S(1)}, u32[]{:S(2)}, u32[]{:S(2)}) collective-permute-start(bf16[1024,128]{1,0:T(8,128)(2,1)S(1)} %fusion.64), channel_id=1, source_target_pairs={{0,2},{1,3},{2,0},{3,1},{4,6},{5,7},{6,4},{7,5},{8,10},{9,11},{10,... | collective-permute-start | bytes 786440 | tf_op jit(solution)/shard_map/ppermute | solution.py:57
  135.0 13.0 %all-to-all-start.2 = ((bf16[32,2,512]{2,1,0:T(2,128)(2,1)}), bf16[32,2,512]{2,1,0:T(2,128)(2,1)S(1)}, u32[]{:S(2)}, u32[]{:S(2)}) async-start(bf16[32,2,512]{2,1,0:T(2,128)(2,1)} %reshape.415), calls=%async_computation.2 | async-start | bytes 131072 | tf_op jit(solution)/shard_map/all_to_all | solution.py:189
  148.2 7.1 %all-to-all-done.2 = bf16[32,2,512]{2,1,0:T(2,128)(2,1)S(1)} async-done(((bf16[32,2,512]{2,1,0:T(2,128)(2,1)}), bf16[32,2,512]{2,1,0:T(2,128)(2,1)S(1)}, u32[]{:S(2)}, u32[]{:S(2)}) %all-to-all-start.2) | async-done | bytes 65568 | tf_op jit(solution)/shard_map/all_to_all | solution.py:189
  157.5 2.9 %collective-permute-start.17 = (bf16[8,4,1024]{2,0,1:T(8,128)(2,1)S(1)}, bf16[8,4,1024]{2,0,1:T(8,128)(2,1)S(1)}, u32[]{:S(2)}, u32[]{:S(2)}) collective-permute-start(bf16[8,4,1024]{2,0,1:T(8,128)(2,1)S(1)} %all_to_all.37), channel_id=1, source_target_pairs={{0,2},{1,3},{2,0},{3,1},{4,6},{5,7},{6,4},{7,5},{8,10},{9,11},{10,... | collective-permute-start | bytes 196616 | tf_op jit(solution)/shard_map/ppermute | solution.py:57
  161.1 4.5 %fusion.29 = f32[1024,1024,1]{1,0,2:T(8,128)} fusion(bf16[1,1024,128]{2,1,0:T(8,128)(2,1)S(1)} %bitcast.241, bf16[1,1024,128]{2,1,0:T(8,128)(2,1)S(1)} %bitcast.240, bf16[1,1024,128]{2,1,0:T(8,128)(2,1)} %bitcast.28, bf16[1,1024,128]{2,1,0:T(8,128)(2,1)S(1)} %fusion.56, bf16[1,128,1024]{2,1,0:T(8,128)(2,1)} %bitcast.38, bf16[1,128,1024]{2,1,0:T(8,128)(2,1)} %bitcast.36, ...), kind=kOutput, calls=%fused_computation.30 | convolution fusion | flops 1076887552 | bytes 6291456 | tf_op jit(solution)/shard_map/dot_general | solution.py:209
  165.9 2.9 %bitcast_add_fusion = f32[1024,1024]{1,0:T(8,128)S(1)} fusion(f32[1024,1024,1]{1,0,2:T(8,128)} %fusion.29, bf16[1,8,4,1024]{3,1,2,0:T(8,128)(2,1)S(1)} %bitcast.247, bf16[1,8,4,1024]{3,1,2,0:T(8,128)(2,1)S(1)} %bitcast.246, bf16[1,8,4,1024]{3,1,2,0:T(8,128)(2,1)S(1)} %bitcast.245, bf16[1,8,4,1024]{3,1,2,0:T(8,128)(2,1)S(1)} %stack.133, ...), kind=kOutput, calls=%fused_computation.8 | convolution fusion | flops 270270464 | bytes 8912896 | tf_op jit(solution)/shard_map/dkr,dkf->rf/dot_general | solution.py:210
  170.7 2.3 %collective-permute-done.22 = bf16[1024,512]{1,0:T(8,128)(2,1)S(1)} collective-permute-done((bf16[1024,512]{1,0:T(8,128)(2,1)S(1)}, bf16[1024,512]{1,0:T(8,128)(2,1)S(1)}, u32[]{:S(2)}, u32[]{:S(2)}) %collective-permute-start.22) | collective-permute-done | bytes 1048608 | tf_op jit(solution)/shard_map/ppermute | solution.py:215
  174.3 4.1 %all-to-all-start.3 = ((bf16[32,32,512]{2,1,0:T(8,128)(2,1)}), bf16[32,32,512]{2,1,0:T(8,128)(2,1)S(1)}, u32[]{:S(2)}, u32[]{:S(2)}) async-start(bf16[32,32,512]{2,1,0:T(8,128)(2,1)} %bitcast.76), calls=%async_computation.3 | async-start | bytes 2097152 | tf_op jit(solution)/shard_map/all_to_all | solution.py:219
  178.4 17.1 %all-to-all-done.3 = bf16[32,32,512]{2,1,0:T(8,128)(2,1)S(1)} async-done(((bf16[32,32,512]{2,1,0:T(8,128)(2,1)}), bf16[32,32,512]{2,1,0:T(8,128)(2,1)S(1)}, u32[]{:S(2)}, u32[]{:S(2)}) %all-to-all-start.3) | async-done | bytes 1048608 | tf_op jit(solution)/shard_map/all_to_all | solution.py:219
  (176 shorter events, 54.7 us)
Async XLA Ops:
  0.0 8.5 %collective-permute-start = (bf16[32,1024]{1,0:T(8,128)(2,1)}, bf16[32,1024]{1,0:T(8,128)(2,1)S(1)}, u32[]{:S(2)}, u32[]{:S(2)}) collective-permute-start(bf16[32,1024]{1,0:T(8,128)(2,1)} %param.15), channel_id=1, source_target_pairs={{0,1},{1,2},{2,3},{3,0},{4,5},{5,6},{6,7},{7,4},{8,9},{9,10},{10,1... | collective-permute-start | bytes 196616 | tf_op jit(solution)/shard_map/ppermute | solution.py:57
  2.0 6.4 %collective-permute-start.1 = (bf16[32,1024]{1,0:T(8,128)(2,1)}, bf16[32,1024]{1,0:T(8,128)(2,1)S(1)}, u32[]{:S(2)}, u32[]{:S(2)}) collective-permute-start(bf16[32,1024]{1,0:T(8,128)(2,1)} %param.15), channel_id=1, source_target_pairs={{0,2},{1,3},{2,0},{3,1},{4,6},{5,7},{6,4},{7,5},{8,10},{9,11},{10,... | collective-permute-start | bytes 196616 | tf_op jit(solution)/shard_map/ppermute | solution.py:57
  13.7 43.9 %all-to-all-start = ((bf16[32,32,1280]{2,0,1:T(8,128)(2,1)}), bf16[32,32,1280]{2,0,1:T(8,128)(2,1)S(1)}, u32[]{:S(2)}, u32[]{:S(2)}) async-start(bf16[32,32,1280]{2,0,1:T(8,128)(2,1)} %pad_maximum_fusion), calls=%async_computation | async-start | bytes 5242880 | tf_op jit(solution)/shard_map/all_to_all | solution.py:109
  62.4 54.5 %all-to-all-start.1 = ((bf16[32,32,3,512]{3,1,2,0:T(8,128)(2,1)}), bf16[32,32,3,512]{3,1,2,0:T(8,128)(2,1)S(1)}, u32[]{:S(2)}, u32[]{:S(2)}) async-start(bf16[32,32,3,512]{3,1,2,0:T(8,128)(2,1)} %copy.168), calls=%async_computation.1 | async-start | bytes 6291456 | tf_op jit(solution)/shard_map/all_to_all | solution.py:127
  70.8 17.4 %collective-permute-start.3 = (bf16[1024,128]{1,0:T(8,128)(2,1)}, bf16[1024,128]{1,0:T(8,128)(2,1)}, u32[]{:S(2)}, u32[]{:S(2)}) collective-permute-start(bf16[1024,128]{1,0:T(8,128)(2,1)} %get-tuple-element.18), channel_id=1, source_target_pairs={{0,1},{1,2},{2,3},{3,0},{4,5},{5,6},{6,7},{7,4},{8,9},{9,10},{10,1... | collective-permute-start | bytes 786440 | tf_op jit(solution)/shard_map/ppermute | solution.py:44
  71.1 17.1 %collective-permute-start.4 = (bf16[1024,128]{1,0:T(8,128)(2,1)}, bf16[1024,128]{1,0:T(8,128)(2,1)}, u32[]{:S(2)}, u32[]{:S(2)}) collective-permute-start(bf16[1024,128]{1,0:T(8,128)(2,1)} %get-tuple-element.17), channel_id=1, source_target_pairs={{0,2},{1,3},{2,0},{3,1},{4,6},{5,7},{6,4},{7,5},{8,10},{9,11},{10,... | collective-permute-start | bytes 786440 | tf_op jit(solution)/shard_map/ppermute | solution.py:44
  74.4 13.9 %collective-permute-start.5 = (bf16[1024,128]{1,0:T(8,128)(2,1)}, bf16[1024,128]{1,0:T(8,128)(2,1)}, u32[]{:S(2)}, u32[]{:S(2)}) collective-permute-start(bf16[1024,128]{1,0:T(8,128)(2,1)} %get-tuple-element.16), channel_id=1, source_target_pairs={{0,3},{1,0},{2,1},{3,2},{4,7},{5,4},{6,5},{7,6},{8,11},{9,8},{10,9... | collective-permute-start | bytes 786440 | tf_op jit(solution)/shard_map/ppermute | solution.py:44
  83.2 50.6 %collective-permute-start.12 = (bf16[128,1024]{1,0:T(8,128)(2,1)}, bf16[128,1024]{1,0:T(8,128)(2,1)}, u32[]{:S(2)}, u32[]{:S(2)}) collective-permute-start(bf16[128,1024]{1,0:T(8,128)(2,1)} %bitcast.196), channel_id=1, source_target_pairs={{0,1},{1,2},{2,3},{3,0},{4,5},{5,6},{6,7},{7,4},{8,9},{9,10},{10,1... | collective-permute-start | bytes 786440 | tf_op jit(solution)/shard_map/ppermute | solution.py:44
  85.5 70.4 %collective-permute-start.13 = (bf16[128,1024]{1,0:T(8,128)(2,1)}, bf16[128,1024]{1,0:T(8,128)(2,1)}, u32[]{:S(2)}, u32[]{:S(2)}) collective-permute-start(bf16[128,1024]{1,0:T(8,128)(2,1)} %bitcast.195), channel_id=1, source_target_pairs={{0,2},{1,3},{2,0},{3,1},{4,6},{5,7},{6,4},{7,5},{8,10},{9,11},{10,... | collective-permute-start | bytes 786440 | tf_op jit(solution)/shard_map/ppermute | solution.py:44
  96.2 9.6 %collective-permute-start.6 = (bf16[1024,128]{0,1:T(8,128)(2,1)S(1)}, bf16[1024,128]{0,1:T(8,128)(2,1)S(1)}, u32[]{:S(2)}, u32[]{:S(2)}) collective-permute-start(bf16[1024,128]{0,1:T(8,128)(2,1)S(1)} %get-tuple-element.14), channel_id=1, source_target_pairs={{0,1},{1,2},{2,3},{3,0},{4,5},{5,6},{6,7},{7,4},{8,9},{9,10},{10,1... | collective-permute-start | bytes 786440 | tf_op jit(solution)/shard_map/ppermute | solution.py:70
  98.1 12.3 %collective-permute-start.7 = (bf16[1024,128]{0,1:T(8,128)(2,1)S(1)}, bf16[1024,128]{0,1:T(8,128)(2,1)S(1)}, u32[]{:S(2)}, u32[]{:S(2)}) collective-permute-start(bf16[1024,128]{0,1:T(8,128)(2,1)S(1)} %get-tuple-element.13), channel_id=1, source_target_pairs={{0,2},{1,3},{2,0},{3,1},{4,6},{5,7},{6,4},{7,5},{8,10},{9,11},{10,... | collective-permute-start | bytes 786440 | tf_op jit(solution)/shard_map/ppermute | solution.py:70
  99.8 10.6 %collective-permute-start.8 = (bf16[1024,128]{0,1:T(8,128)(2,1)S(1)}, bf16[1024,128]{0,1:T(8,128)(2,1)S(1)}, u32[]{:S(2)}, u32[]{:S(2)}) collective-permute-start(bf16[1024,128]{0,1:T(8,128)(2,1)S(1)} %get-tuple-element.12), channel_id=1, source_target_pairs={{0,3},{1,0},{2,1},{3,2},{4,7},{5,4},{6,5},{7,6},{8,11},{9,8},{10,9... | collective-permute-start | bytes 786440 | tf_op jit(solution)/shard_map/ppermute | solution.py:70
  105.9 50.1 %collective-permute-start.14 = (bf16[128,1024]{1,0:T(8,128)(2,1)}, bf16[128,1024]{1,0:T(8,128)(2,1)}, u32[]{:S(2)}, u32[]{:S(2)}) collective-permute-start(bf16[128,1024]{1,0:T(8,128)(2,1)} %bitcast.194), channel_id=1, source_target_pairs={{0,3},{1,0},{2,1},{3,2},{4,7},{5,4},{6,5},{7,6},{8,11},{9,8},{10,9... | collective-permute-start | bytes 786440 | tf_op jit(solution)/shard_map/ppermute | solution.py:44
  110.4 20.9 %collective-permute-start.19 = (bf16[8,4,1024]{2,0,1:T(8,128)(2,1)}, bf16[8,4,1024]{2,0,1:T(8,128)(2,1)S(1)}, u32[]{:S(2)}, u32[]{:S(2)}) collective-permute-start(bf16[8,4,1024]{2,0,1:T(8,128)(2,1)} %bitcast.201), channel_id=1, source_target_pairs={{0,1},{1,2},{2,3},{3,0},{4,5},{5,6},{6,7},{7,4},{8,9},{9,10},{10,1... | collective-permute-start | bytes 196616 | tf_op jit(solution)/shard_map/ppermute | solution.py:44
  114.7 42.8 %collective-permute-start.9 = (bf16[1024,128]{1,0:T(8,128)(2,1)S(1)}, bf16[1024,128]{1,0:T(8,128)(2,1)}, u32[]{:S(2)}, u32[]{:S(2)}) collective-permute-start(bf16[1024,128]{1,0:T(8,128)(2,1)S(1)} %fusion.64), channel_id=1, source_target_pairs={{0,1},{1,2},{2,3},{3,0},{4,5},{5,6},{6,7},{7,4},{8,9},{9,10},{10,1... | collective-permute-start | bytes 786440 | tf_op jit(solution)/shard_map/ppermute | solution.py:57
  131.3 26.2 %collective-permute-start.10 = (bf16[1024,128]{1,0:T(8,128)(2,1)S(1)}, bf16[1024,128]{1,0:T(8,128)(2,1)S(1)}, u32[]{:S(2)}, u32[]{:S(2)}) collective-permute-start(bf16[1024,128]{1,0:T(8,128)(2,1)S(1)} %fusion.64), channel_id=1, source_target_pairs={{0,2},{1,3},{2,0},{3,1},{4,6},{5,7},{6,4},{7,5},{8,10},{9,11},{10,... | collective-permute-start | bytes 786440 | tf_op jit(solution)/shard_map/ppermute | solution.py:57
  133.8 26.6 %collective-permute-start.11 = (bf16[1024,128]{1,0:T(8,128)(2,1)S(1)}, bf16[1024,128]{1,0:T(8,128)(2,1)S(1)}, u32[]{:S(2)}, u32[]{:S(2)}) collective-permute-start(bf16[1024,128]{1,0:T(8,128)(2,1)S(1)} %fusion.64), channel_id=1, source_target_pairs={{0,3},{1,0},{2,1},{3,2},{4,7},{5,4},{6,5},{7,6},{8,11},{9,8},{10,9... | collective-permute-start | bytes 786440 | tf_op jit(solution)/shard_map/ppermute | solution.py:57
  135.0 20.3 %all-to-all-start.2 = ((bf16[32,2,512]{2,1,0:T(2,128)(2,1)}), bf16[32,2,512]{2,1,0:T(2,128)(2,1)S(1)}, u32[]{:S(2)}, u32[]{:S(2)}) async-start(bf16[32,2,512]{2,1,0:T(2,128)(2,1)} %reshape.415), calls=%async_computation.2 | async-start | bytes 131072 | tf_op jit(solution)/shard_map/all_to_all | solution.py:189
  155.9 10.0 %collective-permute-start.20 = (bf16[8,4,1024]{2,0,1:T(8,128)(2,1)S(1)}, bf16[8,4,1024]{2,0,1:T(8,128)(2,1)S(1)}, u32[]{:S(2)}, u32[]{:S(2)}) collective-permute-start(bf16[8,4,1024]{2,0,1:T(8,128)(2,1)S(1)} %bitcast.234), channel_id=1, source_target_pairs={{0,2},{1,3},{2,0},{3,1},{4,6},{5,7},{6,4},{7,5},{8,10},{9,11},{10,... | collective-permute-start | bytes 196616 | tf_op jit(solution)/shard_map/ppermute | solution.py:44
  156.0 9.9 %collective-permute-start.21 = (bf16[8,4,1024]{2,0,1:T(8,128)(2,1)S(1)}, bf16[8,4,1024]{2,0,1:T(8,128)(2,1)S(1)}, u32[]{:S(2)}, u32[]{:S(2)}) collective-permute-start(bf16[8,4,1024]{2,0,1:T(8,128)(2,1)S(1)} %bitcast.233), channel_id=1, source_target_pairs={{0,3},{1,0},{2,1},{3,2},{4,7},{5,4},{6,5},{7,6},{8,11},{9,8},{10,9... | collective-permute-start | bytes 196616 | tf_op jit(solution)/shard_map/ppermute | solution.py:44
  157.5 8.4 %collective-permute-start.16 = (bf16[8,4,1024]{2,0,1:T(8,128)(2,1)S(1)}, bf16[8,4,1024]{2,0,1:T(8,128)(2,1)S(1)}, u32[]{:S(2)}, u32[]{:S(2)}) collective-permute-start(bf16[8,4,1024]{2,0,1:T(8,128)(2,1)S(1)} %all_to_all.37), channel_id=1, source_target_pairs={{0,1},{1,2},{2,3},{3,0},{4,5},{5,6},{6,7},{7,4},{8,9},{9,10},{10,1... | collective-permute-start | bytes 196616 | tf_op jit(solution)/shard_map/ppermute | solution.py:57
  157.5 8.4 %collective-permute-start.17 = (bf16[8,4,1024]{2,0,1:T(8,128)(2,1)S(1)}, bf16[8,4,1024]{2,0,1:T(8,128)(2,1)S(1)}, u32[]{:S(2)}, u32[]{:S(2)}) collective-permute-start(bf16[8,4,1024]{2,0,1:T(8,128)(2,1)S(1)} %all_to_all.37), channel_id=1, source_target_pairs={{0,2},{1,3},{2,0},{3,1},{4,6},{5,7},{6,4},{7,5},{8,10},{9,11},{10,... | collective-permute-start | bytes 196616 | tf_op jit(solution)/shard_map/ppermute | solution.py:57
  160.4 5.5 %collective-permute-start.18 = (bf16[8,4,1024]{2,0,1:T(8,128)(2,1)S(1)}, bf16[8,4,1024]{2,0,1:T(8,128)(2,1)S(1)}, u32[]{:S(2)}, u32[]{:S(2)}) collective-permute-start(bf16[8,4,1024]{2,0,1:T(8,128)(2,1)S(1)} %all_to_all.37), channel_id=1, source_target_pairs={{0,3},{1,0},{2,1},{3,2},{4,7},{5,4},{6,5},{7,6},{8,11},{9,8},{10,9... | collective-permute-start | bytes 196616 | tf_op jit(solution)/shard_map/ppermute | solution.py:57
  174.3 21.3 %all-to-all-start.3 = ((bf16[32,32,512]{2,1,0:T(8,128)(2,1)}), bf16[32,32,512]{2,1,0:T(8,128)(2,1)S(1)}, u32[]{:S(2)}, u32[]{:S(2)}) async-start(bf16[32,32,512]{2,1,0:T(8,128)(2,1)} %bitcast.76), calls=%async_computation.3 | async-start | bytes 2097152 | tf_op jit(solution)/shard_map/all_to_all | solution.py:219
  (20 other events, 223.1 us)

commit v11 on v6

--- a/solution.py
+++ b/solution.py
@@ -34,7 +34,7 @@
     return jnp.concatenate([turned, values[..., ROT:]], axis=-1)
 
 
-def head_exchange(pieces, axis):
+def head_exchange(pieces, axis, ordered=True):
     count = lax.axis_size("head")
     here = lax.axis_index("head")
     received = []
@@ -44,16 +44,20 @@
             piece = lax.ppermute(piece, "head", [(i, (i + shift) % count) for i in range(count)])
         received.append(piece)
     stacked = jnp.stack(received, axis=0)
+    if not ordered:
+        return stacked
     return jnp.take(stacked, (here - jnp.arange(count)) % count, axis=0)
 
 
-def head_gather(piece):
+def head_gather(piece, ordered=True):
     count = lax.axis_size("head")
     here = lax.axis_index("head")
     received = [piece]
     for shift in range(1, count):
         received.append(lax.ppermute(piece, "head", [(i, (i + shift) % count) for i in range(count)]))
     stacked = jnp.stack(received, axis=0)
+    if not ordered:
+        return stacked
     return jnp.take(stacked, (here - jnp.arange(count)) % count, axis=0)
 
 
@@ -164,13 +168,13 @@
     transposed = jnp.transpose(attended, (2, 1, 0))
     slices = lax.all_to_all(transposed, "grp", split_axis=0, concat_axis=2, tiled=True)
     dim_here = slices.shape[0]
-    slices = jnp.moveaxis(head_gather(slices), 0, 1).reshape(dim_here, heads_here * head_count, -1)
+    slices = jnp.moveaxis(head_gather(slices, ordered=False), 0, 1).reshape(dim_here, heads_here * head_count, -1)
     out_blocks = head_exchange(
-        w_attn_out.reshape(dim_here, heads_here, head_count, width_here), 2
+        w_attn_out.reshape(dim_here, heads_here, head_count, width_here), 2, ordered=False
     )
     out_blocks = jnp.moveaxis(out_blocks, 0, 1).reshape(dim_here, heads_here * head_count, width_here)
     units = w_in.shape[1]
-    down_blocks = head_exchange(w_down.reshape(units, head_count, width_here), 1).reshape(
+    down_blocks = head_exchange(w_down.reshape(units, head_count, width_here), 1, ordered=False).reshape(
         units * head_count, width_here
     )
     hidden = jax.nn.gelu(
@@ -182,7 +186,7 @@
         + b_in.astype(jnp.float32),
         approximate=True,
     ).astype(jnp.bfloat16)
-    hidden = lax.all_gather(hidden, "head", axis=1, tiled=True)
+    hidden = jnp.moveaxis(head_gather(hidden, ordered=False), 0, 1).reshape(hidden.shape[0], -1)
     mlp_part = jnp.dot(hidden, down_blocks, preferred_element_type=jnp.float32)
     attn_part = jnp.einsum("dkr,dkf->rf", slices, out_blocks, preferred_element_type=jnp.float32)
     combined = mlp_part + attn_part

time: 194 us -> 199 us (1.026)
  waiting for transfers between devices: 84.7 us -> 88.6 us
    all_to_all x1, waiting for transfers between devices: 39.9 us -> 44.7 us  [local(): lax.all_to_all(term.reshape(grp_count, local_rows, 3, half), 'grp', 0, 0,...]
    all_to_all x1, starting transfers between devices: 6.49 us -> 3.96 us  [local(): lax.all_to_all(pair_sum.reshape(grp_count, local_rows, half_width), 'grp'...]
    ppermute x6 -> x9, waiting for transfers between devices: 6.15 us -> 3.67 us  [head_gather(): lax.ppermute(piece, 'head', [(i, (i + shift) % count) for i in range(coun...]
    ppermute x6 -> x9, starting transfers between devices: 7.16 us -> 9.34 us  [head_gather(): lax.ppermute(piece, 'head', [(i, (i + shift) % count) for i in range(coun...]
    unnamed x34 -> x39, local copies, waits for them, and re-layouts: 4.14 us -> 3.27 us
  transfers between devices with their start and end apart: 20 -> 22, of which waited for: 10 -> 9; matrix products, arithmetic and copies ran while one was open for 22% -> 23% of each run, Pallas kernels for 0% -> 0%
where the time goes in v11:
time: 199 us; the launch traced here: 198 us
  waiting for transfers between devices  88.6 us (45%)
  starting transfers between devices  43.6 us (22%)
  matrix products  22.4 us (11%)
  other arithmetic  15.4 us (8%)
  local copies, waits for them, and re-layouts  14.4 us (7%)
  between operations  14.2 us (7%)
    all_to_all x1, waiting for transfers between devices, local(): lax.all_to_all(term.reshape(grp_count, local_rows, 3, half), 'grp', 0, 0,...  44.7 us
    all_to_all x1, waiting for transfers between devices, local(): lax.all_to_all(pair_sum.reshape(grp_count, local_rows, half_width), 'grp'...  17.1 us
    all_to_all x1, waiting for transfers between devices, local(): lax.all_to_all(jnp.repeat(pair_rows, 2, axis=1), 'grp', split_axis=1, con...  12.2 us
    all_to_all x1, starting transfers between devices, local(): lax.all_to_all(jnp.repeat(pair_rows, 2, axis=1), 'grp', split_axis=1, con...  10.6 us
    ppermute x9, starting transfers between devices, head_gather(): lax.ppermute(piece, 'head', [(i, (i + shift) % count) for i in range(coun...  9.34 us
    all_to_all x1, waiting for transfers between devices, local(): lax.all_to_all(transposed, 'grp', split_axis=0, concat_axis=2, tiled=True)  7.08 us
    ppermute x6, starting transfers between devices, head_exchange(): lax.ppermute(piece, 'head', [(i, (i + shift) % count) for i in range(coun...  6.93 us
    dot_general x1, matrix products, local(): jnp.dot(gathered, w_in, preferred_element_type=jnp.float32)  6.45 us
  transfers between devices with their start and end apart: 22, of which 9 were waited for; matrix products, arithmetic and copies ran while one was open for 23% of the time, Pallas kernels for 0%

profile of v11, /device:TPU:1, one launch (start us, length us, event | category | flops | bytes accessed | tf_op | source)
XLA Modules:
  0.0 198.4 jit_solution(9816164419366427086)
XLA Ops:
  6.5 2.1 %collective-permute-start = (bf16[32,1024]{1,0:T(8,128)(2,1)}, bf16[32,1024]{1,0:T(8,128)(2,1)S(1)}, u32[]{:S(2)}, u32[]{:S(2)}) collective-permute-start(bf16[32,1024]{1,0:T(8,128)(2,1)} %param.15), channel_id=1, source_target_pairs={{0,1},{1,2},{2,3},{3,0},{4,5},{5,6},{6,7},{7,4},{8,9},{9,10},{10,1... | collective-permute-start | bytes 196616 | tf_op jit(solution)/shard_map/ppermute | solution.py:57
  10.0 1.6 collective-permute-start.1
  13.1 1.7 collective-permute-done.1
  19.8 10.6 %all-to-all-start = ((bf16[32,32,256]{2,0,1:T(8,128)(2,1)}), bf16[32,32,256]{2,0,1:T(8,128)(2,1)S(1)}, u32[]{:S(2)}, u32[]{:S(2)}) async-start(bf16[32,32,256]{2,0,1:T(8,128)(2,1)} %bitcast.19), calls=%async_computation | async-start | bytes 1048576 | tf_op jit(solution)/shard_map/all_to_all | solution.py:91
  32.3 12.2 %all-to-all-done = bf16[32,32,256]{2,0,1:T(8,128)(2,1)S(1)} async-done(((bf16[32,32,256]{2,0,1:T(8,128)(2,1)}), bf16[32,32,256]{2,0,1:T(8,128)(2,1)S(1)}, u32[]{:S(2)}, u32[]{:S(2)}) %all-to-all-start) | async-done | bytes 524320 | tf_op jit(solution)/shard_map/all_to_all | solution.py:91
  45.5 2.2 %copy.131 = bf16[32,32,3,512]{3,1,2,0:T(8,128)(2,1)} copy(bf16[32,32,3,512]{3,1,0,2:T(8,128)(2,1)S(1)} %bitcast.179) | data formatting | bytes 6291456 | tf_op jit(solution)/shard_map/reshape | solution.py:108
  47.6 4.9 %all-to-all-start.1 = ((bf16[32,32,3,512]{3,1,2,0:T(8,128)(2,1)}), bf16[32,32,3,512]{3,1,2,0:T(8,128)(2,1)}, u32[]{:S(2)}, u32[]{:S(2)}) async-start(bf16[32,32,3,512]{3,1,2,0:T(8,128)(2,1)} %copy.131), calls=%async_computation.1 | async-start | bytes 6291456 | tf_op jit(solution)/shard_map/all_to_all | solution.py:107
  55.8 2.2 %constant_dynamic-slice_fusion.9 = (bf16[128,1,1024]{2,1,0:T(2,128)(2,1)S(1)}, bf16[128,1,1024]{2,1,0:T(2,128)(2,1)S(1)}, bf16[128,1,1024]{2,1,0:T(2,128)(2,1)S(1)}, bf16[128,1,1024]{2,1,0:T(2,128)(2,1)S(1)}) fusion(bf16[128,4,1024]{2,1,0:T(4,128)(2,1)S(1)} %reshape.301, s32[]{:T(128)S(6)} %select_n.134, s32[]{:T(128)S(6)} %select_n.138, s32[]{:T(128)S(6)} %select_n.136, ...), kind=kLoop, calls=%fused_computation.138 | loop fusion | bytes 2097168 | tf_op jit(solution)/shard_map/jit(dynamic_index_in_dim)/dynamic_slice | solution.py:42
  64.5 44.7 %all-to-all-done.1 = bf16[32,32,3,512]{3,1,2,0:T(8,128)(2,1)} async-done(((bf16[32,32,3,512]{3,1,2,0:T(8,128)(2,1)}), bf16[32,32,3,512]{3,1,2,0:T(8,128)(2,1)}, u32[]{:S(2)}, u32[]{:S(2)}) %all-to-all-start.1) | async-done | bytes 3145760 | tf_op jit(solution)/shard_map/all_to_all | solution.py:107
  109.3 2.5 %convert_reduce_fusion = f32[2,32,3,512]{3,1,2,0:T(8,128)S(1)} fusion(bf16[16,2,32,3,512]{4,2,3,1,0:T(8,128)(2,1)} %bitcast.63), kind=kLoop, calls=%fused_computation.1 | loop fusion | flops 3047424 | bytes 3538944 | tf_op jit(solution)/shard_map/reduce_sum | solution.py:110
  117.0 3.5 %fusion.95 = (f32[2,16,4]{1,2,0:T(4,128)S(1)}, f32[2,16,4,1024]{3,1,2,0:T(8,128)S(1)}) fusion(bf16[2,128,4,8,256]{4,3,2,1,0:T(8,128)(2,1)} %bitcast.176, bf16[2,16,4,64]{3,1,2,0:T(8,128)(2,1)S(1)} %copy.136, pred[2,1024]{1,0:T(4,128)(4,1)} %iota_compare_fusion.1, bf16[2,16,4,192]{3,1,0,2:T(8,128)(2,1)S(1)} %bitcast.185), kind=kOutput, calls=%fused_computation.170 | convolution fusion | flops 67633024 | bytes 4786688 | tf_op jit(solution)/shard_map/gqhd,gjhd->gqhj/dot_general | solution.py:128
  120.6 2.2 %fusion.9 = f32[32,4,1,32]{3,2,1,0:T(1,128)S(1)} fusion(bf16[32,4,4,8,256]{4,3,2,1,0:T(8,128)(2,1)} %bitcast.204, bf16[32,4,256,1]{2,0,1,3:T(8,128)(2,1)S(1)} %get-tuple-element.25), kind=kOutput, calls=%fused_computation.13 | convolution fusion | flops 2097152 | bytes 2179072 | tf_op jit(solution)/shard_map/rhd,rthd->rht/dot_general | solution.py:136
  123.1 2.9 %fusion.21 = f32[2,16,4,256]{3,1,2,0:T(8,128)S(1)} fusion(bf16[2,128,4,8,256]{4,3,2,1,0:T(8,128)(2,1)} %bitcast.177, f32[2,16,4,1024]{3,1,2,0:T(8,128)S(1)} %get-tuple-element.32, f32[2,16,4]{1,2,0:T(4,128)S(1)} %copy.143), kind=kOutput, calls=%fused_computation.23 | convolution fusion | flops 67371008 | bytes 4850176 | tf_op jit(solution)/shard_map/gqhj,gjhd->gqhd/dot_general | solution.py:154
  126.5 2.0 %fusion.6 = f32[32,4,1,256]{3,2,1,0:T(1,128)S(1)} fusion(bf16[32,4,4,8,256]{4,3,2,1,0:T(8,128)(2,1)} %bitcast.205, bf16[32,4,32,1]{2,0,1,3:T(8,128)(2,1)S(1)} %get-tuple-element.28), kind=kOutput, calls=%fused_computation.10 | convolution fusion | flops 2097152 | bytes 2236416 | tf_op jit(solution)/shard_map/rht,rthd->rhd/dot_general | solution.py:161
  128.5 6.5 %fusion.51 = bf16[1024,128]{1,0:T(8,128)(2,1)} fusion(bf16[1024,4096]{1,0:T(8,128)(2,1)} %all-gather.2.cloned.1.call-done, bf16[4096,128]{1,0:T(8,128)(2,1)S(1)} %copy-done, f32[128]{0:T(128)S(1)} %copy-done.12), kind=kOutput, calls=%fused_computation.58 | convolution fusion | flops 1075052544 | bytes 9699840 | tf_op jit(solution)/shard_map/dot_general | solution.py:181
  137.8 5.0 %all-to-all-start.2 = ((bf16[32,2,512]{2,1,0:T(2,128)(2,1)}), bf16[32,2,512]{2,1,0:T(2,128)(2,1)S(1)}, u32[]{:S(2)}, u32[]{:S(2)}) async-start(bf16[32,2,512]{2,1,0:T(2,128)(2,1)} %reshape.342), calls=%async_computation.2 | async-start | bytes 131072 | tf_op jit(solution)/shard_map/all_to_all | solution.py:169
  143.2 7.1 %all-to-all-done.2 = bf16[32,2,512]{2,1,0:T(2,128)(2,1)S(1)} async-done(((bf16[32,2,512]{2,1,0:T(2,128)(2,1)}), bf16[32,2,512]{2,1,0:T(2,128)(2,1)S(1)}, u32[]{:S(2)}, u32[]{:S(2)}) %all-to-all-start.2) | async-done | bytes 65568 | tf_op jit(solution)/shard_map/all_to_all | solution.py:169
  152.7 1.8 collective-permute-start.14
  154.5 1.9 collective-permute-start.12
  157.0 2.7 %fusion.24 = f32[1024,1024,1]{1,0,2:T(8,128)S(1)} fusion(bf16[1,1024,128]{2,1,0:T(8,128)(2,1)} %bitcast.9, bf16[1,1024,128]{2,1,0:T(8,128)(2,1)} %bitcast.8, bf16[1,1024,128]{2,1,0:T(8,128)(2,1)} %bitcast.7, bf16[1,1024,128]{2,1,0:T(8,128)(2,1)} %bitcast.6, bf16[1,128,1024]{2,1,0:T(8,128)(2,1)} %bitcast.17, bf16[1,128,1024]{2,1,0:T(8,128)(2,1)} %bitcast.15, ...), kind=kOutput, calls=%fused_computation.25 | convolution fusion | flops 1076887552 | bytes 6291456 | tf_op jit(solution)/shard_map/dot_general | solution.py:190
  163.5 2.5 %collective-permute-start.16 = (bf16[1024,512]{1,0:T(8,128)(2,1)S(1)}, bf16[1024,512]{1,0:T(8,128)(2,1)S(1)}, u32[]{:S(2)}, u32[]{:S(2)}) collective-permute-start(bf16[1024,512]{1,0:T(8,128)(2,1)S(1)} %dynamic-slice_convert_fusion), channel_id=1, source_target_pairs={{0,4},{4,0},{8,12},{12,8},{16,20},{20,16},{24,28},{28,24},{32,36},... | collective-permute-start | bytes 3145736 | tf_op jit(solution)/shard_map/ppermute | solution.py:196
  166.0 2.3 %collective-permute-done.16 = bf16[1024,512]{1,0:T(8,128)(2,1)S(1)} collective-permute-done((bf16[1024,512]{1,0:T(8,128)(2,1)S(1)}, bf16[1024,512]{1,0:T(8,128)(2,1)S(1)}, u32[]{:S(2)}, u32[]{:S(2)}) %collective-permute-start.16) | collective-permute-done | bytes 1048608 | tf_op jit(solution)/shard_map/ppermute | solution.py:196
  169.6 4.0 %all-to-all-start.3 = ((bf16[32,32,512]{2,1,0:T(8,128)(2,1)}), bf16[32,32,512]{2,1,0:T(8,128)(2,1)S(1)}, u32[]{:S(2)}, u32[]{:S(2)}) async-start(bf16[32,32,512]{2,1,0:T(8,128)(2,1)} %bitcast.57), calls=%async_computation.3 | async-start | bytes 2097152 | tf_op jit(solution)/shard_map/all_to_all | solution.py:200
  173.6 17.1 %all-to-all-done.3 = bf16[32,32,512]{2,1,0:T(8,128)(2,1)S(1)} async-done(((bf16[32,32,512]{2,1,0:T(8,128)(2,1)}), bf16[32,32,512]{2,1,0:T(8,128)(2,1)S(1)}, u32[]{:S(2)}, u32[]{:S(2)}) %all-to-all-start.3) | async-done | bytes 1048608 | tf_op jit(solution)/shard_map/all_to_all | solution.py:200
  (149 shorter events, 38.1 us)
Async XLA Ops:
  6.5 122.0 %copy-start = (bf16[4096,128]{1,0:T(8,128)(2,1)S(1)}, bf16[4096,128]{1,0:T(8,128)(2,1)}, u32[]{:S(2)}) copy-start(bf16[4096,128]{1,0:T(8,128)(2,1)} %param.26) | copy-start | bytes 3145732
  6.5 122.0 %all-gather.2.cloned.1.call-start = ((), (), s32[]{:S(2)}) async-start(), calls=%async_computation.4 | async-start | bytes 8650752 | tf_op jit(solution)/shard_map/all_gather | solution.py:88
  6.5 6.5 %collective-permute-start = (bf16[32,1024]{1,0:T(8,128)(2,1)}, bf16[32,1024]{1,0:T(8,128)(2,1)S(1)}, u32[]{:S(2)}, u32[]{:S(2)}) collective-permute-start(bf16[32,1024]{1,0:T(8,128)(2,1)} %param.15), channel_id=1, source_target_pairs={{0,1},{1,2},{2,3},{3,0},{4,5},{5,6},{6,7},{7,4},{8,9},{9,10},{10,1... | collective-permute-start | bytes 196616 | tf_op jit(solution)/shard_map/ppermute | solution.py:57
  8.6 4.5 %collective-permute-start.2 = (bf16[32,1024]{1,0:T(8,128)(2,1)}, bf16[32,1024]{1,0:T(8,128)(2,1)S(1)}, u32[]{:S(2)}, u32[]{:S(2)}) collective-permute-start(bf16[32,1024]{1,0:T(8,128)(2,1)} %param.15), channel_id=1, source_target_pairs={{0,3},{1,0},{2,1},{3,2},{4,7},{5,4},{6,5},{7,6},{8,11},{9,8},{10,9... | collective-permute-start | bytes 196616 | tf_op jit(solution)/shard_map/ppermute | solution.py:57
  10.0 4.8 %collective-permute-start.1 = (bf16[32,1024]{1,0:T(8,128)(2,1)}, bf16[32,1024]{1,0:T(8,128)(2,1)S(1)}, u32[]{:S(2)}, u32[]{:S(2)}) collective-permute-start(bf16[32,1024]{1,0:T(8,128)(2,1)} %param.15), channel_id=1, source_target_pairs={{0,2},{1,3},{2,0},{3,1},{4,6},{5,7},{6,4},{7,5},{8,10},{9,11},{10,... | collective-permute-start | bytes 196616 | tf_op jit(solution)/shard_map/ppermute | solution.py:57
  19.8 24.7 %all-to-all-start = ((bf16[32,32,256]{2,0,1:T(8,128)(2,1)}), bf16[32,32,256]{2,0,1:T(8,128)(2,1)S(1)}, u32[]{:S(2)}, u32[]{:S(2)}) async-start(bf16[32,32,256]{2,0,1:T(8,128)(2,1)} %bitcast.19), calls=%async_computation | async-start | bytes 1048576 | tf_op jit(solution)/shard_map/all_to_all | solution.py:91
  30.5 1.8 collective-permute-start.9
  47.6 61.6 %all-to-all-start.1 = ((bf16[32,32,3,512]{3,1,2,0:T(8,128)(2,1)}), bf16[32,32,3,512]{3,1,2,0:T(8,128)(2,1)}, u32[]{:S(2)}, u32[]{:S(2)}) async-start(bf16[32,32,3,512]{3,1,2,0:T(8,128)(2,1)} %copy.131), calls=%async_computation.1 | async-start | bytes 6291456 | tf_op jit(solution)/shard_map/all_to_all | solution.py:107
  54.2 81.2 %collective-permute-start.15 = (bf16[8,4,1024]{2,0,1:T(8,128)(2,1)}, bf16[8,4,1024]{2,0,1:T(8,128)(2,1)}, u32[]{:S(2)}, u32[]{:S(2)}) collective-permute-start(bf16[8,4,1024]{2,0,1:T(8,128)(2,1)} %bitcast.172), channel_id=1, source_target_pairs={{0,3},{1,0},{2,1},{3,2},{4,7},{5,4},{6,5},{7,6},{8,11},{9,8},{10,9... | collective-permute-start | bytes 196616 | tf_op jit(solution)/shard_map/ppermute | solution.py:44
  58.7 77.3 %collective-permute-start.8 = (bf16[128,1024]{1,0:T(8,128)(2,1)}, bf16[128,1024]{1,0:T(8,128)(2,1)}, u32[]{:S(2)}, u32[]{:S(2)}) collective-permute-start(bf16[128,1024]{1,0:T(8,128)(2,1)} %bitcast.167), channel_id=1, source_target_pairs={{0,3},{1,0},{2,1},{3,2},{4,7},{5,4},{6,5},{7,6},{8,11},{9,8},{10,9... | collective-permute-start | bytes 786440 | tf_op jit(solution)/shard_map/ppermute | solution.py:44
  59.5 91.7 %collective-permute-start.6 = (bf16[128,1024]{1,0:T(8,128)(2,1)S(1)}, bf16[128,1024]{1,0:T(8,128)(2,1)}, u32[]{:S(2)}, u32[]{:S(2)}) collective-permute-start(bf16[128,1024]{1,0:T(8,128)(2,1)S(1)} %bitcast.193), channel_id=1, source_target_pairs={{0,1},{1,2},{2,3},{3,0},{4,5},{5,6},{6,7},{7,4},{8,9},{9,10},{10,1... | collective-permute-start | bytes 786440 | tf_op jit(solution)/shard_map/ppermute | solution.py:44
  60.5 92.2 %collective-permute-start.7 = (bf16[128,1024]{1,0:T(8,128)(2,1)S(1)}, bf16[128,1024]{1,0:T(8,128)(2,1)}, u32[]{:S(2)}, u32[]{:S(2)}) collective-permute-start(bf16[128,1024]{1,0:T(8,128)(2,1)S(1)} %bitcast.192), channel_id=1, source_target_pairs={{0,2},{1,3},{2,0},{3,1},{4,6},{5,7},{6,4},{7,5},{8,10},{9,11},{10,... | collective-permute-start | bytes 786440 | tf_op jit(solution)/shard_map/ppermute | solution.py:44
  135.0 19.5 %collective-permute-start.5 = (bf16[1024,128]{1,0:T(8,128)(2,1)}, bf16[1024,128]{1,0:T(8,128)(2,1)}, u32[]{:S(2)}, u32[]{:S(2)}) collective-permute-start(bf16[1024,128]{1,0:T(8,128)(2,1)} %fusion.51), channel_id=1, source_target_pairs={{0,3},{1,0},{2,1},{3,2},{4,7},{5,4},{6,5},{7,6},{8,11},{9,8},{10,9... | collective-permute-start | bytes 786440 | tf_op jit(solution)/shard_map/ppermute | solution.py:57
  135.4 21.0 %collective-permute-start.4 = (bf16[1024,128]{1,0:T(8,128)(2,1)}, bf16[1024,128]{1,0:T(8,128)(2,1)}, u32[]{:S(2)}, u32[]{:S(2)}) collective-permute-start(bf16[1024,128]{1,0:T(8,128)(2,1)} %fusion.51), channel_id=1, source_target_pairs={{0,2},{1,3},{2,0},{3,1},{4,6},{5,7},{6,4},{7,5},{8,10},{9,11},{10,... | collective-permute-start | bytes 786440 | tf_op jit(solution)/shard_map/ppermute | solution.py:57
  136.1 20.3 %collective-permute-start.3 = (bf16[1024,128]{1,0:T(8,128)(2,1)}, bf16[1024,128]{1,0:T(8,128)(2,1)}, u32[]{:S(2)}, u32[]{:S(2)}) collective-permute-start(bf16[1024,128]{1,0:T(8,128)(2,1)} %fusion.51), channel_id=1, source_target_pairs={{0,1},{1,2},{2,3},{3,0},{4,5},{5,6},{6,7},{7,4},{8,9},{9,10},{10,1... | collective-permute-start | bytes 786440 | tf_op jit(solution)/shard_map/ppermute | solution.py:57
  137.8 12.5 %all-to-all-start.2 = ((bf16[32,2,512]{2,1,0:T(2,128)(2,1)}), bf16[32,2,512]{2,1,0:T(2,128)(2,1)S(1)}, u32[]{:S(2)}, u32[]{:S(2)}) async-start(bf16[32,2,512]{2,1,0:T(2,128)(2,1)} %reshape.342), calls=%async_computation.2 | async-start | bytes 131072 | tf_op jit(solution)/shard_map/all_to_all | solution.py:169
  151.2 8.6 %collective-permute-start.13 = (bf16[8,4,1024]{2,0,1:T(8,128)(2,1)S(1)}, bf16[8,4,1024]{2,0,1:T(8,128)(2,1)S(1)}, u32[]{:S(2)}, u32[]{:S(2)}) collective-permute-start(bf16[8,4,1024]{2,0,1:T(8,128)(2,1)S(1)} %bitcast.200), channel_id=1, source_target_pairs={{0,1},{1,2},{2,3},{3,0},{4,5},{5,6},{6,7},{7,4},{8,9},{9,10},{10,1... | collective-permute-start | bytes 196616 | tf_op jit(solution)/shard_map/ppermute | solution.py:44
  152.7 7.1 %collective-permute-start.14 = (bf16[8,4,1024]{2,0,1:T(8,128)(2,1)S(1)}, bf16[8,4,1024]{2,0,1:T(8,128)(2,1)S(1)}, u32[]{:S(2)}, u32[]{:S(2)}) collective-permute-start(bf16[8,4,1024]{2,0,1:T(8,128)(2,1)S(1)} %bitcast.199), channel_id=1, source_target_pairs={{0,2},{1,3},{2,0},{3,1},{4,6},{5,7},{6,4},{7,5},{8,10},{9,11},{10,... | collective-permute-start | bytes 196616 | tf_op jit(solution)/shard_map/ppermute | solution.py:44
  154.5 5.3 %collective-permute-start.12 = (bf16[8,4,1024]{2,0,1:T(8,128)(2,1)S(1)}, bf16[8,4,1024]{2,0,1:T(8,128)(2,1)S(1)}, u32[]{:S(2)}, u32[]{:S(2)}) collective-permute-start(bf16[8,4,1024]{2,0,1:T(8,128)(2,1)S(1)} %all_to_all.37), channel_id=1, source_target_pairs={{0,3},{1,0},{2,1},{3,2},{4,7},{5,4},{6,5},{7,6},{8,11},{9,8},{10,9... | collective-permute-start | bytes 196616 | tf_op jit(solution)/shard_map/ppermute | solution.py:57
  156.4 4.7 %collective-permute-start.11 = (bf16[8,4,1024]{2,0,1:T(8,128)(2,1)S(1)}, bf16[8,4,1024]{2,0,1:T(8,128)(2,1)S(1)}, u32[]{:S(2)}, u32[]{:S(2)}) collective-permute-start(bf16[8,4,1024]{2,0,1:T(8,128)(2,1)S(1)} %all_to_all.37), channel_id=1, source_target_pairs={{0,2},{1,3},{2,0},{3,1},{4,6},{5,7},{6,4},{7,5},{8,10},{9,11},{10,... | collective-permute-start | bytes 196616 | tf_op jit(solution)/shard_map/ppermute | solution.py:57
  156.4 5.3 %collective-permute-start.10 = (bf16[8,4,1024]{2,0,1:T(8,128)(2,1)S(1)}, bf16[8,4,1024]{2,0,1:T(8,128)(2,1)S(1)}, u32[]{:S(2)}, u32[]{:S(2)}) collective-permute-start(bf16[8,4,1024]{2,0,1:T(8,128)(2,1)S(1)} %all_to_all.37), channel_id=1, source_target_pairs={{0,1},{1,2},{2,3},{3,0},{4,5},{5,6},{6,7},{7,4},{8,9},{9,10},{10,1... | collective-permute-start | bytes 196616 | tf_op jit(solution)/shard_map/ppermute | solution.py:57
  163.5 27.4 %copy-start.4 = (bf16[32,1024]{1,0:T(8,128)(2,1)S(1)}, bf16[32,1024]{1,0:T(8,128)(2,1)}, u32[]{:S(2)}) copy-start(bf16[32,1024]{1,0:T(8,128)(2,1)} %param.15) | copy-start | bytes 196612
  163.5 4.8 %collective-permute-start.16 = (bf16[1024,512]{1,0:T(8,128)(2,1)S(1)}, bf16[1024,512]{1,0:T(8,128)(2,1)S(1)}, u32[]{:S(2)}, u32[]{:S(2)}) collective-permute-start(bf16[1024,512]{1,0:T(8,128)(2,1)S(1)} %dynamic-slice_convert_fusion), channel_id=1, source_target_pairs={{0,4},{4,0},{8,12},{12,8},{16,20},{20,16},{24,28},{28,24},{32,36},... | collective-permute-start | bytes 3145736 | tf_op jit(solution)/shard_map/ppermute | solution.py:196
  169.6 21.1 %all-to-all-start.3 = ((bf16[32,32,512]{2,1,0:T(8,128)(2,1)}), bf16[32,32,512]{2,1,0:T(8,128)(2,1)S(1)}, u32[]{:S(2)}, u32[]{:S(2)}) async-start(bf16[32,32,512]{2,1,0:T(8,128)(2,1)} %bitcast.57), calls=%async_computation.3 | async-start | bytes 2097152 | tf_op jit(solution)/shard_map/all_to_all | solution.py:200
  (11 other events, 89.2 us)
Sparse Core Ops, SparseCore 0:
  18.0 90.7 all-gather.1

commit v12 on v6

--- a/solution.py
+++ b/solution.py
@@ -100,18 +100,23 @@
     term = jnp.einsum(
         "rf,fch->rch", columns, pair_weights, preferred_element_type=jnp.float32
     ).astype(jnp.bfloat16)
-    received = lax.all_to_all(
-        term.reshape(grp_count, local_rows, 3, half), "grp", 0, 0, tiled=True
-    ).reshape(grp_count // 2, 2, local_rows, 3, half)
-    qkv = jnp.sum(received.astype(jnp.float32), axis=0)
-    qkv = jnp.transpose(qkv, (1, 2, 0, 3)).reshape(local_rows, 3, 2 * half)
+    def exchange(part):
+        which = part.shape[1]
+        got = lax.all_to_all(
+            part.reshape(grp_count, local_rows, which, half), "grp", 0, 0, tiled=True
+        ).reshape(grp_count // 2, 2, local_rows, which, half)
+        got = jnp.sum(got.astype(jnp.float32), axis=0)
+        return jnp.transpose(got, (1, 2, 0, 3)).reshape(local_rows, which, 2 * half)
+
+    q_sum = exchange(term[:, :1])
+    kv_sum = exchange(term[:, 1:])
     heads_here = w_qkv.shape[2] // HS
     member = (jnp.arange(local_rows) // GSIZE)[:, None] == jnp.arange(groups_here)[None, :]
     row_prompt = jnp.sum(jnp.where(member, prompt_len[None, :], 0), axis=1)
     positions = (row_prompt + own_len).astype(jnp.float32)
-    query = rotate(qkv[:, 0].reshape(local_rows, heads_here, HS), positions).astype(jnp.bfloat16)
-    key_new = rotate(qkv[:, 1].reshape(local_rows, heads_here, HS), positions).astype(jnp.bfloat16)
-    value_new = qkv[:, 2].reshape(local_rows, heads_here, HS).astype(jnp.bfloat16)
+    query = rotate(q_sum[:, 0].reshape(local_rows, heads_here, HS), positions).astype(jnp.bfloat16)
+    key_new = rotate(kv_sum[:, 0].reshape(local_rows, heads_here, HS), positions).astype(jnp.bfloat16)
+    value_new = kv_sum[:, 1].reshape(local_rows, heads_here, HS).astype(jnp.bfloat16)
     scale = 1.0 / math.sqrt(HS)
     longest = prefix_keys.shape[1]
     own_count = own_keys.shape[1]

time: 194 us -> 198 us (1.021)
  waiting for transfers between devices: 84.7 us -> 64.2 us
  starting transfers between devices: 41.8 us -> 54.5 us
  local copies, waits for them, and re-layouts: 14.8 us -> 24.7 us
  matrix products: 21.4 us -> 23.5 us
    all_to_all x1, waiting for transfers between devices: 12.2 us -> 0.4 us  [local(): lax.all_to_all(jnp.repeat(pair_rows, 2, axis=1), 'grp', split_axis=1, con...]
    all_to_all x1 -> x2, starting transfers between devices: 4.95 us -> 14.6 us  [exchange(): lax.all_to_all(part.reshape(grp_count, local_rows, which, half), 'grp', 0...]
    all_to_all x1 -> x2, waiting for transfers between devices: 39.9 us -> 32.9 us  [exchange(): lax.all_to_all(part.reshape(grp_count, local_rows, which, half), 'grp', 0...]
    dynamic_slice x6, local copies, waits for them, and re-layouts: 1.98 us -> 5.78 us  [head_exchange(): lax.dynamic_index_in_dim(pieces, (here + shift) % count, axis, keepdims=F...]
    unnamed x34 -> x51, local copies, waits for them, and re-layouts: 4.14 us -> 6.33 us
    dynamic_slice x1, local copies, waits for them, and re-layouts: 0.08 us -> 2.16 us  [local(): own = lax.dynamic_slice_in_dim(w_qkv, parity * half, half, axis=2)]
  transfers between devices with their start and end apart: 20 -> 21, of which waited for: 10 -> 10; matrix products, arithmetic and copies ran while one was open for 22% -> 27% of each run, Pallas kernels for 0% -> 0%
where the time goes in v12:
time: 198 us; the launch traced here: 197 us
  waiting for transfers between devices  64.2 us (32%)
  starting transfers between devices  54.5 us (28%)
  local copies, waits for them, and re-layouts  24.7 us (12%)
  matrix products  23.5 us (12%)
  other arithmetic  15.9 us (8%)
  between operations  14.3 us (7%)
    all_to_all x2, waiting for transfers between devices, exchange(): lax.all_to_all(part.reshape(grp_count, local_rows, which, half), 'grp', 0...  32.9 us
    all_to_all x1, waiting for transfers between devices, local(): lax.all_to_all(pair_sum.reshape(grp_count, local_rows, half_width), 'grp'...  17 us
    all_to_all x2, starting transfers between devices, exchange(): lax.all_to_all(part.reshape(grp_count, local_rows, which, half), 'grp', 0...  14.6 us
    all_to_all x1, starting transfers between devices, local(): lax.all_to_all(jnp.repeat(pair_rows, 2, axis=1), 'grp', split_axis=1, con...  10.6 us
    ppermute x6, starting transfers between devices, head_gather(): lax.ppermute(piece, 'head', [(i, (i + shift) % count) for i in range(coun...  8.49 us
    ppermute x6, starting transfers between devices, head_exchange(): lax.ppermute(piece, 'head', [(i, (i + shift) % count) for i in range(coun...  6.94 us
    dot_general x1, matrix products, local(): jnp.dot(gathered, w_in, preferred_element_type=jnp.float32)  6.52 us
    all_to_all x1, starting transfers between devices, local(): lax.all_to_all(pair_sum.reshape(grp_count, local_rows, half_width), 'grp'...  6.34 us
  transfers between devices with their start and end apart: 21, of which 10 were waited for; matrix products, arithmetic and copies ran while one was open for 27% of the time, Pallas kernels for 0%

profile of v12, /device:TPU:1, one launch (start us, length us, event | category | flops | bytes accessed | tf_op | source)
XLA Modules:
  0.0 197.0 jit_solution(15052190357203412155)
XLA Ops:
  6.5 2.1 %collective-permute-start = (bf16[32,1024]{1,0:T(8,128)(2,1)}, bf16[32,1024]{1,0:T(8,128)(2,1)S(1)}, u32[]{:S(2)}, u32[]{:S(2)}) collective-permute-start(bf16[32,1024]{1,0:T(8,128)(2,1)} %param.17), channel_id=1, source_target_pairs={{0,1},{1,2},{2,3},{3,0},{4,5},{5,6},{6,7},{7,4},{8,9},{9,10},{10,1... | collective-permute-start | bytes 196616 | tf_op jit(solution)/shard_map/ppermute | solution.py:55
  13.1 1.7 collective-permute-done.1
  19.7 10.6 %all-to-all-start = ((bf16[32,32,256]{2,0,1:T(8,128)(2,1)}), bf16[32,32,256]{2,0,1:T(8,128)(2,1)}, u32[]{:S(2)}, u32[]{:S(2)}) async-start(bf16[32,32,256]{2,0,1:T(8,128)(2,1)} %bitcast.16), calls=%async_computation | async-start | bytes 1048576 | tf_op jit(solution)/shard_map/all_to_all | solution.py:87
  30.4 2.2 %constant_dynamic-slice_fusion.5 = (bf16[128,3,512]{2,0,1:T(8,128)(2,1)}, bf16[128,3,512]{2,0,1:T(8,128)(2,1)}) fusion(bf16[128,3,1024]{2,0,1:T(8,128)(2,1)} %param.20, s32[]{:T(128)S(6)} %select_n.163, s32[]{:T(128)S(6)} %select_n.164), kind=kLoop, calls=%fused_computation.114 | loop fusion | bytes 1572872 | tf_op jit(solution)/shard_map/dynamic_slice | solution.py:92
  44.5 2.3 %convolution_convert_fusion = bf16[1024,3,512]{2,0,1:T(8,128)(2,1)S(1)} fusion(bf16[1024,256,1]{1,0,2:T(8,128)(2,1)} %bitcast.20, bf16[128,3,512]{2,0,1:T(8,128)(2,1)} %collective-permute-done.6, bf16[128,3,512]{2,0,1:T(8,128)(2,1)S(1)} %copy-done.6, pred[]{:T(512)S(6)} %eq.31), kind=kOutput, calls=%fused_computation.12 | convolution fusion | flops 810418176 | bytes 4456449 | tf_op jit(solution)/shard_map/rf,fch->rch/dot_general | solution.py:100
  49.5 8.2 %all-to-all-start.1 = ((bf16[32,32,1,512]{3,1,2,0:T(8,128)(2,1)}), bf16[32,32,1,512]{3,1,2,0:T(8,128)(2,1)}, u32[]{:S(2)}, u32[]{:S(2)}) async-start(bf16[32,32,1,512]{3,1,2,0:T(8,128)(2,1)} %bitcast.22), calls=%async_computation.1 | async-start | bytes 2097152 | tf_op jit(solution)/shard_map/all_to_all | solution.py:105
  60.2 1.8 copy.132
  65.3 18.9 %all-to-all-done.1 = bf16[32,32,1,512]{3,1,2,0:T(8,128)(2,1)} async-done(((bf16[32,32,1,512]{3,1,2,0:T(8,128)(2,1)}), bf16[32,32,1,512]{3,1,2,0:T(8,128)(2,1)}, u32[]{:S(2)}, u32[]{:S(2)}) %all-to-all-start.1) | async-done | bytes 1048608 | tf_op jit(solution)/shard_map/all_to_all | solution.py:105
  84.2 6.5 %all-to-all-start.2 = ((bf16[32,32,2,512]{3,1,2,0:T(8,128)(2,1)}), bf16[32,32,2,512]{3,1,2,0:T(8,128)(2,1)S(1)}, u32[]{:S(2)}, u32[]{:S(2)}) async-start(bf16[32,32,2,512]{3,1,2,0:T(8,128)(2,1)} %copy.147), calls=%async_computation.2 | async-start | bytes 4194304 | tf_op jit(solution)/shard_map/all_to_all | solution.py:105
  91.5 1.8 collective-permute-start.5
  98.1 4.2 %fusion.73 = (f32[2,16,4]{1,2,0:T(4,128)S(1)}, f32[2,16,4,1024]{3,1,2,0:T(8,128)}) fusion(bf16[2,128,4,8,256]{4,3,2,1,0:T(8,128)(2,1)} %bitcast.180, bf16[2,16,4,192]{3,1,2,0:T(8,128)(2,1)S(1)} %copy.143, bf16[2,16,4,64]{3,1,2,0:T(8,128)(2,1)S(1)} %copy.142, pred[2,1024]{1,0:T(4,128)(4,1)S(1)} %iota_compare_fusion.1), kind=kOutput, calls=%fused_computation.151 | convolution fusion | flops 67633024 | bytes 4786688 | tf_op jit(solution)/shard_map/gqhd,gjhd->gqhj/dot_general | solution.py:129
  102.6 2.2 %fusion.9 = f32[32,4,1,32]{3,2,1,0:T(1,128)S(1)} fusion(bf16[32,4,4,8,256]{4,3,2,1,0:T(8,128)(2,1)} %bitcast.207, bf16[32,4,256,1]{2,1,0,3:T(4,128)(2,1)S(1)} %get-tuple-element.24), kind=kOutput, calls=%fused_computation.16 | convolution fusion | flops 2097152 | bytes 2179072 | tf_op jit(solution)/shard_map/rhd,rthd->rht/dot_general | solution.py:137
  104.9 14.1 %all-to-all-done.2 = bf16[32,32,2,512]{3,1,2,0:T(8,128)(2,1)S(1)} async-done(((bf16[32,32,2,512]{3,1,2,0:T(8,128)(2,1)}), bf16[32,32,2,512]{3,1,2,0:T(8,128)(2,1)S(1)}, u32[]{:S(2)}, u32[]{:S(2)}) %all-to-all-start.2) | async-done | bytes 2097184 | tf_op jit(solution)/shard_map/all_to_all | solution.py:105
  122.0 2.0 %fusion.6 = f32[32,4,1,256]{3,2,1,0:T(1,128)S(1)} fusion(bf16[32,4,4,8,256]{4,3,2,1,0:T(8,128)(2,1)} %bitcast.208, bf16[32,4,32,1]{2,0,1,3:T(8,128)(2,1)S(1)} %get-tuple-element.27), kind=kOutput, calls=%fused_computation.13 | convolution fusion | flops 2097152 | bytes 2236416 | tf_op jit(solution)/shard_map/rht,rthd->rhd/dot_general | solution.py:162
  124.0 6.5 %fusion.37 = bf16[1024,128]{1,0:T(8,128)(2,1)} fusion(bf16[1024,4096]{1,0:T(8,128)(2,1)} %all-gather.3.cloned.1.call-done, bf16[4096,128]{1,0:T(8,128)(2,1)S(1)} %copy-done, f32[128]{0:T(128)S(1)} %copy-done.20), kind=kOutput, calls=%fused_computation.49 | convolution fusion | flops 1075052544 | bytes 9699840 | tf_op jit(solution)/shard_map/dot_general | solution.py:182
  130.6 2.9 %fusion.21 = f32[2,16,4,256]{3,1,2,0:T(8,128)S(1)} fusion(bf16[2,128,4,8,256]{4,3,2,1,0:T(8,128)(2,1)} %bitcast.182, f32[2,16,4,1024]{3,1,2,0:T(8,128)S(1)} %copy-done.3, f32[2,16,4]{1,2,0:T(4,128)S(1)} %copy.153), kind=kOutput, calls=%fused_computation.27 | convolution fusion | flops 67371008 | bytes 4850176 | tf_op jit(solution)/shard_map/gqhj,gjhd->gqhd/dot_general | solution.py:155
  134.8 5.6 %all-to-all-start.3 = ((bf16[32,2,512]{2,1,0:T(2,128)(2,1)}), bf16[32,2,512]{2,1,0:T(2,128)(2,1)S(1)}, u32[]{:S(2)}, u32[]{:S(2)}) async-start(bf16[32,2,512]{2,1,0:T(2,128)(2,1)} %reshape.404), calls=%async_computation.3 | async-start | bytes 131072 | tf_op jit(solution)/shard_map/all_to_all | solution.py:170
  142.4 5.5 %all-to-all-done.3 = bf16[32,2,512]{2,1,0:T(2,128)(2,1)S(1)} async-done(((bf16[32,2,512]{2,1,0:T(2,128)(2,1)}), bf16[32,2,512]{2,1,0:T(2,128)(2,1)S(1)}, u32[]{:S(2)}, u32[]{:S(2)}) %all-to-all-start.3) | async-done | bytes 65568 | tf_op jit(solution)/shard_map/all_to_all | solution.py:170
  152.5 2.3 %collective-permute-done.8 = bf16[8,4,1024]{2,0,1:T(8,128)(2,1)S(1)} collective-permute-done((bf16[8,4,1024]{2,0,1:T(8,128)(2,1)S(1)}, bf16[8,4,1024]{2,0,1:T(8,128)(2,1)S(1)}, u32[]{:S(2)}, u32[]{:S(2)}) %collective-permute-start.8) | collective-permute-done | bytes 65568 | tf_op jit(solution)/shard_map/ppermute | solution.py:55
  154.8 1.8 collective-permute-done.7
  157.2 2.5 %fusion.74 = f32[1024,1024]{1,0:T(8,128)S(1)} fusion(bf16[1024,512]{1,0:T(8,128)(2,1)} %all-gather.5.cloned.1.call-done, bf16[512,1024]{1,0:T(8,128)(2,1)S(1)} %bitcast_select_fusion), kind=kOutput, calls=%fused_computation.152 | convolution fusion | flops 1073741824 | bytes 6291456 | tf_op jit(solution)/shard_map/dot_general | solution.py:191
  162.3 2.3 %collective-permute-done.13 = bf16[1024,512]{1,0:T(8,128)(2,1)S(1)} collective-permute-done((bf16[1024,512]{1,0:T(8,128)(2,1)S(1)}, bf16[1024,512]{1,0:T(8,128)(2,1)S(1)}, u32[]{:S(2)}, u32[]{:S(2)}) %collective-permute-start.13) | collective-permute-done | bytes 1048608 | tf_op jit(solution)/shard_map/ppermute | solution.py:197
  165.9 6.3 %all-to-all-start.4 = ((bf16[32,32,512]{2,1,0:T(8,128)(2,1)}), bf16[32,32,512]{2,1,0:T(8,128)(2,1)S(1)}, u32[]{:S(2)}, u32[]{:S(2)}) async-start(bf16[32,32,512]{2,1,0:T(8,128)(2,1)} %bitcast.55), calls=%async_computation.4 | async-start | bytes 2097152 | tf_op jit(solution)/shard_map/all_to_all | solution.py:201
  172.3 17.0 %all-to-all-done.4 = bf16[32,32,512]{2,1,0:T(8,128)(2,1)S(1)} async-done(((bf16[32,32,512]{2,1,0:T(8,128)(2,1)}), bf16[32,32,512]{2,1,0:T(8,128)(2,1)S(1)}, u32[]{:S(2)}, u32[]{:S(2)}) %all-to-all-start.4) | async-done | bytes 1048608 | tf_op jit(solution)/shard_map/all_to_all | solution.py:201
  (179 shorter events, 51.3 us)
Async XLA Ops:
  6.5 117.5 %copy-start = (bf16[4096,128]{1,0:T(8,128)(2,1)S(1)}, bf16[4096,128]{1,0:T(8,128)(2,1)}, u32[]{:S(2)}) copy-start(bf16[4096,128]{1,0:T(8,128)(2,1)} %param.28) | copy-start | bytes 3145732
  6.5 117.5 %all-gather.3.cloned.1.call-start = ((), (), s32[]{:S(2)}) async-start(), calls=%async_computation.5 | async-start | bytes 8650752 | tf_op jit(solution)/shard_map/all_gather | solution.py:84
  6.5 6.6 %collective-permute-start = (bf16[32,1024]{1,0:T(8,128)(2,1)}, bf16[32,1024]{1,0:T(8,128)(2,1)S(1)}, u32[]{:S(2)}, u32[]{:S(2)}) collective-permute-start(bf16[32,1024]{1,0:T(8,128)(2,1)} %param.17), channel_id=1, source_target_pairs={{0,1},{1,2},{2,3},{3,0},{4,5},{5,6},{6,7},{7,4},{8,9},{9,10},{10,1... | collective-permute-start | bytes 196616 | tf_op jit(solution)/shard_map/ppermute | solution.py:55
  8.6 4.5 %collective-permute-start.2 = (bf16[32,1024]{1,0:T(8,128)(2,1)}, bf16[32,1024]{1,0:T(8,128)(2,1)S(1)}, u32[]{:S(2)}, u32[]{:S(2)}) collective-permute-start(bf16[32,1024]{1,0:T(8,128)(2,1)} %param.17), channel_id=1, source_target_pairs={{0,3},{1,0},{2,1},{3,2},{4,7},{5,4},{6,5},{7,6},{8,11},{9,8},{10,9... | collective-permute-start | bytes 196616 | tf_op jit(solution)/shard_map/ppermute | solution.py:55
  10.0 4.8 %collective-permute-start.1 = (bf16[32,1024]{1,0:T(8,128)(2,1)}, bf16[32,1024]{1,0:T(8,128)(2,1)S(1)}, u32[]{:S(2)}, u32[]{:S(2)}) collective-permute-start(bf16[32,1024]{1,0:T(8,128)(2,1)} %param.17), channel_id=1, source_target_pairs={{0,2},{1,3},{2,0},{3,1},{4,6},{5,7},{6,4},{7,5},{8,10},{9,11},{10,... | collective-permute-start | bytes 196616 | tf_op jit(solution)/shard_map/ppermute | solution.py:55
  13.1 77.6 %copy-start.13 = (pred[4]{0:T(512)(128)(4,1)}, pred[4]{0:T(512)(128)(4,1)S(1)}, u32[]{:S(2)}) copy-start(pred[4]{0:T(512)(128)(4,1)S(1)} %compare_and_fusion) | copy-start | bytes 16
  19.7 24.8 %all-to-all-start = ((bf16[32,32,256]{2,0,1:T(8,128)(2,1)}), bf16[32,32,256]{2,0,1:T(8,128)(2,1)}, u32[]{:S(2)}, u32[]{:S(2)}) async-start(bf16[32,32,256]{2,0,1:T(8,128)(2,1)} %bitcast.16), calls=%async_computation | async-start | bytes 1048576 | tf_op jit(solution)/shard_map/all_to_all | solution.py:87
  32.5 10.9 %collective-permute-start.6 = (bf16[128,3,512]{2,0,1:T(8,128)(2,1)}, bf16[128,3,512]{2,0,1:T(8,128)(2,1)}, u32[]{:S(2)}, u32[]{:S(2)}) collective-permute-start(bf16[128,3,512]{2,0,1:T(8,128)(2,1)} %get-tuple-element.13), channel_id=1, source_target_pairs={{0,4},{4,0},{8,12},{12,8},{16,20},{20,16},{24,28},{28,24},{32,36},... | collective-permute-start | bytes 1179656 | tf_op jit(solution)/shard_map/ppermute | solution.py:94
  34.4 57.1 %collective-permute-start.12 = (bf16[8,4,1024]{2,0,1:T(8,128)(2,1)}, bf16[8,4,1024]{2,0,1:T(8,128)(2,1)}, u32[]{:S(2)}, u32[]{:S(2)}) collective-permute-start(bf16[8,4,1024]{2,0,1:T(8,128)(2,1)} %bitcast.174), channel_id=1, source_target_pairs={{0,3},{1,0},{2,1},{3,2},{4,7},{5,4},{6,5},{7,6},{8,11},{9,8},{10,9... | collective-permute-start | bytes 196616 | tf_op jit(solution)/shard_map/ppermute | solution.py:44
  36.4 57.0 %collective-permute-start.10 = (bf16[8,4,1024]{2,0,1:T(8,128)(2,1)}, bf16[8,4,1024]{2,0,1:T(8,128)(2,1)}, u32[]{:S(2)}, u32[]{:S(2)}) collective-permute-start(bf16[8,4,1024]{2,0,1:T(8,128)(2,1)} %bitcast.176), channel_id=1, source_target_pairs={{0,1},{1,2},{2,3},{3,0},{4,5},{5,6},{6,7},{7,4},{8,9},{9,10},{10,1... | collective-permute-start | bytes 196616 | tf_op jit(solution)/shard_map/ppermute | solution.py:44
  37.3 56.1 %collective-permute-start.11 = (bf16[8,4,1024]{2,0,1:T(8,128)(2,1)}, bf16[8,4,1024]{2,0,1:T(8,128)(2,1)}, u32[]{:S(2)}, u32[]{:S(2)}) collective-permute-start(bf16[8,4,1024]{2,0,1:T(8,128)(2,1)} %bitcast.175), channel_id=1, source_target_pairs={{0,2},{1,3},{2,0},{3,1},{4,6},{5,7},{6,4},{7,5},{8,10},{9,11},{10,... | collective-permute-start | bytes 196616 | tf_op jit(solution)/shard_map/ppermute | solution.py:44
  41.1 99.4 %collective-permute-start.3 = (bf16[128,1024]{1,0:T(8,128)(2,1)}, bf16[128,1024]{1,0:T(8,128)(2,1)}, u32[]{:S(2)}, u32[]{:S(2)}) collective-permute-start(bf16[128,1024]{1,0:T(8,128)(2,1)} %bitcast.9), channel_id=1, source_target_pairs={{0,1},{1,2},{2,3},{3,0},{4,5},{5,6},{6,7},{7,4},{8,9},{9,10},{10,1... | collective-permute-start | bytes 786440 | tf_op jit(solution)/shard_map/ppermute | solution.py:44
  43.5 97.0 %collective-permute-start.4 = (bf16[128,1024]{1,0:T(8,128)(2,1)}, bf16[128,1024]{1,0:T(8,128)(2,1)}, u32[]{:S(2)}, u32[]{:S(2)}) collective-permute-start(bf16[128,1024]{1,0:T(8,128)(2,1)} %bitcast.11), channel_id=1, source_target_pairs={{0,2},{1,3},{2,0},{3,1},{4,6},{5,7},{6,4},{7,5},{8,10},{9,11},{10,... | collective-permute-start | bytes 786440 | tf_op jit(solution)/shard_map/ppermute | solution.py:44
  49.5 34.7 %all-to-all-start.1 = ((bf16[32,32,1,512]{3,1,2,0:T(8,128)(2,1)}), bf16[32,32,1,512]{3,1,2,0:T(8,128)(2,1)}, u32[]{:S(2)}, u32[]{:S(2)}) async-start(bf16[32,32,1,512]{3,1,2,0:T(8,128)(2,1)} %bitcast.22), calls=%async_computation.1 | async-start | bytes 2097152 | tf_op jit(solution)/shard_map/all_to_all | solution.py:105
  84.2 34.8 %all-to-all-start.2 = ((bf16[32,32,2,512]{3,1,2,0:T(8,128)(2,1)}), bf16[32,32,2,512]{3,1,2,0:T(8,128)(2,1)S(1)}, u32[]{:S(2)}, u32[]{:S(2)}) async-start(bf16[32,32,2,512]{3,1,2,0:T(8,128)(2,1)} %copy.147), calls=%async_computation.2 | async-start | bytes 4194304 | tf_op jit(solution)/shard_map/all_to_all | solution.py:105
  90.7 66.6 %all-gather.5.cloned.1.call-start = ((), (), s32[]{:S(2)}) async-start(), calls=%async_computation.6 | async-start | bytes 1310720 | tf_op jit(solution)/shard_map/all_gather | solution.py:190
  91.5 49.0 %collective-permute-start.5 = (bf16[128,1024]{1,0:T(8,128)(2,1)}, bf16[128,1024]{1,0:T(8,128)(2,1)}, u32[]{:S(2)}, u32[]{:S(2)}) collective-permute-start(bf16[128,1024]{1,0:T(8,128)(2,1)} %bitcast.13), channel_id=1, source_target_pairs={{0,3},{1,0},{2,1},{3,2},{4,7},{5,4},{6,5},{7,6},{8,11},{9,8},{10,9... | collective-permute-start | bytes 786440 | tf_op jit(solution)/shard_map/ppermute | solution.py:44
  134.8 13.1 %all-to-all-start.3 = ((bf16[32,2,512]{2,1,0:T(2,128)(2,1)}), bf16[32,2,512]{2,1,0:T(2,128)(2,1)S(1)}, u32[]{:S(2)}, u32[]{:S(2)}) async-start(bf16[32,2,512]{2,1,0:T(2,128)(2,1)} %reshape.404), calls=%async_computation.3 | async-start | bytes 131072 | tf_op jit(solution)/shard_map/all_to_all | solution.py:170
  148.5 4.0 %collective-permute-start.9 = (bf16[8,4,1024]{2,0,1:T(8,128)(2,1)S(1)}, bf16[8,4,1024]{2,0,1:T(8,128)(2,1)S(1)}, u32[]{:S(2)}, u32[]{:S(2)}) collective-permute-start(bf16[8,4,1024]{2,0,1:T(8,128)(2,1)S(1)} %all_to_all.41), channel_id=1, source_target_pairs={{0,3},{1,0},{2,1},{3,2},{4,7},{5,4},{6,5},{7,6},{8,11},{9,8},{10,9... | collective-permute-start | bytes 196616 | tf_op jit(solution)/shard_map/ppermute | solution.py:55
  150.1 4.6 %collective-permute-start.8 = (bf16[8,4,1024]{2,0,1:T(8,128)(2,1)S(1)}, bf16[8,4,1024]{2,0,1:T(8,128)(2,1)S(1)}, u32[]{:S(2)}, u32[]{:S(2)}) collective-permute-start(bf16[8,4,1024]{2,0,1:T(8,128)(2,1)S(1)} %all_to_all.41), channel_id=1, source_target_pairs={{0,2},{1,3},{2,0},{3,1},{4,6},{5,7},{6,4},{7,5},{8,10},{9,11},{10,... | collective-permute-start | bytes 196616 | tf_op jit(solution)/shard_map/ppermute | solution.py:55
  151.6 5.0 %collective-permute-start.7 = (bf16[8,4,1024]{2,0,1:T(8,128)(2,1)S(1)}, bf16[8,4,1024]{2,0,1:T(8,128)(2,1)S(1)}, u32[]{:S(2)}, u32[]{:S(2)}) collective-permute-start(bf16[8,4,1024]{2,0,1:T(8,128)(2,1)S(1)} %all_to_all.41), channel_id=1, source_target_pairs={{0,1},{1,2},{2,3},{3,0},{4,5},{5,6},{6,7},{7,4},{8,9},{9,10},{10,1... | collective-permute-start | bytes 196616 | tf_op jit(solution)/shard_map/ppermute | solution.py:55
  160.6 29.6 %copy-start.1 = (bf16[4096,128]{1,0:T(8,128)(2,1)S(1)}, bf16[4096,128]{1,0:T(8,128)(2,1)}, u32[]{:S(2)}) copy-start(bf16[4096,128]{1,0:T(8,128)(2,1)} %param.28) | copy-start | bytes 3145732
  160.8 3.8 %collective-permute-start.13 = (bf16[1024,512]{1,0:T(8,128)(2,1)S(1)}, bf16[1024,512]{1,0:T(8,128)(2,1)S(1)}, u32[]{:S(2)}, u32[]{:S(2)}) collective-permute-start(bf16[1024,512]{1,0:T(8,128)(2,1)S(1)} %dynamic-slice_convert_fusion), channel_id=1, source_target_pairs={{0,4},{4,0},{8,12},{12,8},{16,20},{20,16},{24,28},{28,24},{32,36},... | collective-permute-start | bytes 3145736 | tf_op jit(solution)/shard_map/ppermute | solution.py:197
  165.9 23.4 %all-to-all-start.4 = ((bf16[32,32,512]{2,1,0:T(8,128)(2,1)}), bf16[32,32,512]{2,1,0:T(8,128)(2,1)S(1)}, u32[]{:S(2)}, u32[]{:S(2)}) async-start(bf16[32,32,512]{2,1,0:T(8,128)(2,1)} %bitcast.55), calls=%async_computation.4 | async-start | bytes 2097152 | tf_op jit(solution)/shard_map/all_to_all | solution.py:201
  (19 other events, 237.7 us)
Sparse Core Ops, SparseCore 0:
  18.0 70.5 all-gather.2
  130.7 25.3 all-gather.4

commit v13 on v6

--- a/solution.py
+++ b/solution.py
@@ -161,10 +161,19 @@
         jnp.float32
     )
     attended = (mixed / denom[..., None]).astype(jnp.bfloat16)
-    transposed = jnp.transpose(attended, (2, 1, 0))
-    slices = lax.all_to_all(transposed, "grp", split_axis=0, concat_axis=2, tiled=True)
-    dim_here = slices.shape[0]
-    slices = jnp.moveaxis(head_gather(slices), 0, 1).reshape(dim_here, heads_here * head_count, -1)
+    dim_here = HS // grp_count
+    outgoing = jnp.broadcast_to(
+        jnp.transpose(attended.reshape(local_rows, heads_here, grp_count, dim_here), (2, 0, 1, 3))[
+            :, None
+        ],
+        (grp_count, head_count, local_rows, heads_here, dim_here),
+    ).reshape(grp_count * head_count, local_rows, heads_here, dim_here)
+    incoming = lax.all_to_all(outgoing, ("grp", "head"), 0, 0, tiled=True).reshape(
+        grp_count, head_count, local_rows, heads_here, dim_here
+    )
+    slices = jnp.transpose(incoming, (4, 1, 3, 0, 2)).reshape(
+        dim_here, head_count * heads_here, grp_count * local_rows
+    )
     out_blocks = head_exchange(
         w_attn_out.reshape(dim_here, heads_here, head_count, width_here), 2
     )

time: 194 us -> 192 us (0.990)
  starting transfers between devices: 41.8 us -> 37.1 us
  local copies, waits for them, and re-layouts: 14.8 us -> 18 us
  waiting for transfers between devices: 84.7 us -> 82.4 us
    all_to_all x1, waiting for transfers between devices: 39.9 us -> 32.3 us  [local(): lax.all_to_all(term.reshape(grp_count, local_rows, 3, half), 'grp', 0, 0,...]
    all_to_all x1, waiting for transfers between devices: 5.53 us -> 12.8 us  [local(): lax.all_to_all(outgoing, ('grp', 'head'), 0, 0, tiled=True)]
    ppermute x6 -> x3, waiting for transfers between devices: 6.15 us -> 1.71 us  [head_gather(): lax.ppermute(piece, 'head', [(i, (i + shift) % count) for i in range(coun...]
    ppermute x6, waiting for transfers between devices: 0.02 us -> 2.59 us  [head_exchange(): lax.ppermute(piece, 'head', [(i, (i + shift) % count) for i in range(coun...]
    ppermute x6 -> x3, starting transfers between devices: 7.16 us -> 5.1 us  [head_gather(): lax.ppermute(piece, 'head', [(i, (i + shift) % count) for i in range(coun...]
    unnamed x34 -> x50, local copies, waits for them, and re-layouts: 4.14 us -> 5.88 us
  transfers between devices with their start and end apart: 20 -> 17, of which waited for: 10 -> 8; matrix products, arithmetic and copies ran while one was open for 22% -> 21% of each run, Pallas kernels for 0% -> 0%
where the time goes in v13:
time: 192 us; the launch traced here: 191 us
  waiting for transfers between devices  82.4 us (43%)
  starting transfers between devices  37.1 us (19%)
  matrix products  21.4 us (11%)
  local copies, waits for them, and re-layouts  18 us (9%)
  other arithmetic  17.4 us (9%)
  between operations  14.3 us (7%)
    all_to_all x1, waiting for transfers between devices, local(): lax.all_to_all(term.reshape(grp_count, local_rows, 3, half), 'grp', 0, 0,...  32.3 us
    all_to_all x1, waiting for transfers between devices, local(): lax.all_to_all(pair_sum.reshape(grp_count, local_rows, half_width), 'grp'...  17 us
    all_to_all x1, waiting for transfers between devices, local(): lax.all_to_all(outgoing, ('grp', 'head'), 0, 0, tiled=True)  12.8 us
    all_to_all x1, waiting for transfers between devices, local(): lax.all_to_all(jnp.repeat(pair_rows, 2, axis=1), 'grp', split_axis=1, con...  12.1 us
    all_to_all x1, starting transfers between devices, local(): lax.all_to_all(jnp.repeat(pair_rows, 2, axis=1), 'grp', split_axis=1, con...  10.6 us
    ppermute x6, starting transfers between devices, head_exchange(): lax.ppermute(piece, 'head', [(i, (i + shift) % count) for i in range(coun...  6.95 us
    dot_general x1, matrix products, local(): jnp.dot(gathered, w_in, preferred_element_type=jnp.float32)  6.47 us
    unnamed x50, local copies, waits for them, and re-layouts  5.88 us
  transfers between devices with their start and end apart: 17, of which 8 were waited for; matrix products, arithmetic and copies ran while one was open for 21% of the time, Pallas kernels for 0%

profile of v13, /device:TPU:1, one launch (start us, length us, event | category | flops | bytes accessed | tf_op | source)
XLA Modules:
  0.0 190.7 jit_solution(12100319529735048736)
XLA Ops:
  6.5 2.1 %collective-permute-start = (bf16[32,1024]{1,0:T(8,128)(2,1)}, bf16[32,1024]{1,0:T(8,128)(2,1)S(1)}, u32[]{:S(2)}, u32[]{:S(2)}) collective-permute-start(bf16[32,1024]{1,0:T(8,128)(2,1)} %param.15), channel_id=1, source_target_pairs={{0,1},{1,2},{2,3},{3,0},{4,5},{5,6},{6,7},{7,4},{8,9},{9,10},{10,1... | collective-permute-start | bytes 196616 | tf_op jit(solution)/shard_map/ppermute | solution.py:55
  10.0 1.6 collective-permute-start.1
  13.1 1.7 collective-permute-done.1
  19.8 10.6 %all-to-all-start = ((bf16[32,32,256]{2,0,1:T(8,128)(2,1)}), bf16[32,32,256]{2,0,1:T(8,128)(2,1)S(1)}, u32[]{:S(2)}, u32[]{:S(2)}) async-start(bf16[32,32,256]{2,0,1:T(8,128)(2,1)} %bitcast.16), calls=%async_computation | async-start | bytes 1048576 | tf_op jit(solution)/shard_map/all_to_all | solution.py:87
  32.3 12.1 %all-to-all-done = bf16[32,32,256]{2,0,1:T(8,128)(2,1)S(1)} async-done(((bf16[32,32,256]{2,0,1:T(8,128)(2,1)}), bf16[32,32,256]{2,0,1:T(8,128)(2,1)S(1)}, u32[]{:S(2)}, u32[]{:S(2)}) %all-to-all-start) | async-done | bytes 524320 | tf_op jit(solution)/shard_map/all_to_all | solution.py:87
  45.5 2.1 %copy.140 = bf16[32,32,3,512]{3,1,2,0:T(8,128)(2,1)} copy(bf16[32,32,3,512]{3,1,0,2:T(8,128)(2,1)S(1)} %bitcast.166) | data formatting | bytes 6291456 | tf_op jit(solution)/shard_map/reshape | solution.py:104
  47.6 4.9 %all-to-all-start.1 = ((bf16[32,32,3,512]{3,1,2,0:T(8,128)(2,1)}), bf16[32,32,3,512]{3,1,2,0:T(8,128)(2,1)}, u32[]{:S(2)}, u32[]{:S(2)}) async-start(bf16[32,32,3,512]{3,1,2,0:T(8,128)(2,1)} %copy.140), calls=%async_computation.1 | async-start | bytes 6291456 | tf_op jit(solution)/shard_map/all_to_all | solution.py:103
  59.2 1.6 collective-permute-start.3
  66.9 1.8 collective-permute-start.5
  71.7 2.6 %collective-permute-done.4 = bf16[128,1024]{1,0:T(8,128)(2,1)} collective-permute-done((bf16[128,1024]{1,0:T(8,128)(2,1)S(1)}, bf16[128,1024]{1,0:T(8,128)(2,1)}, u32[]{:S(2)}, u32[]{:S(2)}) %collective-permute-start.4) | collective-permute-done | bytes 262176 | tf_op jit(solution)/shard_map/ppermute | solution.py:44
  76.9 32.3 %all-to-all-done.1 = bf16[32,32,3,512]{3,1,2,0:T(8,128)(2,1)} async-done(((bf16[32,32,3,512]{3,1,2,0:T(8,128)(2,1)}), bf16[32,32,3,512]{3,1,2,0:T(8,128)(2,1)}, u32[]{:S(2)}, u32[]{:S(2)}) %all-to-all-start.1) | async-done | bytes 3145760 | tf_op jit(solution)/shard_map/all_to_all | solution.py:103
  109.3 2.5 %convert_reduce_fusion = f32[2,32,3,512]{3,1,2,0:T(8,128)S(1)} fusion(bf16[16,2,32,3,512]{4,2,3,1,0:T(8,128)(2,1)} %bitcast.53), kind=kLoop, calls=%fused_computation.3 | loop fusion | flops 3047424 | bytes 3538944 | tf_op jit(solution)/shard_map/reduce_sum | solution.py:106
  114.2 3.5 %fusion.68 = (f32[2,16,4]{1,2,0:T(4,128)S(1)}, f32[2,16,4,1024]{3,1,2,0:T(8,128)S(1)}) fusion(bf16[2,128,4,8,256]{4,3,2,1,0:T(8,128)(2,1)} %bitcast.161, bf16[2,16,4,64]{3,1,2,0:T(8,128)(2,1)S(1)} %copy.145, pred[2,1024]{1,0:T(4,128)(4,1)S(1)} %copy-done.12, bf16[2,16,4,192]{3,1,0,2:T(8,128)(2,1)S(1)} %bitcast.173), kind=kOutput, calls=%fused_computation.142 | convolution fusion | flops 67633024 | bytes 4786688 | tf_op jit(solution)/shard_map/gqhd,gjhd->gqhj/dot_general | solution.py:124
  117.7 2.2 %fusion.9 = f32[32,4,1,32]{3,2,1,0:T(1,128)S(1)} fusion(bf16[32,4,4,8,256]{4,3,2,1,0:T(8,128)(2,1)} %bitcast.192, bf16[32,4,256,1]{2,0,1,3:T(8,128)(2,1)S(1)} %get-tuple-element.25), kind=kOutput, calls=%fused_computation.15 | convolution fusion | flops 2097152 | bytes 2179072 | tf_op jit(solution)/shard_map/rhd,rthd->rht/dot_general | solution.py:132
  120.2 6.5 %fusion.37 = bf16[1024,128]{1,0:T(8,128)(2,1)} fusion(bf16[1024,4096]{1,0:T(8,128)(2,1)} %all-gather.3.cloned.1.call-done, bf16[4096,128]{1,0:T(8,128)(2,1)S(1)} %copy-done, f32[128]{0:T(128)S(1)} %copy-done.19), kind=kOutput, calls=%fused_computation.47 | convolution fusion | flops 1075052544 | bytes 9699840 | tf_op jit(solution)/shard_map/dot_general | solution.py:186
  126.7 2.9 %fusion.21 = f32[2,16,4,256]{3,1,2,0:T(8,128)S(1)} fusion(bf16[2,128,4,8,256]{4,3,2,1,0:T(8,128)(2,1)} %bitcast.164, f32[2,16,4,1024]{3,1,2,0:T(8,128)S(1)} %get-tuple-element.32, f32[2,16,4]{1,2,0:T(4,128)S(1)} %copy.152), kind=kOutput, calls=%fused_computation.25 | convolution fusion | flops 67371008 | bytes 4850176 | tf_op jit(solution)/shard_map/gqhj,gjhd->gqhd/dot_general | solution.py:150
  130.1 2.0 %fusion.6 = f32[32,4,1,256]{3,2,1,0:T(1,128)S(1)} fusion(bf16[32,4,4,8,256]{4,3,2,1,0:T(8,128)(2,1)} %bitcast.193, bf16[32,4,32,1]{2,0,1,3:T(8,128)(2,1)S(1)} %get-tuple-element.28), kind=kOutput, calls=%fused_computation.12 | convolution fusion | flops 2097152 | bytes 2236416 | tf_op jit(solution)/shard_map/rht,rthd->rhd/dot_general | solution.py:157
  132.7 1.5 reshape.381
  134.2 4.1 %all-to-all-start.2 = ((bf16[128,2,512]{2,1,0:T(2,128)(2,1)}), bf16[128,2,512]{2,1,0:T(2,128)(2,1)S(1)}, u32[]{:S(2)}, u32[]{:S(2)}) async-start(bf16[128,2,512]{2,1,0:T(2,128)(2,1)} %reshape.381), calls=%async_computation.2 | async-start | bytes 524288 | tf_op jit(solution)/shard_map/all_to_all | solution.py:171
  138.5 12.8 %all-to-all-done.2 = bf16[128,2,512]{2,1,0:T(2,128)(2,1)S(1)} async-done(((bf16[128,2,512]{2,1,0:T(2,128)(2,1)}), bf16[128,2,512]{2,1,0:T(2,128)(2,1)S(1)}, u32[]{:S(2)}, u32[]{:S(2)}) %all-to-all-start.2) | async-done | bytes 262176 | tf_op jit(solution)/shard_map/all_to_all | solution.py:171
  153.6 2.5 %fusion.69 = f32[1024,1024]{1,0:T(8,128)S(1)} fusion(bf16[1024,512]{1,0:T(8,128)(2,1)} %all-gather.5.cloned.1.call-done, bf16[512,1024]{1,0:T(8,128)(2,1)S(1)} %bitcast_select_fusion), kind=kOutput, calls=%fused_computation.143 | convolution fusion | flops 1073741824 | bytes 6291456 | tf_op jit(solution)/shard_map/dot_general | solution.py:195
  157.6 2.3 %collective-permute-done.10 = bf16[1024,512]{1,0:T(8,128)(2,1)S(1)} collective-permute-done((bf16[1024,512]{1,0:T(8,128)(2,1)S(1)}, bf16[1024,512]{1,0:T(8,128)(2,1)S(1)}, u32[]{:S(2)}, u32[]{:S(2)}) %collective-permute-start.10) | collective-permute-done | bytes 1048608 | tf_op jit(solution)/shard_map/ppermute | solution.py:201
  161.3 4.7 %all-to-all-start.3 = ((bf16[32,32,512]{2,1,0:T(8,128)(2,1)}), bf16[32,32,512]{2,1,0:T(8,128)(2,1)S(1)}, u32[]{:S(2)}, u32[]{:S(2)}) async-start(bf16[32,32,512]{2,1,0:T(8,128)(2,1)} %bitcast.47), calls=%async_computation.3 | async-start | bytes 2097152 | tf_op jit(solution)/shard_map/all_to_all | solution.py:205
  166.0 17.0 %all-to-all-done.3 = bf16[32,32,512]{2,1,0:T(8,128)(2,1)S(1)} async-done(((bf16[32,32,512]{2,1,0:T(8,128)(2,1)}), bf16[32,32,512]{2,1,0:T(8,128)(2,1)S(1)}, u32[]{:S(2)}, u32[]{:S(2)}) %all-to-all-start.3) | async-done | bytes 1048608 | tf_op jit(solution)/shard_map/all_to_all | solution.py:205
  (161 shorter events, 38.4 us)
Async XLA Ops:
  6.5 113.7 %copy-start = (bf16[4096,128]{1,0:T(8,128)(2,1)S(1)}, bf16[4096,128]{1,0:T(8,128)(2,1)}, u32[]{:S(2)}) copy-start(bf16[4096,128]{1,0:T(8,128)(2,1)} %param.26) | copy-start | bytes 3145732
  6.5 11.4 %copy-start.10 = (bf16[4096]{0:T(1024)(128)(2,1)S(1)}, bf16[4096]{0:T(1024)(128)(2,1)}, u32[]{:S(2)}) copy-start(bf16[4096]{0:T(1024)(128)(2,1)} %param.16) | copy-start | bytes 24580
  6.5 11.4 %copy-start.11 = (bf16[4096]{0:T(1024)(128)(2,1)S(1)}, bf16[4096]{0:T(1024)(128)(2,1)}, u32[]{:S(2)}) copy-start(bf16[4096]{0:T(1024)(128)(2,1)} %param.17) | copy-start | bytes 24580
  6.5 113.7 %all-gather.3.cloned.1.call-start = ((), (), s32[]{:S(2)}) async-start(), calls=%async_computation.4 | async-start | bytes 8650752 | tf_op jit(solution)/shard_map/all_gather | solution.py:84
  6.5 6.6 %collective-permute-start = (bf16[32,1024]{1,0:T(8,128)(2,1)}, bf16[32,1024]{1,0:T(8,128)(2,1)S(1)}, u32[]{:S(2)}, u32[]{:S(2)}) collective-permute-start(bf16[32,1024]{1,0:T(8,128)(2,1)} %param.15), channel_id=1, source_target_pairs={{0,1},{1,2},{2,3},{3,0},{4,5},{5,6},{6,7},{7,4},{8,9},{9,10},{10,1... | collective-permute-start | bytes 196616 | tf_op jit(solution)/shard_map/ppermute | solution.py:55
  8.6 4.5 %collective-permute-start.2 = (bf16[32,1024]{1,0:T(8,128)(2,1)}, bf16[32,1024]{1,0:T(8,128)(2,1)S(1)}, u32[]{:S(2)}, u32[]{:S(2)}) collective-permute-start(bf16[32,1024]{1,0:T(8,128)(2,1)} %param.15), channel_id=1, source_target_pairs={{0,3},{1,0},{2,1},{3,2},{4,7},{5,4},{6,5},{7,6},{8,11},{9,8},{10,9... | collective-permute-start | bytes 196616 | tf_op jit(solution)/shard_map/ppermute | solution.py:55
  10.0 4.8 %collective-permute-start.1 = (bf16[32,1024]{1,0:T(8,128)(2,1)}, bf16[32,1024]{1,0:T(8,128)(2,1)S(1)}, u32[]{:S(2)}, u32[]{:S(2)}) collective-permute-start(bf16[32,1024]{1,0:T(8,128)(2,1)} %param.15), channel_id=1, source_target_pairs={{0,2},{1,3},{2,0},{3,1},{4,6},{5,7},{6,4},{7,5},{8,10},{9,11},{10,... | collective-permute-start | bytes 196616 | tf_op jit(solution)/shard_map/ppermute | solution.py:55
  17.0 13.4 %copy-start.3 = (bf16[128,3,1024]{2,0,1:T(8,128)(2,1)S(1)}, bf16[128,3,1024]{2,0,1:T(8,128)(2,1)}, u32[]{:S(2)}) copy-start(bf16[128,3,1024]{2,0,1:T(8,128)(2,1)} %param.18) | copy-start | bytes 2359300
  19.8 24.6 %all-to-all-start = ((bf16[32,32,256]{2,0,1:T(8,128)(2,1)}), bf16[32,32,256]{2,0,1:T(8,128)(2,1)S(1)}, u32[]{:S(2)}, u32[]{:S(2)}) async-start(bf16[32,32,256]{2,0,1:T(8,128)(2,1)} %bitcast.16), calls=%async_computation | async-start | bytes 1048576 | tf_op jit(solution)/shard_map/all_to_all | solution.py:87
  30.5 1.8 collective-permute-start.6
  47.6 10.7 %copy-start.2 = (bf16[128,4096]{1,0:T(8,128)(2,1)S(1)}, bf16[128,4096]{1,0:T(8,128)(2,1)}, u32[]{:S(2)}) copy-start(bf16[128,4096]{1,0:T(8,128)(2,1)} %param.28) | copy-start | bytes 3145732
  47.6 61.6 %all-to-all-start.1 = ((bf16[32,32,3,512]{3,1,2,0:T(8,128)(2,1)}), bf16[32,32,3,512]{3,1,2,0:T(8,128)(2,1)}, u32[]{:S(2)}, u32[]{:S(2)}) async-start(bf16[32,32,3,512]{3,1,2,0:T(8,128)(2,1)} %copy.140), calls=%async_computation.1 | async-start | bytes 6291456 | tf_op jit(solution)/shard_map/all_to_all | solution.py:103
  52.6 101.0 %all-gather.5.cloned.1.call-start = ((), (), s32[]{:S(2)}) async-start(), calls=%async_computation.5 | async-start | bytes 1310720 | tf_op jit(solution)/shard_map/all_gather | solution.py:194
  54.3 12.6 %collective-permute-start.9 = (bf16[8,4,1024]{2,0,1:T(8,128)(2,1)}, bf16[8,4,1024]{2,0,1:T(8,128)(2,1)}, u32[]{:S(2)}, u32[]{:S(2)}) collective-permute-start(bf16[8,4,1024]{2,0,1:T(8,128)(2,1)} %bitcast.156), channel_id=1, source_target_pairs={{0,3},{1,0},{2,1},{3,2},{4,7},{5,4},{6,5},{7,6},{8,11},{9,8},{10,9... | collective-permute-start | bytes 196616 | tf_op jit(solution)/shard_map/ppermute | solution.py:44
  55.9 12.8 %collective-permute-start.7 = (bf16[8,4,1024]{2,0,1:T(8,128)(2,1)}, bf16[8,4,1024]{2,0,1:T(8,128)(2,1)}, u32[]{:S(2)}, u32[]{:S(2)}) collective-permute-start(bf16[8,4,1024]{2,0,1:T(8,128)(2,1)} %bitcast.158), channel_id=1, source_target_pairs={{0,1},{1,2},{2,3},{3,0},{4,5},{5,6},{6,7},{7,4},{8,9},{9,10},{10,1... | collective-permute-start | bytes 196616 | tf_op jit(solution)/shard_map/ppermute | solution.py:44
  57.2 11.5 %collective-permute-start.8 = (bf16[8,4,1024]{2,0,1:T(8,128)(2,1)}, bf16[8,4,1024]{2,0,1:T(8,128)(2,1)}, u32[]{:S(2)}, u32[]{:S(2)}) collective-permute-start(bf16[8,4,1024]{2,0,1:T(8,128)(2,1)} %bitcast.157), channel_id=1, source_target_pairs={{0,2},{1,3},{2,0},{3,1},{4,6},{5,7},{6,4},{7,5},{8,10},{9,11},{10,... | collective-permute-start | bytes 196616 | tf_op jit(solution)/shard_map/ppermute | solution.py:44
  59.2 12.5 %collective-permute-start.3 = (bf16[128,1024]{1,0:T(8,128)(2,1)S(1)}, bf16[128,1024]{1,0:T(8,128)(2,1)S(1)}, u32[]{:S(2)}, u32[]{:S(2)}) collective-permute-start(bf16[128,1024]{1,0:T(8,128)(2,1)S(1)} %bitcast.182), channel_id=1, source_target_pairs={{0,1},{1,2},{2,3},{3,0},{4,5},{5,6},{6,7},{7,4},{8,9},{9,10},{10,1... | collective-permute-start | bytes 786440 | tf_op jit(solution)/shard_map/ppermute | solution.py:44
  61.0 13.3 %collective-permute-start.4 = (bf16[128,1024]{1,0:T(8,128)(2,1)S(1)}, bf16[128,1024]{1,0:T(8,128)(2,1)}, u32[]{:S(2)}, u32[]{:S(2)}) collective-permute-start(bf16[128,1024]{1,0:T(8,128)(2,1)S(1)} %bitcast.183), channel_id=1, source_target_pairs={{0,2},{1,3},{2,0},{3,1},{4,6},{5,7},{6,4},{7,5},{8,10},{9,11},{10,... | collective-permute-start | bytes 786440 | tf_op jit(solution)/shard_map/ppermute | solution.py:44
  66.9 7.4 %collective-permute-start.5 = (bf16[128,1024]{1,0:T(8,128)(2,1)S(1)}, bf16[128,1024]{1,0:T(8,128)(2,1)S(1)}, u32[]{:S(2)}, u32[]{:S(2)}) collective-permute-start(bf16[128,1024]{1,0:T(8,128)(2,1)S(1)} %bitcast.184), channel_id=1, source_target_pairs={{0,3},{1,0},{2,1},{3,2},{4,7},{5,4},{6,5},{7,6},{8,11},{9,8},{10,9... | collective-permute-start | bytes 786440 | tf_op jit(solution)/shard_map/ppermute | solution.py:44
  134.2 17.1 %all-to-all-start.2 = ((bf16[128,2,512]{2,1,0:T(2,128)(2,1)}), bf16[128,2,512]{2,1,0:T(2,128)(2,1)S(1)}, u32[]{:S(2)}, u32[]{:S(2)}) async-start(bf16[128,2,512]{2,1,0:T(2,128)(2,1)} %reshape.381), calls=%async_computation.2 | async-start | bytes 524288 | tf_op jit(solution)/shard_map/all_to_all | solution.py:171
  156.9 26.9 %copy-start.1 = (bf16[4096,128]{1,0:T(8,128)(2,1)S(1)}, bf16[4096,128]{1,0:T(8,128)(2,1)}, u32[]{:S(2)}) copy-start(bf16[4096,128]{1,0:T(8,128)(2,1)} %param.26) | copy-start | bytes 3145732
  157.1 26.1 %copy-start.6 = (bf16[32,1024]{1,0:T(8,128)(2,1)S(1)}, bf16[32,1024]{1,0:T(8,128)(2,1)}, u32[]{:S(2)}) copy-start(bf16[32,1024]{1,0:T(8,128)(2,1)} %param.15) | copy-start | bytes 196612
  157.1 2.8 %collective-permute-start.10 = (bf16[1024,512]{1,0:T(8,128)(2,1)S(1)}, bf16[1024,512]{1,0:T(8,128)(2,1)S(1)}, u32[]{:S(2)}, u32[]{:S(2)}) collective-permute-start(bf16[1024,512]{1,0:T(8,128)(2,1)S(1)} %dynamic-slice_convert_fusion), channel_id=1, source_target_pairs={{0,4},{4,0},{8,12},{12,8},{16,20},{20,16},{24,28},{28,24},{32,36},... | collective-permute-start | bytes 3145736 | tf_op jit(solution)/shard_map/ppermute | solution.py:201
  161.3 21.7 %all-to-all-start.3 = ((bf16[32,32,512]{2,1,0:T(8,128)(2,1)}), bf16[32,32,512]{2,1,0:T(8,128)(2,1)S(1)}, u32[]{:S(2)}, u32[]{:S(2)}) async-start(bf16[32,32,512]{2,1,0:T(8,128)(2,1)} %bitcast.47), calls=%async_computation.3 | async-start | bytes 2097152 | tf_op jit(solution)/shard_map/all_to_all | solution.py:205
  (13 other events, 69.1 us)
Sparse Core Ops, SparseCore 0:
  18.0 90.7 all-gather.2
  126.8 22.8 all-gather.4
